TPU v7x, 512 devices: a whole 4x8x8 slice. The times are simulated.
512 devices in a mesh: dp: 8 (over y_lo, core), seq: 64 (over x, z, y_hi).
Axes of the slice: x: 4, y: 8 (y_hi: 2, y_lo: 4; y = y_hi * 4 + y_lo), z: 8, core: 2. Of those that a mesh axis runs over, the one named last changes fastest.
Arguments:
- queries: bfloat16 [8, 8192, 2048], P('dp', 'seq'), may hold values from -62 to 62
- keys: bfloat16 [8, 8192, 2048], P('dp', 'seq'), may hold values from -4 to 4
- values: bfloat16 [8, 8192, 2048], P('dp', 'seq'), may hold values from -4 to 4
- cotangent: bfloat16 [8, 8192, 2048], P('dp', 'seq'), may hold values from -4 to 4
- cluster_of: int32 [8, 16, 128], P('dp', None, 'seq'), may hold values from 0 to 127, as said below
- block_list: int32 [8, 2048, 4], P('dp', 'seq'), may hold values from -1 to 127, as said below
- centroid_sums: float32 [2048, 128], P('seq'), may hold values from -5 to 5
Outputs:
- attn_out: bfloat16 [8, 8192, 2048], P('dp', 'seq')
- grad_q: bfloat16 [8, 8192, 2048], P('dp', 'seq')
- grad_k: bfloat16 [8, 8192, 2048], P('dp', 'seq')
- grad_v: bfloat16 [8, 8192, 2048], P('dp', 'seq')
- centroid_next: float32 [2048, 128], P('seq')
Inputs may be any that keep to these rules, and one draw needn't show every extreme that they name: cluster_of[d, h, b] is the cluster under head h of block b of document d; the centroid of cluster c of head h lies on seq index h * 4 + c // 32. Of the 2 blocks on one seq index, at most 1 share the value c // 32 under one head, and in every draw some reach 1. Row h * 128 + c of block_list[d] lists in increasing order the blocks b with cluster_of[d, h, b] == c, then -1; every block appears once for each head; a cluster holds at most 4 blocks, and in every draw some cluster holds exactly 4.
All inputs are finite; a program needn't handle non-finite values.
Results may differ from a plain program's by a relative error of at most 0.015.
Values may be sent and summed in bfloat16 or wider, within the bound.
No kernel may reach another device: no remote copies, remote signals or barrier semaphores. Data moves between devices by JAX's collectives and lax.ppermute only.
A program may use at most 64 MiB of HBM per device.

v0:
```python
import math

import jax
import jax.numpy as jnp
from jax import lax
from jax.sharding import PartitionSpec as P

decay_rate = 0.99
neg_fill = -1e30


def shortened(x):
    return jax.tree.map(lambda a: a.astype(jnp.bfloat16) if a.dtype == jnp.float32 else a, x)


def forward_tiles(q_tiles, k_tiles, v_tiles, positions, present_rows):
    score_scale = 1.0 / math.sqrt(q_tiles.shape[-1])
    scores = (
        jnp.einsum("crd,csd->crs", q_tiles, k_tiles, preferred_element_type=jnp.float32)
        * score_scale
    )
    visible = present_rows[:, :, None] & present_rows[:, None, :]
    visible = visible & (positions[:, None, :] <= positions[:, :, None])
    scores = jnp.where(visible, scores, neg_fill)
    row_max = jnp.max(scores, axis=-1, keepdims=True)
    raised = jnp.exp(scores - row_max)
    probabilities = jnp.where(visible, raised / jnp.sum(raised, axis=-1, keepdims=True), 0.0)
    weights = probabilities.astype(jnp.bfloat16)
    out_full = jnp.einsum("crs,csd->crd", weights, v_tiles, preferred_element_type=jnp.float32)
    return (probabilities, weights, out_full, score_scale)


def output_tiles(q_tiles, k_tiles, v_tiles, positions, present_rows):
    results = forward_tiles(q_tiles, k_tiles, v_tiles, positions, present_rows)
    return (results[2].astype(jnp.bfloat16),)


def all_tiles(q_tiles, k_tiles, v_tiles, d_tiles, positions, present_rows):
    probabilities, weights, out_full, score_scale = forward_tiles(
        q_tiles, k_tiles, v_tiles, positions, present_rows
    )
    dprobs = jnp.einsum("crd,csd->crs", d_tiles, v_tiles, preferred_element_type=jnp.float32)
    row_dot = jnp.sum(d_tiles.astype(jnp.float32) * out_full, axis=-1, keepdims=True)
    dscores = (probabilities * (dprobs - row_dot) * score_scale).astype(jnp.bfloat16)
    grad_values = jnp.einsum("crs,crd->csd", weights, d_tiles, preferred_element_type=jnp.float32)
    grad_queries = jnp.einsum("crs,csd->crd", dscores, k_tiles, preferred_element_type=jnp.float32)
    grad_keys = jnp.einsum("crs,crd->csd", dscores, q_tiles, preferred_element_type=jnp.float32)
    return (
        out_full.astype(jnp.bfloat16),
        grad_queries.astype(jnp.bfloat16),
        grad_keys.astype(jnp.bfloat16),
        grad_values.astype(jnp.bfloat16),
    )


def grad_tiles(q_tiles, k_tiles, v_tiles, d_tiles, positions, present_rows):
    return all_tiles(q_tiles, k_tiles, v_tiles, d_tiles, positions, present_rows)[1:]


def per_device(queries, keys, values, cotangent, cluster_of, block_list, centroid_sums):
    seq_size = lax.axis_size("seq")
    head_count = cluster_of.shape[1]
    block_count = cluster_of.shape[2]
    token_count = queries.shape[1]
    block_len = token_count // block_count
    head_dim = centroid_sums.shape[1]
    groups_here = block_list.shape[1]
    cluster_cap = block_list.shape[2]
    owner_count = seq_size // head_count
    slot_cap = min(block_count, max(1, 2 * block_count // owner_count))
    tile_rows = cluster_cap * block_len
    step_target = 1 << max(0, max(1, 2048 // tile_rows).bit_length() - 1)
    group_size = math.gcd(groups_here, step_target)
    cluster_ids = cluster_of[0]
    owner_local = cluster_ids // groups_here
    earlier = jnp.arange(block_count)[:, None] < jnp.arange(block_count)[None, :]
    same_owner = owner_local[:, :, None] == owner_local[:, None, :]
    slot_of = jnp.sum(same_owner & earlier[None], axis=1)
    selector = owner_local[:, None, None, :] == jnp.arange(owner_count)[None, :, None, None]
    selector = selector & (slot_of[:, None, None, :] == jnp.arange(slot_cap)[None, None, :, None])
    selector = selector.astype(jnp.bfloat16)

    def pack(source):
        blocks_in = source[0].reshape(block_count, block_len, head_count, head_dim)
        outgoing = jnp.einsum(
            "hlcj,jthd->hlctd", selector, blocks_in, preferred_element_type=jnp.float32
        )
        return outgoing.astype(jnp.bfloat16).reshape(seq_size, slot_cap, block_len, head_dim)

    def unpack(returned):
        arranged = returned.reshape(head_count, owner_count, slot_cap, block_len, head_dim)
        gathered = jnp.einsum(
            "hlcj,hlctd->jthd", selector, arranged, preferred_element_type=jnp.float32
        )
        return gathered.astype(jnp.bfloat16).reshape(1, token_count, head_count * head_dim)

    members = block_list[0].reshape(-1)
    present = members >= 0
    source_dev = jnp.where(present, members // block_count, -1)
    before = (
        present[None, :]
        & (source_dev[None, :] == source_dev[:, None])
        & (members[None, :] < members[:, None])
    )
    slot_at = jnp.sum(before, axis=1)
    recv_row = jnp.where(present, source_dev * slot_cap + slot_at, 0)
    drop_row = jnp.where(present, source_dev * slot_cap + slot_at, seq_size * slot_cap)
    token_offsets = jnp.arange(block_len)
    positions = (
        jnp.where(present, members, 0)[:, None] * block_len + token_offsets[None, :]
    ).reshape(groups_here, tile_rows)
    present_rows = jnp.broadcast_to(present[:, None], (members.shape[0], block_len)).reshape(
        groups_here, tile_rows
    )

    def to_tiles(arrived):
        flat_rows = arrived.reshape(seq_size * slot_cap, block_len, head_dim)
        return flat_rows[recv_row].reshape(groups_here, tile_rows, head_dim)

    def from_tiles(tiles_in):
        flat_rows = jnp.zeros((seq_size * slot_cap, block_len, head_dim), jnp.bfloat16)
        flat_rows = flat_rows.at[drop_row].set(
            tiles_in.reshape(-1, block_len, head_dim), mode="drop"
        )
        return flat_rows.reshape(seq_size, slot_cap, block_len, head_dim)

    def grouped(worker, tiles_all):
        shaped = tuple(
            (
                item.reshape((groups_here // group_size, group_size) + item.shape[1:])
                for item in tiles_all
            )
        )
        outcome = lax.map(lambda tiles_in: worker(*tiles_in), shaped)
        return tuple((item.reshape((groups_here,) + item.shape[2:]) for item in outcome))

    arrived = (
        lax.all_to_all(pack(queries), "seq", split_axis=0, concat_axis=0, tiled=True),
        lax.all_to_all(pack(keys), "seq", split_axis=0, concat_axis=0, tiled=True),
        lax.all_to_all(pack(values), "seq", split_axis=0, concat_axis=0, tiled=True),
    )
    q_tiles, key_tiles, v_tiles = (to_tiles(item) for item in arrived)
    forward_out = grouped(output_tiles, (q_tiles, key_tiles, v_tiles, positions, present_rows))
    out_back = lax.all_to_all(
        from_tiles(forward_out[0]), "seq", split_axis=0, concat_axis=0, tiled=True
    )
    d_arrived = lax.all_to_all(pack(cotangent), "seq", split_axis=0, concat_axis=0, tiled=True)
    d_tiles = to_tiles(d_arrived)
    gradients = grouped(grad_tiles, (q_tiles, key_tiles, v_tiles, d_tiles, positions, present_rows))
    grads_back = lax.all_to_all(
        shortened(tuple((from_tiles(item) for item in gradients))),
        "seq",
        split_axis=0,
        concat_axis=0,
        tiled=True,
    )
    returned = (out_back,) + tuple(grads_back)
    key_sum = jnp.einsum(
        "cr,crd->cd",
        present_rows.astype(jnp.bfloat16),
        key_tiles,
        preferred_element_type=jnp.float32,
    )
    summed = lax.psum(key_sum, "dp")
    centroid_next = decay_rate * centroid_sums + (1.0 - decay_rate) * summed
    return (
        unpack(returned[0]),
        unpack(returned[1]),
        unpack(returned[2]),
        unpack(returned[3]),
        centroid_next,
    )


def solution(mesh):
    in_specs = (
        P("dp", "seq", None),
        P("dp", "seq", None),
        P("dp", "seq", None),
        P("dp", "seq", None),
        P("dp", None, "seq"),
        P("dp", "seq", None),
        P("seq", None),
    )
    out_specs = (
        P("dp", "seq", None),
        P("dp", "seq", None),
        P("dp", "seq", None),
        P("dp", "seq", None),
        P("seq", None),
    )
    return jax.shard_map(
        per_device, mesh=mesh, in_specs=in_specs, out_specs=out_specs, check_vma=False
    )
```

profile of v0, /device:TPU:6, one launch (start us, length us, event | category | flops | bytes accessed | tf_op | source)
XLA Modules:
  0.0 462.8 jit_solution(16298377348726236299)
XLA Ops:
  5.4 19.3 %all-to-all-start.1 = ((bf16[64,1,64,128]{3,2,1,0:T(8,128)(2,1)}), bf16[64,1,64,128]{3,2,1,0:T(8,128)(2,1)S(1)}, u32[]{:S(2)}, u32[]{:S(2)}) async-start(bf16[64,1,64,128]{3,2,1,0:T(8,128)(2,1)} %bitcast.27), calls=%async_computation.1 | async-start | bytes 2097152 | tf_op jit(solution)/shard_map/all_to_all | solution.py:139
  27.5 24.4 %all-to-all-done.1 = bf16[64,1,64,128]{3,2,1,0:T(8,128)(2,1)S(1)} async-done(((bf16[64,1,64,128]{3,2,1,0:T(8,128)(2,1)}), bf16[64,1,64,128]{3,2,1,0:T(8,128)(2,1)S(1)}, u32[]{:S(2)}, u32[]{:S(2)}) %all-to-all-start.1) | async-done | bytes 1048608 | tf_op jit(solution)/shard_map/all_to_all | solution.py:139
  51.9 11.7 %all-to-all-start = ((bf16[64,1,64,128]{3,2,1,0:T(8,128)(2,1)}), bf16[64,1,64,128]{3,2,1,0:T(8,128)(2,1)S(1)}, u32[]{:S(2)}, u32[]{:S(2)}) async-start(bf16[64,1,64,128]{3,2,1,0:T(8,128)(2,1)} %bitcast.21), calls=%async_computation | async-start | bytes 2097152 | tf_op jit(solution)/shard_map/all_to_all | solution.py:138
  66.3 25.3 %all-to-all-done = bf16[64,1,64,128]{3,2,1,0:T(8,128)(2,1)S(1)} async-done(((bf16[64,1,64,128]{3,2,1,0:T(8,128)(2,1)}), bf16[64,1,64,128]{3,2,1,0:T(8,128)(2,1)S(1)}, u32[]{:S(2)}, u32[]{:S(2)}) %all-to-all-start) | async-done | bytes 1048608 | tf_op jit(solution)/shard_map/all_to_all | solution.py:138
  91.6 10.6 %all-to-all-start.2 = ((bf16[64,1,64,128]{3,2,1,0:T(8,128)(2,1)}), bf16[64,1,64,128]{3,2,1,0:T(8,128)(2,1)S(1)}, u32[]{:S(2)}, u32[]{:S(2)}) async-start(bf16[64,1,64,128]{3,2,1,0:T(8,128)(2,1)} %bitcast.246), calls=%async_computation.2 | async-start | bytes 2097152 | tf_op jit(solution)/shard_map/all_to_all | solution.py:140
  106.0 24.5 %all-to-all-done.2 = bf16[64,1,64,128]{3,2,1,0:T(8,128)(2,1)S(1)} async-done(((bf16[64,1,64,128]{3,2,1,0:T(8,128)(2,1)}), bf16[64,1,64,128]{3,2,1,0:T(8,128)(2,1)S(1)}, u32[]{:S(2)}, u32[]{:S(2)}) %all-to-all-start.2) | async-done | bytes 1048608 | tf_op jit(solution)/shard_map/all_to_all | solution.py:140
  130.5 11.1 %all-to-all-start.4 = ((bf16[64,1,64,128]{3,2,1,0:T(8,128)(2,1)}), bf16[64,1,64,128]{3,2,1,0:T(8,128)(2,1)}, u32[]{:S(2)}, u32[]{:S(2)}) async-start(bf16[64,1,64,128]{3,2,1,0:T(8,128)(2,1)} %bitcast.245), calls=%async_computation.4 | async-start | bytes 2097152 | tf_op jit(solution)/shard_map/all_to_all | solution.py:147
  144.0 3.5 gather_fusion
  149.6 19.8 %all-to-all-done.4 = bf16[64,1,64,128]{3,2,1,0:T(8,128)(2,1)} async-done(((bf16[64,1,64,128]{3,2,1,0:T(8,128)(2,1)}), bf16[64,1,64,128]{3,2,1,0:T(8,128)(2,1)}, u32[]{:S(2)}, u32[]{:S(2)}) %all-to-all-start.4) | async-done | bytes 1048608 | tf_op jit(solution)/shard_map/all_to_all | solution.py:147
  169.4 3.4 gather_fusion.3
  178.2 56.5 %while.25 = (s32[]{:T(128)}, bf16[4,8,256,128]{3,2,1,0:T(8,128)(2,1)}, bf16[4,8,256,128]{3,2,1,0:T(8,128)(2,1)}, bf16[4,8,256,128]{3,2,1,0:T(8,128)(2,1)}, pred[...) while((s32[]{:T(128)}, ...), condition=%wide.region_11.12_spmd, body=%wide.region_7.11_spmd.sunk | while | flops 821557504 | bytes 43149512 | solution.py:134
  178.3 3.1 fusion.153
  181.3 3.2 fusion.157
  185.2 2.4 fusion.154
  188.8 2.3 fusion.156
  192.4 3.1 fusion.153
  195.5 3.2 fusion.157
  199.3 2.4 fusion.154
  202.9 2.3 fusion.156
  206.6 3.1 fusion.153
  209.7 3.2 fusion.157
  213.5 2.3 fusion.154
  217.1 2.3 fusion.156
  220.7 3.1 fusion.153
  223.8 3.2 fusion.157
  227.6 2.3 fusion.154
  231.2 2.3 fusion.156
  236.0 17.7 %scatter_fusion.1 = bf16[64,64,128]{2,1,0:T(8,128)(2,1)} fusion(bf16[64,64,128]{2,1,0:T(8,128)(2,1)} %broadcast.373.clone.1, s32[128]{0:T(128)S(1)} %fusion.96, bf16[128,64,128]{2,1,0:T(8,128)(2,1)} %bitcast.42), kind=kCustom, calls=%fused_computation.5 | custom fusion | bytes 6291968 | tf_op jit(solution)/shard_map/scatter | solution.py:122
  253.7 10.8 %all-to-all-start.5 = ((bf16[64,1,64,128]{3,2,1,0:T(8,128)(2,1)}), bf16[64,1,64,128]{3,2,1,0:T(8,128)(2,1)S(1)}, u32[]{:S(2)}, u32[]{:S(2)}) async-start(bf16[64,1,64,128]{3,2,1,0:T(8,128)(2,1)} %bitcast.44), calls=%async_computation.5 | async-start | bytes 2097152 | tf_op jit(solution)/shard_map/all_to_all | solution.py:150
  265.8 17.8 %scatter_fusion.2 = bf16[64,64,128]{2,1,0:T(8,128)(2,1)} fusion(bf16[64,64,128]{2,1,0:T(8,128)(2,1)} %broadcast.373.clone.2, s32[128]{0:T(128)S(1)} %fusion.96, bf16[128,64,128]{2,1,0:T(8,128)(2,1)} %bitcast.47), kind=kCustom, calls=%fused_computation.6 | custom fusion | bytes 6291968 | tf_op jit(solution)/shard_map/scatter | solution.py:122
  283.6 8.9 %all-to-all-done.5 = bf16[64,1,64,128]{3,2,1,0:T(8,128)(2,1)S(1)} async-done(((bf16[64,1,64,128]{3,2,1,0:T(8,128)(2,1)}), bf16[64,1,64,128]{3,2,1,0:T(8,128)(2,1)S(1)}, u32[]{:S(2)}, u32[]{:S(2)}) %all-to-all-start.5) | async-done | bytes 1048608 | tf_op jit(solution)/shard_map/all_to_all | solution.py:150
  292.4 10.0 %all-to-all-start.6 = ((bf16[64,1,64,128]{3,2,1,0:T(8,128)(2,1)}), bf16[64,1,64,128]{3,2,1,0:T(8,128)(2,1)}, u32[]{:S(2)}, u32[]{:S(2)}) async-start(bf16[64,1,64,128]{3,2,1,0:T(8,128)(2,1)} %bitcast.49), calls=%async_computation.6 | async-start | bytes 2097152 | tf_op jit(solution)/shard_map/all_to_all | solution.py:150
  303.7 17.7 %scatter_fusion.3 = bf16[64,64,128]{2,1,0:T(8,128)(2,1)} fusion(bf16[64,64,128]{2,1,0:T(8,128)(2,1)} %broadcast.373.clone.3, s32[128]{0:T(128)S(1)} %fusion.96, bf16[128,64,128]{2,1,0:T(8,128)(2,1)} %bitcast.243), kind=kCustom, calls=%fused_computation.7 | custom fusion | bytes 6291968 | tf_op jit(solution)/shard_map/scatter | solution.py:122
  321.5 5.4 %all-to-all-done.6 = bf16[64,1,64,128]{3,2,1,0:T(8,128)(2,1)} async-done(((bf16[64,1,64,128]{3,2,1,0:T(8,128)(2,1)}), bf16[64,1,64,128]{3,2,1,0:T(8,128)(2,1)}, u32[]{:S(2)}, u32[]{:S(2)}) %all-to-all-start.6) | async-done | bytes 1048608 | tf_op jit(solution)/shard_map/all_to_all | solution.py:150
  326.9 11.9 %all-to-all-start.7 = ((bf16[64,1,64,128]{3,2,1,0:T(8,128)(2,1)}), bf16[64,1,64,128]{3,2,1,0:T(8,128)(2,1)}, u32[]{:S(2)}, u32[]{:S(2)}) async-start(bf16[64,1,64,128]{3,2,1,0:T(8,128)(2,1)} %bitcast.54), calls=%async_computation.7 | async-start | bytes 2097152 | tf_op jit(solution)/shard_map/all_to_all | solution.py:150
  340.6 27.1 %while.24 = (s32[]{:T(128)}, bf16[4,8,256,128]{3,2,1,0:T(8,128)(2,1)}, pred[4,8,256]{2,1,0:T(8,128)(4,1)S(1)}, s32[4,8,256]{2,1,0:T(8,128)S(1)}, bf16[4,8,256,12...) while((s32[]{:T(128)}, ...), condition=%wide.region_5.6_spmd, body=%wide.region_2.5_spmd.sunk | while | flops 275513600 | bytes 6371421 | solution.py:134
  340.6 3.1 fusion.139
  343.8 3.6 fusion.140
  347.4 3.1 fusion.139
  350.5 3.6 fusion.140
  354.2 3.1 fusion.139
  357.3 3.6 fusion.140
  360.9 3.1 fusion.139
  364.1 3.6 fusion.140
  369.0 19.6 %scatter_fusion = bf16[64,64,128]{2,1,0:T(8,128)(2,1)} fusion(bf16[64,64,128]{2,1,0:T(8,128)(2,1)} %broadcast.373.clone, s32[128]{0:T(128)S(1)} %fusion.96, bf16[128,64,128]{2,1,0:T(8,128)(2,1)} %bitcast.244), kind=kCustom, calls=%fused_computation.4 | custom fusion | bytes 6291968 | tf_op jit(solution)/shard_map/scatter | solution.py:122
  388.6 15.5 %all-to-all-start.3 = ((bf16[64,1,64,128]{3,2,1,0:T(8,128)(2,1)}), bf16[64,1,64,128]{3,2,1,0:T(8,128)(2,1)}, u32[]{:S(2)}, u32[]{:S(2)}) async-start(bf16[64,1,64,128]{3,2,1,0:T(8,128)(2,1)} %bitcast.35), calls=%async_computation.3 | async-start | bytes 2097152 | tf_op jit(solution)/shard_map/all_to_all | solution.py:144
  404.8 44.3 %psum.7 = f32[32,128]{1,0:T(8,128)S(1)} all-reduce(f32[32,128]{1,0:T(8,128)S(1)} %bitcast.258), channel_id=1, replica_groups=mesh['dp'=8,'seq'=64] {'dp'}, use_global_device_ids=true, to_apply=%region_15.16 | all-reduce | flops 4096 | bytes 32768 | tf_op jit(solution)/shard_map/psum | solution.py:164
  452.1 2.2 fusion.77
  (130 shorter events, 55.6 us)
Async XLA Ops:
  4.1 20.6 %copy-start.5 = (bf16[1,128,2048]{2,1,0:T(8,128)(2,1)S(1)}, bf16[1,128,2048]{2,1,0:T(8,128)(2,1)}, u32[]{:S(2)}) copy-start(bf16[1,128,2048]{2,1,0:T(8,128)(2,1)} %param.11) | copy-start | bytes 1572868
  5.4 46.5 %all-to-all-start.1 = ((bf16[64,1,64,128]{3,2,1,0:T(8,128)(2,1)}), bf16[64,1,64,128]{3,2,1,0:T(8,128)(2,1)S(1)}, u32[]{:S(2)}, u32[]{:S(2)}) async-start(bf16[64,1,64,128]{3,2,1,0:T(8,128)(2,1)} %bitcast.27), calls=%async_computation.1 | async-start | bytes 2097152 | tf_op jit(solution)/shard_map/all_to_all | solution.py:139
  27.5 36.1 %copy-start.6 = (bf16[1,128,2048]{2,1,0:T(8,128)(2,1)S(1)}, bf16[1,128,2048]{2,1,0:T(8,128)(2,1)}, u32[]{:S(2)}) copy-start(bf16[1,128,2048]{2,1,0:T(8,128)(2,1)} %param.13) | copy-start | bytes 1572868
  51.9 39.7 %all-to-all-start = ((bf16[64,1,64,128]{3,2,1,0:T(8,128)(2,1)}), bf16[64,1,64,128]{3,2,1,0:T(8,128)(2,1)S(1)}, u32[]{:S(2)}, u32[]{:S(2)}) async-start(bf16[64,1,64,128]{3,2,1,0:T(8,128)(2,1)} %bitcast.21), calls=%async_computation | async-start | bytes 2097152 | tf_op jit(solution)/shard_map/all_to_all | solution.py:138
  91.6 13.1 %copy-start = (bf16[64,1,64,128]{3,2,1,0:T(8,128)(2,1)}, bf16[64,1,64,128]{3,2,1,0:T(8,128)(2,1)S(1)}, u32[]{:S(2)}) copy-start(bf16[64,1,64,128]{3,2,1,0:T(8,128)(2,1)S(1)} %all-to-all-done) | copy-start | bytes 3145732
  91.6 38.9 %all-to-all-start.2 = ((bf16[64,1,64,128]{3,2,1,0:T(8,128)(2,1)}), bf16[64,1,64,128]{3,2,1,0:T(8,128)(2,1)S(1)}, u32[]{:S(2)}, u32[]{:S(2)}) async-start(bf16[64,1,64,128]{3,2,1,0:T(8,128)(2,1)} %bitcast.246), calls=%async_computation.2 | async-start | bytes 2097152 | tf_op jit(solution)/shard_map/all_to_all | solution.py:140
  104.7 36.9 %copy-start.7 = (s32[1,32,4]{1,2,0:T(4,128)S(1)}, s32[1,32,4]{1,2,0:T(4,128)}, u32[]{:S(2)}) copy-start(s32[1,32,4]{1,2,0:T(4,128)} %param.16) | copy-start | bytes 1540
  130.5 12.5 %copy-start.1 = (bf16[64,1,64,128]{3,2,1,0:T(8,128)(2,1)}, bf16[64,1,64,128]{3,2,1,0:T(8,128)(2,1)S(1)}, u32[]{:S(2)}) copy-start(bf16[64,1,64,128]{3,2,1,0:T(8,128)(2,1)S(1)} %all-to-all-done.2) | copy-start | bytes 3145732
  130.5 38.9 %all-to-all-start.4 = ((bf16[64,1,64,128]{3,2,1,0:T(8,128)(2,1)}), bf16[64,1,64,128]{3,2,1,0:T(8,128)(2,1)}, u32[]{:S(2)}, u32[]{:S(2)}) async-start(bf16[64,1,64,128]{3,2,1,0:T(8,128)(2,1)} %bitcast.245), calls=%async_computation.4 | async-start | bytes 2097152 | tf_op jit(solution)/shard_map/all_to_all | solution.py:147
  144.0 3.5 copy-start.2
  181.3 3.2 copy-start.3
  181.3 3.2 copy-start.4
  181.3 3.8 copy-start.9
  195.5 3.2 copy-start.3
  195.5 3.2 copy-start.4
  195.5 3.8 copy-start.9
  209.7 3.2 copy-start.3
  209.7 3.2 copy-start.4
  209.7 3.8 copy-start.9
  223.7 3.2 copy-start.3
  223.8 3.2 copy-start.4
  223.8 3.8 copy-start.9
  253.7 38.7 %all-to-all-start.5 = ((bf16[64,1,64,128]{3,2,1,0:T(8,128)(2,1)}), bf16[64,1,64,128]{3,2,1,0:T(8,128)(2,1)S(1)}, u32[]{:S(2)}, u32[]{:S(2)}) async-start(bf16[64,1,64,128]{3,2,1,0:T(8,128)(2,1)} %bitcast.44), calls=%async_computation.5 | async-start | bytes 2097152 | tf_op jit(solution)/shard_map/all_to_all | solution.py:150
  292.4 34.5 %all-to-all-start.6 = ((bf16[64,1,64,128]{3,2,1,0:T(8,128)(2,1)}), bf16[64,1,64,128]{3,2,1,0:T(8,128)(2,1)}, u32[]{:S(2)}, u32[]{:S(2)}) async-start(bf16[64,1,64,128]{3,2,1,0:T(8,128)(2,1)} %bitcast.49), calls=%async_computation.6 | async-start | bytes 2097152 | tf_op jit(solution)/shard_map/all_to_all | solution.py:150
  326.9 61.7 %all-to-all-start.7 = ((bf16[64,1,64,128]{3,2,1,0:T(8,128)(2,1)}), bf16[64,1,64,128]{3,2,1,0:T(8,128)(2,1)}, u32[]{:S(2)}, u32[]{:S(2)}) async-start(bf16[64,1,64,128]{3,2,1,0:T(8,128)(2,1)} %bitcast.54), calls=%async_computation.7 | async-start | bytes 2097152 | tf_op jit(solution)/shard_map/all_to_all | solution.py:150
  388.6 60.6 %copy-start.8 = (f32[32,128]{1,0:T(8,128)S(1)}, f32[32,128]{1,0:T(8,128)}, u32[]{:S(2)}) copy-start(f32[32,128]{1,0:T(8,128)} %param.17) | copy-start | bytes 49156
  388.6 70.7 %all-to-all-start.3 = ((bf16[64,1,64,128]{3,2,1,0:T(8,128)(2,1)}), bf16[64,1,64,128]{3,2,1,0:T(8,128)(2,1)}, u32[]{:S(2)}, u32[]{:S(2)}) async-start(bf16[64,1,64,128]{3,2,1,0:T(8,128)(2,1)} %bitcast.35), calls=%async_computation.3 | async-start | bytes 2097152 | tf_op jit(solution)/shard_map/all_to_all | solution.py:144
where the time goes:
time: 465 us; the launch traced here: 463 us
  local copies, waits for them, and re-layouts  112 us (24%)
  waiting for transfers between devices  108 us (23%)
  starting transfers between devices  101 us (22%)
  matrix products  94.1 us (20%)
  blocking collectives  44.3 us (10%)
    scatter x4, local copies, waits for them, and re-layouts, from_tiles(): flat_rows.at[drop_row]  72.8 us
    psum x1, blocking collectives, per_device(): summed = lax.psum(key_sum, 'dp')  44.3 us
    all_to_all x3, starting transfers between devices, per_device(): lax.all_to_all(shortened(tuple((from_tiles(item) for item in gradients)))...  32.7 us
    all_to_all x1, waiting for transfers between devices, per_device(): lax.all_to_all(pack(queries), 'seq', split_axis=0, concat_axis=0, tiled=T...  25.3 us
    sub x8, matrix products, forward_tiles(): raised = jnp.exp(scores - row_max)  24.9 us
    all_to_all x1, waiting for transfers between devices, per_device(): lax.all_to_all(pack(values), 'seq', split_axis=0, concat_axis=0, tiled=True)  24.5 us
    all_to_all x1, waiting for transfers between devices, per_device(): lax.all_to_all(pack(keys), 'seq', split_axis=0, concat_axis=0, tiled=True)  24.4 us
    dot_general x8, matrix products, forward_tiles(): jnp.einsum('crs,csd->crd', weights, v_tiles, preferred_element_type=jnp.f...  23.9 us
  transfers between devices with their start and end apart: 8, of which 6 were waited for; matrix products, arithmetic and copies ran while one was open for 25% of the time, Pallas kernels for 0%

commit v1 on v0

--- a/solution.py
+++ b/solution.py
@@ -80,19 +80,24 @@
     selector = selector & (slot_of[:, None, None, :] == jnp.arange(slot_cap)[None, None, :, None])
     selector = selector.astype(jnp.bfloat16)
 
-    def pack(source):
-        blocks_in = source[0].reshape(block_count, block_len, head_count, head_dim)
+    def pack(sources):
+        stacked = jnp.stack([item[0] for item in sources])
+        blocks_in = stacked.reshape(len(sources), block_count, block_len, head_count, head_dim)
         outgoing = jnp.einsum(
-            "hlcj,jthd->hlctd", selector, blocks_in, preferred_element_type=jnp.float32
+            "hlcj,ajthd->hlcatd", selector, blocks_in, preferred_element_type=jnp.float32
         )
-        return outgoing.astype(jnp.bfloat16).reshape(seq_size, slot_cap, block_len, head_dim)
+        return outgoing.astype(jnp.bfloat16).reshape(
+            seq_size * slot_cap, len(sources), block_len, head_dim
+        )
 
     def unpack(returned):
-        arranged = returned.reshape(head_count, owner_count, slot_cap, block_len, head_dim)
+        count = returned.shape[0]
+        arranged = returned.reshape(count, head_count, owner_count, slot_cap, block_len, head_dim)
         gathered = jnp.einsum(
-            "hlcj,hlctd->jthd", selector, arranged, preferred_element_type=jnp.float32
+            "hlcj,ahlctd->ajthd", selector, arranged, preferred_element_type=jnp.float32
         )
-        return gathered.astype(jnp.bfloat16).reshape(1, token_count, head_count * head_dim)
+        gathered = gathered.astype(jnp.bfloat16).reshape(count, 1, token_count, head_count * head_dim)
+        return tuple(gathered[index] for index in range(count))
 
     members = block_list[0].reshape(-1)
     present = members >= 0
@@ -104,7 +109,10 @@
     )
     slot_at = jnp.sum(before, axis=1)
     recv_row = jnp.where(present, source_dev * slot_cap + slot_at, 0)
-    drop_row = jnp.where(present, source_dev * slot_cap + slot_at, seq_size * slot_cap)
+    slot_ids = jnp.arange(seq_size * slot_cap)
+    hit = present[None, :] & (recv_row[None, :] == slot_ids[:, None])
+    member_of_slot = jnp.sum(jnp.where(hit, jnp.arange(members.shape[0])[None, :], 0), axis=1)
+    slot_used = jnp.any(hit, axis=1)
     token_offsets = jnp.arange(block_len)
     positions = (
         jnp.where(present, members, 0)[:, None] * block_len + token_offsets[None, :]
@@ -112,17 +120,6 @@
     present_rows = jnp.broadcast_to(present[:, None], (members.shape[0], block_len)).reshape(
         groups_here, tile_rows
     )
-
-    def to_tiles(arrived):
-        flat_rows = arrived.reshape(seq_size * slot_cap, block_len, head_dim)
-        return flat_rows[recv_row].reshape(groups_here, tile_rows, head_dim)
-
-    def from_tiles(tiles_in):
-        flat_rows = jnp.zeros((seq_size * slot_cap, block_len, head_dim), jnp.bfloat16)
-        flat_rows = flat_rows.at[drop_row].set(
-            tiles_in.reshape(-1, block_len, head_dim), mode="drop"
-        )
-        return flat_rows.reshape(seq_size, slot_cap, block_len, head_dim)
 
     def grouped(worker, tiles_all):
         shaped = tuple(
@@ -134,42 +131,30 @@
         outcome = lax.map(lambda tiles_in: worker(*tiles_in), shaped)
         return tuple((item.reshape((groups_here,) + item.shape[2:]) for item in outcome))
 
-    arrived = (
-        lax.all_to_all(pack(queries), "seq", split_axis=0, concat_axis=0, tiled=True),
-        lax.all_to_all(pack(keys), "seq", split_axis=0, concat_axis=0, tiled=True),
-        lax.all_to_all(pack(values), "seq", split_axis=0, concat_axis=0, tiled=True),
+    arrived = lax.all_to_all(
+        pack((queries, keys, values, cotangent)), "seq", split_axis=0, concat_axis=0, tiled=True
     )
-    q_tiles, key_tiles, v_tiles = (to_tiles(item) for item in arrived)
-    forward_out = grouped(output_tiles, (q_tiles, key_tiles, v_tiles, positions, present_rows))
-    out_back = lax.all_to_all(
-        from_tiles(forward_out[0]), "seq", split_axis=0, concat_axis=0, tiled=True
+    picked = arrived[recv_row]
+    q_tiles, key_tiles, v_tiles, d_tiles = (
+        picked[:, index].reshape(groups_here, tile_rows, head_dim) for index in range(4)
     )
-    d_arrived = lax.all_to_all(pack(cotangent), "seq", split_axis=0, concat_axis=0, tiled=True)
-    d_tiles = to_tiles(d_arrived)
-    gradients = grouped(grad_tiles, (q_tiles, key_tiles, v_tiles, d_tiles, positions, present_rows))
-    grads_back = lax.all_to_all(
-        shortened(tuple((from_tiles(item) for item in gradients))),
-        "seq",
-        split_axis=0,
-        concat_axis=0,
-        tiled=True,
-    )
-    returned = (out_back,) + tuple(grads_back)
     key_sum = jnp.einsum(
         "cr,crd->cd",
         present_rows.astype(jnp.bfloat16),
         key_tiles,
         preferred_element_type=jnp.float32,
     )
-    summed = lax.psum(key_sum, "dp")
+    summed = jnp.sum(lax.all_gather(key_sum, "dp"), axis=0)
+    results = grouped(all_tiles, (q_tiles, key_tiles, v_tiles, d_tiles, positions, present_rows))
+    by_member = jnp.stack(
+        [item.reshape(groups_here * cluster_cap, block_len, head_dim) for item in results]
+    )
+    outgoing = jnp.where(
+        slot_used[None, :, None, None], by_member[:, member_of_slot], jnp.zeros((), jnp.bfloat16)
+    )
+    returned = lax.all_to_all(outgoing, "seq", split_axis=1, concat_axis=1, tiled=True)
     centroid_next = decay_rate * centroid_sums + (1.0 - decay_rate) * summed
-    return (
-        unpack(returned[0]),
-        unpack(returned[1]),
-        unpack(returned[2]),
-        unpack(returned[3]),
-        centroid_next,
-    )
+    return unpack(returned) + (centroid_next,)
 
 
 def solution(mesh):

time: 465 us -> 376 us (0.81)
  the two profiles are of different devices: /device:TPU:6 before, /device:TPU:8 now
where the time goes in v1:
time: 376 us; the launch traced here: 375 us
  waiting for transfers between devices  113 us (30%)
  blocking collectives  105 us (28%)
  matrix products  64 us (17%)
  local copies, waits for them, and re-layouts  47 us (12%)
  starting transfers between devices  30.3 us (8%)
  other arithmetic  15.3 us (4%)
    all_to_all x1, waiting for transfers between devices, per_device(): lax.all_to_all(pack((queries, keys, values, cotangent)), 'seq', split_axi...  107 us
    all_gather x1, blocking collectives, per_device(): summed = jnp.sum(lax.all_gather(key_sum, 'dp'), axis=0)  105 us
    all_to_all x1, starting transfers between devices, per_device(): lax.all_to_all(pack((queries, keys, values, cotangent)), 'seq', split_axi...  18.5 us
    sub x4, matrix products, forward_tiles(): raised = jnp.exp(scores - row_max)  12.6 us
    dot_general x4, matrix products, forward_tiles(): jnp.einsum('crs,csd->crd', weights, v_tiles, preferred_element_type=jnp.f...  12.2 us
    all_to_all x1, starting transfers between devices, per_device(): lax.all_to_all(outgoing, 'seq', split_axis=1, concat_axis=1, tiled=True)  11.7 us
    dot_general x4, matrix products, all_tiles(): jnp.einsum('crs,crd->csd', dscores, q_tiles, preferred_element_type=jnp.f...  9.11 us
    gather x1, local copies, waits for them, and re-layouts, per_device(): picked = arrived[recv_row]  8.55 us
  transfers between devices with their start and end apart: 2, of which 2 were waited for; matrix products, arithmetic and copies ran while one was open for 1% of the time, Pallas kernels for 0%

profile of v1, /device:TPU:8, one launch (start us, length us, event | category | flops | bytes accessed | tf_op | source)
XLA Modules:
  0.0 375.2 jit_solution(936266493952709770)
XLA Ops:
  1.6 1.8 pad_maximum_fusion.1
  4.0 4.4 %convolution_convert_fusion.3 = bf16[16,4,4,64,128]{4,1,3,2,0:T(4,128)(2,1)S(1)} fusion(bf16[4,2,64,16,128]{4,3,2,1,0:T(8,128)(2,1)S(1)} %bitcast.158, pred[16,2]{1,0:T(8,128)(4,1)S(1)} %copy.69, s32[16,2]{1,0:T(8,128)S(1)} %copy.68), kind=kOutput, calls=%fused_computation.50 | convolution fusion | flops 10486016 | bytes 6291616 | tf_op jit(solution)/shard_map/hlcj,ajthd->hlcatd/dot_general | solution.py:86
  8.4 3.1 copy.71
  11.5 18.5 %all-to-all-start = ((bf16[64,4,64,128]{3,2,1,0:T(8,128)(2,1)}), bf16[64,4,64,128]{3,2,1,0:T(8,128)(2,1)}, u32[]{:S(2)}, u32[]{:S(2)}) async-start(bf16[64,4,64,128]{3,2,1,0:T(8,128)(2,1)} %bitcast.154), calls=%async_computation | async-start | bytes 8388608 | tf_op jit(solution)/shard_map/all_to_all | solution.py:134
  31.8 106.5 %all-to-all-done = bf16[64,4,64,128]{3,2,1,0:T(8,128)(2,1)} async-done(((bf16[64,4,64,128]{3,2,1,0:T(8,128)(2,1)}), bf16[64,4,64,128]{3,2,1,0:T(8,128)(2,1)}, u32[]{:S(2)}, u32[]{:S(2)}) %all-to-all-start) | async-done | bytes 4194336 | tf_op jit(solution)/shard_map/all_to_all | solution.py:134
  138.3 8.6 %gather_fusion = bf16[128,4,64,128]{3,2,1,0:T(8,128)(2,1)} fusion(bf16[64,4,64,128]{3,2,1,0:T(8,128)(2,1)} %all-to-all-done, s32[1024]{0:T(1024)S(1)} %pad_clamp_fusion.1), kind=kCustom, calls=%fused_computation | custom fusion | bytes 16777728 | tf_op jit(solution)/shard_map/gather | solution.py:137
  146.9 6.1 %fusion.69 = (bf16[128,1,64,128]{3,2,1,0:T(8,128)(2,1)}, bf16[128,1,64,128]{3,2,1,0:T(8,128)(2,1)}, bf16[128,1,64,128]{3,2,1,0:T(8,128)(2,1)S(1)}, bf16[128,1,64,128]{3,2,1,0:T(8,128)(2,1)}) fusion(bf16[128,4,64,128]{3,2,1,0:T(8,128)(2,1)} %gather_fusion), kind=kLoop, calls=%fused_computation.105 | loop fusion | bytes 16777216 | tf_op jit(solution)/shard_map/slice | solution.py:139
  152.9 67.0 %while.16 = (s32[]{:T(128)}, bf16[4,8,256,128]{3,2,1,0:T(8,128)(2,1)}, bf16[4,8,256,128]{3,2,1,0:T(8,128)(2,1)}, bf16[4,8,256,128]{3,2,1,0:T(8,128)(2,1)}, bf16[...) while((s32[]{:T(128)}, ...), condition=%wide.region_7.8_spmd, body=%wide.region_3.7_spmd.sunk | while | flops 821819648 | bytes 39479480 | solution.py:131
  152.9 3.2 fusion.108
  156.1 1.1 constant_dynamic-slice_fusion.4
  158.2 3.1 multiply_reduce_fusion.2
  161.4 1.9 multiply_convert_fusion.2
  163.3 2.3 fusion.110
  165.6 1.3 fusion.109
  166.9 1.7 fusion.111
  169.7 3.1 fusion.108
  172.8 1.1 constant_dynamic-slice_fusion.4
  174.9 3.1 multiply_reduce_fusion.2
  178.1 1.9 multiply_convert_fusion.2
  180.0 2.3 fusion.110
  182.3 1.3 fusion.109
  183.6 1.7 fusion.111
  186.4 3.2 fusion.108
  189.6 1.1 constant_dynamic-slice_fusion.4
  191.7 3.1 multiply_reduce_fusion.2
  194.8 1.9 multiply_convert_fusion.2
  196.8 2.3 fusion.110
  199.1 1.3 fusion.109
  200.4 1.7 fusion.111
  203.2 3.1 fusion.108
  206.3 1.1 constant_dynamic-slice_fusion.4
  208.4 3.1 multiply_reduce_fusion.2
  211.6 1.9 multiply_convert_fusion.2
  213.5 2.3 fusion.110
  215.8 1.3 fusion.109
  217.1 1.7 fusion.111
  219.9 7.1 %pad_maximum_fusion = bf16[4,128,64,128]{3,2,1,0:T(8,128)(2,1)} fusion(bf16[1,128,64,128]{3,2,1,0:T(8,128)(2,1)} %bitcast.163, bf16[1,128,64,128]{3,2,1,0:T(8,128)(2,1)} %bitcast.162, bf16[1,128,64,128]{3,2,1,0:T(8,128)(2,1)} %bitcast.161, bf16[1,128,64,128]{3,2,1,0:T(8,128)(2,1)} %bitcast.160), kind=kLoop, calls=%fused_computation.49 | loop fusion | flops 12582912 | bytes 16777216 | tf_op jit(solution)/shard_map/stack | solution.py:149
  227.0 6.4 %gather_fusion.1 = bf16[64,4,64,128]{3,2,1,0:T(8,128)(2,1)} fusion(bf16[4,128,64,128]{3,2,1,0:T(8,128)(2,1)} %pad_maximum_fusion, s32[1024]{0:T(1024)S(1)} %pad_clamp_fusion), kind=kCustom, calls=%fused_computation.1 | custom fusion | bytes 8388864 | tf_op jit(solution)/shard_map/gather | solution.py:153
  233.5 4.5 %select_bitcast_fusion = bf16[4,64,64,128]{3,2,0,1:T(8,128)(2,1)} fusion(bf16[64,4,64,128]{3,2,1,0:T(8,128)(2,1)} %gather_fusion.1, pred[64]{0:T(512)(128)(4,1)S(1)} %fusion.52), kind=kLoop, calls=%fused_computation.51 | loop fusion | flops 2097152 | bytes 8388672 | tf_op jit(solution)/shard_map/jit(_where)/select_n | solution.py:152
  238.0 11.7 %all-to-all-start.1 = ((bf16[4,64,64,128]{3,2,0,1:T(8,128)(2,1)}), bf16[4,64,64,128]{3,2,0,1:T(8,128)(2,1)}, u32[]{:S(2)}, u32[]{:S(2)}) async-start(bf16[4,64,64,128]{3,2,0,1:T(8,128)(2,1)} %select_bitcast_fusion), calls=%async_computation.1 | async-start | bytes 8388608 | tf_op jit(solution)/shard_map/all_to_all | solution.py:155
  250.4 104.8 %all-gather = f32[256,128]{1,0:T(8,128)S(1)} all-gather(f32[32,128]{1,0:T(8,128)S(1)} %bitcast.165), channel_id=2, replica_groups=mesh['dp'=8,'seq'=64] {'dp'}, dimensions={0}, use_global_device_ids=true | all-gather | bytes 147456 | tf_op jit(solution)/shard_map/all_gather | solution.py:147
  355.8 6.3 %all-to-all-done.1 = bf16[4,64,64,128]{3,2,0,1:T(8,128)(2,1)} async-done(((bf16[4,64,64,128]{3,2,0,1:T(8,128)(2,1)}), bf16[4,64,64,128]{3,2,0,1:T(8,128)(2,1)}, u32[]{:S(2)}, u32[]{:S(2)}) %all-to-all-start.1) | async-done | bytes 4194336 | tf_op jit(solution)/shard_map/all_to_all | solution.py:155
  362.2 5.6 %fusion.47 = bf16[4,2,64,16,128]{4,1,2,0,3:T(2,128)(2,1)S(1)} fusion(bf16[4,16,4,64,128]{4,3,0,2,1:T(8,128)(2,1)} %bitcast.27, pred[16,2]{1,0:T(8,128)(4,1)S(1)} %copy.69, s32[16,2]{1,0:T(8,128)S(1)} %copy.68), kind=kOutput, calls=%fused_computation.55 | convolution fusion | flops 9437440 | bytes 6291616 | tf_op jit(solution)/shard_map/hlcj,ahlctd->ajthd/dot_general | solution.py:96
  367.8 2.0 fusion.70
  370.1 1.0 squeeze.33
  371.5 1.0 squeeze.34
  372.8 1.0 squeeze.35
  374.2 1.0 squeeze.36
  (87 shorter events, 14.7 us)
Async XLA Ops:
  11.5 18.6 %copy-start.1 = (s32[1,32,4]{1,2,0:T(4,128)S(1)}, s32[1,32,4]{1,2,0:T(4,128)}, u32[]{:S(2)}) copy-start(s32[1,32,4]{1,2,0:T(4,128)} %param.14) | copy-start | bytes 1540
  11.5 126.8 %all-to-all-start = ((bf16[64,4,64,128]{3,2,1,0:T(8,128)(2,1)}), bf16[64,4,64,128]{3,2,1,0:T(8,128)(2,1)}, u32[]{:S(2)}, u32[]{:S(2)}) async-start(bf16[64,4,64,128]{3,2,1,0:T(8,128)(2,1)} %bitcast.154), calls=%async_computation | async-start | bytes 8388608 | tf_op jit(solution)/shard_map/all_to_all | solution.py:134
  158.2 3.1 copy-start
  158.2 3.2 copy-start.3
  174.9 3.1 copy-start
  174.9 3.2 copy-start.3
  191.7 3.1 copy-start
  191.7 3.2 copy-start.3
  208.4 3.1 copy-start
  208.4 3.2 copy-start.3
  238.0 124.2 %all-to-all-start.1 = ((bf16[4,64,64,128]{3,2,0,1:T(8,128)(2,1)}), bf16[4,64,64,128]{3,2,0,1:T(8,128)(2,1)}, u32[]{:S(2)}, u32[]{:S(2)}) async-start(bf16[4,64,64,128]{3,2,0,1:T(8,128)(2,1)} %select_bitcast_fusion), calls=%async_computation.1 | async-start | bytes 8388608 | tf_op jit(solution)/shard_map/all_to_all | solution.py:155
  249.7 105.5 %copy-start.2 = (f32[32,128]{1,0:T(8,128)S(1)}, f32[32,128]{1,0:T(8,128)}, u32[]{:S(2)}) copy-start(f32[32,128]{1,0:T(8,128)} %param.15) | copy-start | bytes 49156

commit v2 on v1

v2 whole, which is shorter than its diff:
```python
import math

import jax
import jax.numpy as jnp
from jax import lax
from jax.experimental import pallas as pl
from jax.experimental.pallas import tpu as pltpu
from jax.sharding import PartitionSpec as P

decay_rate = 0.99
neg_fill = -1e30


def attend_block(q, k, v, g, query_pos, key_pos):
    score_scale = 1.0 / math.sqrt(q.shape[-1])
    scores = (
        lax.dot_general(q, k, (((1,), (1,)), ((), ())), preferred_element_type=jnp.float32)
        * score_scale
    )
    visible = key_pos <= query_pos
    scores = jnp.where(visible, scores, neg_fill)
    row_max = jnp.max(scores, axis=-1, keepdims=True)
    raised = jnp.exp(scores - row_max)
    probabilities = jnp.where(visible, raised / jnp.sum(raised, axis=-1, keepdims=True), 0.0)
    weights = probabilities.astype(jnp.bfloat16)
    out_full = jnp.dot(weights, v, preferred_element_type=jnp.float32)
    dprobs = lax.dot_general(g, v, (((1,), (1,)), ((), ())), preferred_element_type=jnp.float32)
    row_dot = jnp.sum(g.astype(jnp.float32) * out_full, axis=-1, keepdims=True)
    dscores_wide = probabilities * (dprobs - row_dot) * score_scale
    dscores = dscores_wide.astype(jnp.bfloat16)
    grad_values = jnp.dot(
        probabilities.T.astype(jnp.bfloat16), g, preferred_element_type=jnp.float32
    )
    grad_queries = jnp.dot(dscores, k, preferred_element_type=jnp.float32)
    grad_keys = jnp.dot(dscores_wide.T.astype(jnp.bfloat16), q, preferred_element_type=jnp.float32)
    return (out_full, grad_queries, grad_keys, grad_values)


def routed_kernel(recv_ref, count_ref, member_ref, arrived_ref, out_ref):
    cluster_count, cluster_cap = member_ref.shape
    block_len = arrived_ref.shape[2]
    out_ref[...] = jnp.zeros(out_ref.shape, out_ref.dtype)

    def one_cluster(cluster, carry):
        present_count = count_ref[cluster]
        for used in range(1, cluster_cap + 1):

            @pl.when(present_count == used)
            def _():
                rows = [recv_ref[cluster, slot] for slot in range(used)]
                tiles = [
                    jnp.concatenate([arrived_ref[row, index] for row in rows], axis=0)
                    for index in range(4)
                ]
                offsets = lax.broadcasted_iota(jnp.int32, (used * block_len, 1), 0)
                query_pos = offsets % block_len
                key_offsets = lax.broadcasted_iota(jnp.int32, (1, used * block_len), 1)
                key_pos = key_offsets % block_len
                for slot in range(used):
                    base = member_ref[cluster, slot] * block_len
                    query_pos = jnp.where(offsets // block_len == slot, query_pos + base, query_pos)
                    key_pos = jnp.where(key_offsets // block_len == slot, key_pos + base, key_pos)
                results = attend_block(*tiles, query_pos, key_pos)
                for slot in range(used):
                    for index in range(4):
                        out_ref[rows[slot], index] = results[index][
                            slot * block_len : (slot + 1) * block_len
                        ].astype(out_ref.dtype)

        return carry

    lax.fori_loop(0, cluster_count, one_cluster, 0)


def routed_attention(recv_table, present_count, member_table, arrived):
    smem = pl.BlockSpec(memory_space=pltpu.SMEM)
    vmem = pl.BlockSpec(memory_space=pltpu.VMEM)
    return pl.pallas_call(
        routed_kernel,
        out_shape=jax.ShapeDtypeStruct(arrived.shape, arrived.dtype),
        in_specs=[smem, smem, smem, vmem],
        out_specs=vmem,
    )(recv_table, present_count, member_table, arrived)


def per_device(queries, keys, values, cotangent, cluster_of, block_list, centroid_sums):
    seq_size = lax.axis_size("seq")
    head_count = cluster_of.shape[1]
    block_count = cluster_of.shape[2]
    token_count = queries.shape[1]
    block_len = token_count // block_count
    head_dim = centroid_sums.shape[1]
    groups_here = block_list.shape[1]
    cluster_cap = block_list.shape[2]
    owner_count = seq_size // head_count
    slot_cap = min(block_count, max(1, 2 * block_count // owner_count))
    cluster_ids = cluster_of[0]
    owner_local = cluster_ids // groups_here
    earlier = jnp.arange(block_count)[:, None] < jnp.arange(block_count)[None, :]
    same_owner = owner_local[:, :, None] == owner_local[:, None, :]
    slot_of = jnp.sum(same_owner & earlier[None], axis=1)
    selector = owner_local[:, None, None, :] == jnp.arange(owner_count)[None, :, None, None]
    selector = selector & (slot_of[:, None, None, :] == jnp.arange(slot_cap)[None, None, :, None])
    selector = selector.astype(jnp.bfloat16)

    def pack(sources):
        stacked = jnp.stack([item[0] for item in sources])
        blocks_in = stacked.reshape(len(sources), block_count, block_len, head_count, head_dim)
        outgoing = jnp.einsum(
            "hlcj,ajthd->hlcatd", selector, blocks_in, preferred_element_type=jnp.float32
        )
        return outgoing.astype(jnp.bfloat16).reshape(
            seq_size * slot_cap, len(sources), block_len, head_dim
        )

    def unpack(returned):
        count = returned.shape[1]
        arranged = returned.reshape(head_count, owner_count, slot_cap, count, block_len, head_dim)
        gathered = jnp.einsum(
            "hlcj,hlcatd->ajthd", selector, arranged, preferred_element_type=jnp.float32
        )
        gathered = gathered.astype(jnp.bfloat16).reshape(count, 1, token_count, head_count * head_dim)
        return tuple(gathered[index] for index in range(count))

    members = block_list[0].reshape(-1)
    present = members >= 0
    source_dev = jnp.where(present, members // block_count, -1)
    before = (
        present[None, :]
        & (source_dev[None, :] == source_dev[:, None])
        & (members[None, :] < members[:, None])
    )
    slot_at = jnp.sum(before, axis=1)
    recv_row = jnp.where(present, source_dev * slot_cap + slot_at, 0)

    arrived = lax.all_to_all(
        pack((queries, keys, values, cotangent)), "seq", split_axis=0, concat_axis=0, tiled=True
    )
    block_sums = jnp.sum(arrived[:, 1].astype(jnp.float32), axis=1)
    key_sum = jnp.sum(
        jnp.where(present[:, None], block_sums[recv_row], 0.0).reshape(
            groups_here, cluster_cap, head_dim
        ),
        axis=1,
    )
    summed = jnp.sum(lax.all_gather(key_sum, "dp"), axis=0)
    summed, arrived = lax.optimization_barrier((summed, arrived))
    present_count = jnp.sum(present.reshape(groups_here, cluster_cap).astype(jnp.int32), axis=1)
    outgoing = routed_attention(
        recv_row.reshape(groups_here, cluster_cap).astype(jnp.int32),
        present_count,
        jnp.where(present, members, 0).reshape(groups_here, cluster_cap).astype(jnp.int32),
        arrived,
    )
    returned = lax.all_to_all(outgoing, "seq", split_axis=0, concat_axis=0, tiled=True)
    centroid_next = decay_rate * centroid_sums + (1.0 - decay_rate) * summed
    return unpack(returned) + (centroid_next,)


def solution(mesh):
    in_specs = (
        P("dp", "seq", None),
        P("dp", "seq", None),
        P("dp", "seq", None),
        P("dp", "seq", None),
        P("dp", None, "seq"),
        P("dp", "seq", None),
        P("seq", None),
    )
    out_specs = (
        P("dp", "seq", None),
        P("dp", "seq", None),
        P("dp", "seq", None),
        P("dp", "seq", None),
        P("seq", None),
    )
    return jax.shard_map(
        per_device, mesh=mesh, in_specs=in_specs, out_specs=out_specs, check_vma=False
    )
```

time: 376 us -> 310 us (0.82)
  the two profiles are of different devices: /device:TPU:8 before, /device:TPU:26 now
where the time goes in v2:
time: 310 us
  waiting for transfers between devices  217 us (70%)
  starting transfers between devices  28.5 us (9%)
  Pallas kernels  20.3 us (7%)
  blocking collectives  14 us (5%)
  local copies, waits for them, and re-layouts  12.5 us (4%)
  matrix products  10 us (3%)
  other arithmetic  6.87 us (2%)
    all_to_all x1, waiting for transfers between devices, per_device(): lax.all_to_all(outgoing, 'seq', split_axis=0, concat_axis=0, tiled=True)  109 us
    all_to_all x1, waiting for transfers between devices, per_device(): lax.all_to_all(pack((queries, keys, values, cotangent)), 'seq', split_axi...  108 us
    pallas_call x1, Pallas kernels, routed_attention(): pl.pallas_call(routed_kernel, out_shape=jax.ShapeDtypeStruct(arrived.shap...  20.3 us
    all_to_all x1, starting transfers between devices, per_device(): lax.all_to_all(pack((queries, keys, values, cotangent)), 'seq', split_axi...  16.8 us
    all_gather x1, blocking collectives, per_device(): summed = jnp.sum(lax.all_gather(key_sum, 'dp'), axis=0)  14 us
    all_to_all x1, starting transfers between devices, per_device(): lax.all_to_all(outgoing, 'seq', split_axis=0, concat_axis=0, tiled=True)  11.8 us
  transfers between devices with their start and end apart: 2, of which 2 were waited for; matrix products, arithmetic and copies ran while one was open for 1% of the time, Pallas kernels for 0%

profile of v2, /device:TPU:26, one launch (start us, length us, event | category | flops | bytes accessed | tf_op | source)
XLA Modules:
  0.0 309.7 jit_solution(11875578548166382792)
XLA Ops:
  0.6 0.7 and_select_fusion.1
  1.3 0.1 copy.52
  1.4 0.1 fusion.20
  1.5 0.1 copy.53
  1.6 1.8 pad_maximum_fusion
  3.4 0.6 copy.63
  4.0 4.4 %convolution_convert_fusion = bf16[16,4,4,64,128]{4,1,3,2,0:T(4,128)(2,1)S(1)} fusion(bf16[4,2,64,16,128]{4,3,2,1,0:T(8,128)(2,1)S(1)} %bitcast.42, pred[16,2]{1,0:T(8,128)(4,1)S(1)} %copy.53, s32[16,2]{1,0:T(8,128)S(1)} %copy.52), kind=kOutput, calls=%fused_computation.1 | convolution fusion | flops 10486016 | bytes 6291616 | tf_op jit(solution)/shard_map/hlcj,ajthd->hlcatd/dot_general | solution.py:109
  8.4 3.1 %copy.55 = bf16[16,4,4,64,128]{4,3,2,1,0:T(8,128)(2,1)} copy(bf16[16,4,4,64,128]{4,1,3,2,0:T(4,128)(2,1)S(1)} %convolution_convert_fusion) | data formatting | bytes 8388608 | tf_op jit(solution)/shard_map/convert_element_type | solution.py:112
  11.6 0.0 copy-start.1
  11.6 16.8 %all-to-all-start = ((bf16[64,4,64,128]{3,2,1,0:T(8,128)(2,1)}), bf16[64,4,64,128]{3,2,1,0:T(8,128)(2,1)}, u32[]{:S(2)}, u32[]{:S(2)}) async-start(bf16[64,4,64,128]{3,2,1,0:T(8,128)(2,1)} %bitcast.40), calls=%async_computation | async-start | bytes 8388608 | tf_op jit(solution)/shard_map/all_to_all | solution.py:136
  28.3 0.0 copy-done.1
  28.4 0.1 copy.50
  28.4 0.1 reshape_squeeze.8
  28.6 0.1 reshape_squeeze.9
  28.7 0.1 copy.45
  28.8 0.2 convert_reduce_fusion.1
  28.9 0.1 reduce_sum.59
  29.1 0.6 broadcast_select_fusion
  29.7 1.2 convert_reduce_fusion.2
  30.9 107.9 %all-to-all-done.arrived_ref = bf16[64,4,64,128]{3,2,1,0:T(8,128)(2,1)} async-done(((bf16[64,4,64,128]{3,2,1,0:T(8,128)(2,1)}), bf16[64,4,64,128]{3,2,1,0:T(8,128)(2,1)}, u32[]{:S(2)}, u32[]{:S(2)}) %all-to-all-start) | async-done | bytes 4194336 | tf_op jit(solution)/shard_map/all_to_all | solution.py:136
  138.9 1.5 convert_reduce_fusion
  140.4 0.6 gather_fusion
  141.0 0.1 select_reduce_fusion
  141.2 14.0 %all-gather = f32[256,128]{1,0:T(8,128)S(1)} all-gather(f32[32,128]{1,0:T(8,128)S(1)} %select_reduce_fusion), channel_id=2, replica_groups=mesh['dp'=8,'seq'=64] {'dp'}, dimensions={0}, use_global_device_ids=true | all-gather | bytes 147456 | tf_op jit(solution)/shard_map/all_gather | solution.py:146
  155.2 20.3 %shard_map.110 = bf16[64,4,64,128]{3,2,1,0:T(8,128)(2,1)} custom-call(s32[32,4]{1,0:T(8,128)} %get-tuple-element.16.recv_ref, s32[32]{0:T(128)} %get-tuple-element.15.count_ref, s32[32,4]{1,0:T(8,128)} %get-tuple-element.9.member_ref, bf16[64,4,64,128]{3,2,1,0:T(8,128)(2,1)} %all-to-all-done.arrived_ref), custom_call_target="tpu_custom_call" | custom-call | tf_op jit(solution)/shard_map/pallas_call | solution.py:78
  175.4 0.0 copy-start
  175.4 11.8 %all-to-all-start.1 = ((bf16[64,4,64,128]{3,2,1,0:T(8,128)(2,1)}), bf16[64,4,64,128]{3,2,1,0:T(8,128)(2,1)}, u32[]{:S(2)}, u32[]{:S(2)}) async-start(bf16[64,4,64,128]{3,2,1,0:T(8,128)(2,1)} %shard_map.110), calls=%async_computation.1 | async-start | bytes 8388608 | tf_op jit(solution)/shard_map/all_to_all | solution.py:155
  187.2 0.0 copy-done
  187.2 0.6 multiply_add_fusion
  187.8 108.9 %all-to-all-done.1 = bf16[64,4,64,128]{3,2,1,0:T(8,128)(2,1)} async-done(((bf16[64,4,64,128]{3,2,1,0:T(8,128)(2,1)}), bf16[64,4,64,128]{3,2,1,0:T(8,128)(2,1)}, u32[]{:S(2)}, u32[]{:S(2)}) %all-to-all-start.1) | async-done | bytes 4194336 | tf_op jit(solution)/shard_map/all_to_all | solution.py:155
  296.7 5.6 %fusion.5 = bf16[4,2,64,16,128]{4,1,2,0,3:T(2,128)(2,1)S(1)} fusion(bf16[16,4,4,64,128]{4,3,2,1,0:T(8,128)(2,1)} %bitcast.9, pred[16,2]{1,0:T(8,128)(4,1)S(1)} %copy.53, s32[16,2]{1,0:T(8,128)S(1)} %copy.52), kind=kOutput, calls=%fused_computation.5 | convolution fusion | flops 9437440 | bytes 6291616 | tf_op jit(solution)/shard_map/hlcj,hlcatd->ajthd/dot_general | solution.py:119
  302.3 2.0 fusion.24
  304.3 0.3 copy.58
  304.6 1.0 squeeze.17
  305.6 0.3 copy.59
  306.0 1.0 squeeze.18
  307.0 0.3 copy.60
  307.4 1.0 squeeze.19
  308.4 0.3 copy.61
  308.7 1.0 squeeze.20
  (7 shorter events, 0.1 us)
Async XLA Ops:
  11.6 16.8 %copy-start.1 = (s32[1,32,4]{1,2,0:T(4,128)S(1)}, s32[1,32,4]{1,2,0:T(4,128)}, u32[]{:S(2)}) copy-start(s32[1,32,4]{1,2,0:T(4,128)} %param.12) | copy-start | bytes 1540
  11.6 127.3 %all-to-all-start = ((bf16[64,4,64,128]{3,2,1,0:T(8,128)(2,1)}), bf16[64,4,64,128]{3,2,1,0:T(8,128)(2,1)}, u32[]{:S(2)}, u32[]{:S(2)}) async-start(bf16[64,4,64,128]{3,2,1,0:T(8,128)(2,1)} %bitcast.40), calls=%async_computation | async-start | bytes 8388608 | tf_op jit(solution)/shard_map/all_to_all | solution.py:136
  175.4 11.8 %copy-start = (f32[32,128]{1,0:T(8,128)S(1)}, f32[32,128]{1,0:T(8,128)}, u32[]{:S(2)}) copy-start(f32[32,128]{1,0:T(8,128)} %param.13) | copy-start | bytes 49156
  175.4 121.3 %all-to-all-start.1 = ((bf16[64,4,64,128]{3,2,1,0:T(8,128)(2,1)}), bf16[64,4,64,128]{3,2,1,0:T(8,128)(2,1)}, u32[]{:S(2)}, u32[]{:S(2)}) async-start(bf16[64,4,64,128]{3,2,1,0:T(8,128)(2,1)} %shard_map.110), calls=%async_computation.1 | async-start | bytes 8388608 | tf_op jit(solution)/shard_map/all_to_all | solution.py:155

commit v3 on v2

--- a/solution.py
+++ b/solution.py
@@ -114,13 +114,20 @@
         )
 
     def unpack(returned):
-        count = returned.shape[1]
-        arranged = returned.reshape(head_count, owner_count, slot_cap, count, block_len, head_dim)
-        gathered = jnp.einsum(
-            "hlcj,hlcatd->ajthd", selector, arranged, preferred_element_type=jnp.float32
+        arranged = returned.reshape(head_count, owner_count, slot_cap, -1, block_len, head_dim)
+        gathered = (
+            jnp.einsum(
+                "hlcj,hlctd->jthd",
+                selector,
+                arranged[:, :, :, index],
+                preferred_element_type=jnp.float32,
+            )
+            for index in range(arranged.shape[3])
         )
-        gathered = gathered.astype(jnp.bfloat16).reshape(count, 1, token_count, head_count * head_dim)
-        return tuple(gathered[index] for index in range(count))
+        return tuple(
+            item.astype(jnp.bfloat16).reshape(1, token_count, head_count * head_dim)
+            for item in gathered
+        )
 
     members = block_list[0].reshape(-1)
     present = members >= 0
@@ -143,8 +150,14 @@
         ),
         axis=1,
     )
-    summed = jnp.sum(lax.all_gather(key_sum, "dp"), axis=0)
-    summed, arrived = lax.optimization_barrier((summed, arrived))
+    dp_size = lax.axis_size("dp")
+    summed = key_sum
+    stride = 1
+    while stride < dp_size:
+        summed = summed + lax.ppermute(
+            summed, "dp", [(index, index ^ stride) for index in range(dp_size)]
+        )
+        stride *= 2
     present_count = jnp.sum(present.reshape(groups_here, cluster_cap).astype(jnp.int32), axis=1)
     outgoing = routed_attention(
         recv_row.reshape(groups_here, cluster_cap).astype(jnp.int32),
@@ -152,6 +165,7 @@
         jnp.where(present, members, 0).reshape(groups_here, cluster_cap).astype(jnp.int32),
         arrived,
     )
+    outgoing, summed = lax.optimization_barrier((outgoing, summed))
     returned = lax.all_to_all(outgoing, "seq", split_axis=0, concat_axis=0, tiled=True)
     centroid_next = decay_rate * centroid_sums + (1.0 - decay_rate) * summed
     return unpack(returned) + (centroid_next,)

time: 310 us -> 320 us (1.032)
  the two profiles are of different devices: /device:TPU:26 before, /device:TPU:16 now
where the time goes in v3:
time: 320 us
  waiting for transfers between devices  217 us (68%)
  starting transfers between devices  49.7 us (16%)
  Pallas kernels  20.5 us (6%)
  local copies, waits for them, and re-layouts  15.1 us (5%)
  matrix products  9.52 us (3%)
  other arithmetic  6.88 us (2%)
    all_to_all x1, waiting for transfers between devices, per_device(): lax.all_to_all(outgoing, 'seq', split_axis=0, concat_axis=0, tiled=True)  118 us
    all_to_all x1, waiting for transfers between devices, per_device(): lax.all_to_all(pack((queries, keys, values, cotangent)), 'seq', split_axi...  96.4 us
    pallas_call x1, Pallas kernels, routed_attention(): pl.pallas_call(routed_kernel, out_shape=jax.ShapeDtypeStruct(arrived.shap...  20.5 us
    ppermute x3, starting transfers between devices, per_device(): lax.ppermute(summed, 'dp', [(index, index ^ stride) for index in range(dp...  20 us
    all_to_all x1, starting transfers between devices, per_device(): lax.all_to_all(pack((queries, keys, values, cotangent)), 'seq', split_axi...  17.6 us
    all_to_all x1, starting transfers between devices, per_device(): lax.all_to_all(outgoing, 'seq', split_axis=0, concat_axis=0, tiled=True)  12.1 us
  transfers between devices with their start and end apart: 5, of which 4 were waited for; matrix products, arithmetic and copies ran while one was open for 1% of the time, Pallas kernels for 6%

profile of v3, /device:TPU:16, one launch (start us, length us, event | category | flops | bytes accessed | tf_op | source)
XLA Modules:
  0.0 319.9 jit_solution(14190496832522734430)
XLA Ops:
  0.6 0.7 and_select_fusion.1
  1.3 0.1 copy.58
  1.4 0.1 fusion.15
  1.5 0.1 copy.59
  1.6 1.8 pad_maximum_fusion
  3.4 0.6 copy.77
  4.0 4.4 %convolution_convert_fusion = bf16[16,4,4,64,128]{4,1,3,2,0:T(4,128)(2,1)S(1)} fusion(bf16[4,2,64,16,128]{4,3,2,1,0:T(8,128)(2,1)S(1)} %bitcast.68, pred[16,2]{1,0:T(8,128)(4,1)S(1)} %copy.59, s32[16,2]{1,0:T(8,128)S(1)} %copy.58), kind=kOutput, calls=%fused_computation.1 | convolution fusion | flops 10486016 | bytes 6291616 | tf_op jit(solution)/shard_map/hlcj,ajthd->hlcatd/dot_general | solution.py:109
  8.4 3.1 copy.61
  11.6 0.0 copy-start.1
  11.6 17.6 %all-to-all-start = ((bf16[64,4,64,128]{3,2,1,0:T(8,128)(2,1)}), bf16[64,4,64,128]{3,2,1,0:T(8,128)(2,1)}, u32[]{:S(2)}, u32[]{:S(2)}) async-start(bf16[64,4,64,128]{3,2,1,0:T(8,128)(2,1)} %bitcast.66), calls=%async_computation | async-start | bytes 8388608 | tf_op jit(solution)/shard_map/all_to_all | solution.py:143
  29.2 0.0 copy-done.1
  29.2 0.1 copy.56
  29.3 0.1 reshape_squeeze.8
  29.4 0.1 reshape_squeeze.9
  29.5 0.1 copy.51
  29.7 0.2 convert_reduce_fusion.1
  29.9 0.6 broadcast_select_fusion
  30.5 96.4 %all-to-all-done.arrived_ref = bf16[64,4,64,128]{3,2,1,0:T(8,128)(2,1)} async-done(((bf16[64,4,64,128]{3,2,1,0:T(8,128)(2,1)}), bf16[64,4,64,128]{3,2,1,0:T(8,128)(2,1)}, u32[]{:S(2)}, u32[]{:S(2)}) %all-to-all-start) | async-done | bytes 4194336 | tf_op jit(solution)/shard_map/all_to_all | solution.py:143
  126.9 1.5 convert_reduce_fusion
  128.4 0.6 gather_fusion
  129.1 0.1 select_reduce_fusion
  129.2 1.9 collective-permute-start
  131.1 1.1 collective-permute-done
  132.3 16.1 %collective-permute-start.1 = (f32[32,128]{1,0:T(8,128)S(1)}, f32[32,128]{1,0:T(8,128)S(1)}, u32[]{:S(2)}, u32[]{:S(2)}) collective-permute-start(f32[32,128]{1,0:T(8,128)S(1)} %add.71), channel_id=1, source_target_pairs={{0,128},{64,192},{128,0},{192,64},{256,384},{320,448},{384,256},{4... | collective-permute-start | bytes 49160 | tf_op jit(solution)/shard_map/ppermute | solution.py:157
  148.4 0.1 reduce_sum.50
  148.5 1.6 collective-permute-done.1
  150.1 1.9 collective-permute-start.2
  152.0 1.2 convert_reduce_fusion.2
  153.3 20.5 %shard_map.110 = bf16[64,4,64,128]{3,2,1,0:T(8,128)(2,1)} custom-call(s32[32,4]{1,0:T(8,128)} %get-tuple-element.16.recv_ref, s32[32]{0:T(128)} %get-tuple-element.15.count_ref, s32[32,4]{1,0:T(8,128)} %get-tuple-element.9.member_ref, bf16[64,4,64,128]{3,2,1,0:T(8,128)(2,1)} %all-to-all-done.arrived_ref), custom_call_target="tpu_custom_call" | custom-call | tf_op jit(solution)/shard_map/pallas_call | solution.py:78
  173.8 0.0 collective-permute-done.2
  173.8 0.0 copy-start
  173.8 12.1 %all-to-all-start.1 = ((bf16[64,4,64,128]{3,2,1,0:T(8,128)(2,1)}), bf16[64,4,64,128]{3,2,1,0:T(8,128)(2,1)}, u32[]{:S(2)}, u32[]{:S(2)}) async-start(bf16[64,4,64,128]{3,2,1,0:T(8,128)(2,1)} %shard_map.110), calls=%async_computation.1 | async-start | bytes 8388608 | tf_op jit(solution)/shard_map/all_to_all | solution.py:169
  185.9 0.0 copy-done
  185.9 0.6 multiply_add_fusion
  186.5 118.2 %all-to-all-done.1 = bf16[64,4,64,128]{3,2,1,0:T(8,128)(2,1)} async-done(((bf16[64,4,64,128]{3,2,1,0:T(8,128)(2,1)}), bf16[64,4,64,128]{3,2,1,0:T(8,128)(2,1)}, u32[]{:S(2)}, u32[]{:S(2)}) %all-to-all-start.1) | async-done | bytes 4194336 | tf_op jit(solution)/shard_map/all_to_all | solution.py:169
  304.7 4.6 %fusion.19 = (bf16[16,4,1,1,64,128]{5,4,3,1,0,2:T(8,128)(2,1)S(1)}, bf16[16,4,1,1,64,128]{5,4,3,1,0,2:T(8,128)(2,1)}, bf16[16,4,1,1,64,128]{5,4,3,1,0,2:T(8,128)(2,1)S(1)}, bf16[16,4,1,1,64,128]{5,4,3,1,0,2:T(8,128)(2,1)S(1)}) fusion(bf16[16,4,1,4,64,128]{5,4,3,1,0,2:T(8,128)(2,1)} %bitcast.8), kind=kLoop, calls=%fused_computation.64 | loop fusion | bytes 8388608 | tf_op jit(solution)/shard_map/slice | solution.py:122
  309.3 1.0 fusion.2
  310.3 0.3 copy.66
  310.7 1.0 reshape.336
  311.7 2.2 fusion.3
  313.9 0.3 copy.68
  314.2 1.0 reshape.338
  315.2 1.0 fusion.4
  316.2 0.3 copy.70
  316.6 1.0 reshape.340
  317.6 1.0 fusion.1
  318.6 0.3 copy.64
  318.9 1.0 reshape.334
  (9 shorter events, 0.1 us)
Async XLA Ops:
  11.6 17.7 %copy-start.1 = (s32[1,32,4]{1,2,0:T(4,128)S(1)}, s32[1,32,4]{1,2,0:T(4,128)}, u32[]{:S(2)}) copy-start(s32[1,32,4]{1,2,0:T(4,128)} %param.12) | copy-start | bytes 1540
  11.6 115.3 %all-to-all-start = ((bf16[64,4,64,128]{3,2,1,0:T(8,128)(2,1)}), bf16[64,4,64,128]{3,2,1,0:T(8,128)(2,1)}, u32[]{:S(2)}, u32[]{:S(2)}) async-start(bf16[64,4,64,128]{3,2,1,0:T(8,128)(2,1)} %bitcast.66), calls=%async_computation | async-start | bytes 8388608 | tf_op jit(solution)/shard_map/all_to_all | solution.py:143
  129.2 3.1 collective-permute-start
  132.3 17.8 %collective-permute-start.1 = (f32[32,128]{1,0:T(8,128)S(1)}, f32[32,128]{1,0:T(8,128)S(1)}, u32[]{:S(2)}, u32[]{:S(2)}) collective-permute-start(f32[32,128]{1,0:T(8,128)S(1)} %add.71), channel_id=1, source_target_pairs={{0,128},{64,192},{128,0},{192,64},{256,384},{320,448},{384,256},{4... | collective-permute-start | bytes 49160 | tf_op jit(solution)/shard_map/ppermute | solution.py:157
  150.1 23.7 %collective-permute-start.2 = (f32[32,128]{1,0:T(8,128)S(1)}, f32[32,128]{1,0:T(8,128)S(1)}, u32[]{:S(2)}, u32[]{:S(2)}) collective-permute-start(f32[32,128]{1,0:T(8,128)S(1)} %add.72), channel_id=1, source_target_pairs={{0,256},{64,320},{128,384},{192,448},{256,0},{320,64},{384,128},{4... | collective-permute-start | bytes 49160 | tf_op jit(solution)/shard_map/ppermute | solution.py:157
  173.8 12.1 %copy-start = (f32[32,128]{1,0:T(8,128)S(1)}, f32[32,128]{1,0:T(8,128)}, u32[]{:S(2)}) copy-start(f32[32,128]{1,0:T(8,128)} %param.13) | copy-start | bytes 49156
  173.8 131.0 %all-to-all-start.1 = ((bf16[64,4,64,128]{3,2,1,0:T(8,128)(2,1)}), bf16[64,4,64,128]{3,2,1,0:T(8,128)(2,1)}, u32[]{:S(2)}, u32[]{:S(2)}) async-start(bf16[64,4,64,128]{3,2,1,0:T(8,128)(2,1)} %shard_map.110), calls=%async_computation.1 | async-start | bytes 8388608 | tf_op jit(solution)/shard_map/all_to_all | solution.py:169

commit v4 on v3

--- a/solution.py
+++ b/solution.py
@@ -83,6 +83,65 @@
     )(recv_table, present_count, member_table, arrived)
 
 
+def pack_kernel(dest_ref, *refs):
+    in_refs, out_ref = refs[:-1], refs[-1]
+    head_count, block_count = dest_ref.shape
+    block_len = out_ref.shape[2]
+    head_dim = out_ref.shape[3]
+    out_ref[...] = jnp.zeros(out_ref.shape, out_ref.dtype)
+    for head in range(head_count):
+        for block in range(block_count):
+            slot = dest_ref[head, block]
+            for index, in_ref in enumerate(in_refs):
+                out_ref[slot, index] = in_ref[
+                    block * block_len : (block + 1) * block_len,
+                    head * head_dim : (head + 1) * head_dim,
+                ]
+
+
+def unpack_kernel(dest_ref, in_ref, *out_refs):
+    head_count, block_count = dest_ref.shape
+    block_len = in_ref.shape[2]
+    head_dim = in_ref.shape[3]
+    for head in range(head_count):
+        for block in range(block_count):
+            slot = dest_ref[head, block]
+            for index, out_ref in enumerate(out_refs):
+                out_ref[
+                    block * block_len : (block + 1) * block_len,
+                    head * head_dim : (head + 1) * head_dim,
+                ] = in_ref[slot, index]
+
+
+def pack_blocks(dest_table, sources, slot_count, block_len):
+    smem = pl.BlockSpec(memory_space=pltpu.SMEM)
+    vmem = pl.BlockSpec(memory_space=pltpu.VMEM)
+    head_dim = sources[0].shape[1] // dest_table.shape[0]
+    return pl.pallas_call(
+        pack_kernel,
+        out_shape=jax.ShapeDtypeStruct(
+            (slot_count, len(sources), block_len, head_dim), sources[0].dtype
+        ),
+        in_specs=[smem] + [vmem] * len(sources),
+        out_specs=vmem,
+    )(dest_table, *sources)
+
+
+def unpack_blocks(dest_table, returned, token_count):
+    smem = pl.BlockSpec(memory_space=pltpu.SMEM)
+    vmem = pl.BlockSpec(memory_space=pltpu.VMEM)
+    width = dest_table.shape[0] * returned.shape[3]
+    count = returned.shape[1]
+    return pl.pallas_call(
+        unpack_kernel,
+        out_shape=tuple(
+            jax.ShapeDtypeStruct((token_count, width), returned.dtype) for _ in range(count)
+        ),
+        in_specs=[smem, vmem],
+        out_specs=tuple(vmem for _ in range(count)),
+    )(dest_table, returned)
+
+
 def per_device(queries, keys, values, cotangent, cluster_of, block_list, centroid_sums):
     seq_size = lax.axis_size("seq")
     head_count = cluster_of.shape[1]
@@ -99,35 +158,9 @@
     earlier = jnp.arange(block_count)[:, None] < jnp.arange(block_count)[None, :]
     same_owner = owner_local[:, :, None] == owner_local[:, None, :]
     slot_of = jnp.sum(same_owner & earlier[None], axis=1)
-    selector = owner_local[:, None, None, :] == jnp.arange(owner_count)[None, :, None, None]
-    selector = selector & (slot_of[:, None, None, :] == jnp.arange(slot_cap)[None, None, :, None])
-    selector = selector.astype(jnp.bfloat16)
-
-    def pack(sources):
-        stacked = jnp.stack([item[0] for item in sources])
-        blocks_in = stacked.reshape(len(sources), block_count, block_len, head_count, head_dim)
-        outgoing = jnp.einsum(
-            "hlcj,ajthd->hlcatd", selector, blocks_in, preferred_element_type=jnp.float32
-        )
-        return outgoing.astype(jnp.bfloat16).reshape(
-            seq_size * slot_cap, len(sources), block_len, head_dim
-        )
-
-    def unpack(returned):
-        arranged = returned.reshape(head_count, owner_count, slot_cap, -1, block_len, head_dim)
-        gathered = (
-            jnp.einsum(
-                "hlcj,hlctd->jthd",
-                selector,
-                arranged[:, :, :, index],
-                preferred_element_type=jnp.float32,
-            )
-            for index in range(arranged.shape[3])
-        )
-        return tuple(
-            item.astype(jnp.bfloat16).reshape(1, token_count, head_count * head_dim)
-            for item in gathered
-        )
+    dest_table = (
+        owner_local * slot_cap + jnp.minimum(slot_of, slot_cap - 1)
+    ).astype(jnp.int32) + (jnp.arange(head_count) * owner_count * slot_cap)[:, None].astype(jnp.int32)
 
     members = block_list[0].reshape(-1)
     present = members >= 0
@@ -141,7 +174,16 @@
     recv_row = jnp.where(present, source_dev * slot_cap + slot_at, 0)
 
     arrived = lax.all_to_all(
-        pack((queries, keys, values, cotangent)), "seq", split_axis=0, concat_axis=0, tiled=True
+        pack_blocks(
+            dest_table,
+            (queries[0], keys[0], values[0], cotangent[0]),
+            seq_size * slot_cap,
+            block_len,
+        ),
+        "seq",
+        split_axis=0,
+        concat_axis=0,
+        tiled=True,
     )
     block_sums = jnp.sum(arrived[:, 1].astype(jnp.float32), axis=1)
     key_sum = jnp.sum(
@@ -168,7 +210,8 @@
     outgoing, summed = lax.optimization_barrier((outgoing, summed))
     returned = lax.all_to_all(outgoing, "seq", split_axis=0, concat_axis=0, tiled=True)
     centroid_next = decay_rate * centroid_sums + (1.0 - decay_rate) * summed
-    return unpack(returned) + (centroid_next,)
+    finished = unpack_blocks(dest_table, returned, token_count)
+    return tuple(item[None] for item in finished) + (centroid_next,)
 
 
 def solution(mesh):

time: 320 us -> 305 us (0.953)
  local copies, waits for them, and re-layouts: 15.1 us -> 2.06 us
  matrix products: 9.52 us -> 0 us
  Pallas kernels: 20.5 us -> 28.2 us
    dot_general x5 -> x0, matrix products: 9.52 us -> none  [the longest x4 5.1 us: unpack(): jnp.einsum('hlcj,hlctd->jthd', selector, arranged[:, :, :, index], prefer...]
    pallas_call x0 -> x2, Pallas kernels: none -> 8.49 us  [the longest x1 4.4 us: pack_blocks(): pl.pallas_call(pack_kernel, out_shape=jax.ShapeDtypeStruct((slot_count, l...]
    slice x1 -> x0, local copies, waits for them, and re-layouts: 4.59 us -> none  [unpack(): arranged[:, :, :, index]]
    convert_element_type x5 -> x0, local copies, waits for them, and re-layouts: 4.5 us -> none  [the longest x1 3.13 us: pack(): outgoing.astype(jnp.bfloat16)]
    reshape x4 -> x0, local copies, waits for them, and re-layouts: 4.07 us -> none  [unpack(): item.astype(jnp.bfloat16).reshape(1, token_count, head_count * head_dim)]
where the time goes in v4:
time: 305 us
  waiting for transfers between devices  218 us (71%)
  starting transfers between devices  50.9 us (17%)
  Pallas kernels  28.2 us (9%)
  other arithmetic  5.08 us (2%)
    all_to_all x1, waiting for transfers between devices, per_device(): lax.all_to_all(outgoing, 'seq', split_axis=0, concat_axis=0, tiled=True)  119 us
    all_to_all x1, waiting for transfers between devices, per_device(): lax.all_to_all(pack_blocks(dest_table, (queries[0], keys[0], values[0], c...  96.5 us
    ppermute x3, starting transfers between devices, per_device(): lax.ppermute(summed, 'dp', [(index, index ^ stride) for index in range(dp...  19.9 us
    pallas_call x1, Pallas kernels, routed_attention(): pl.pallas_call(routed_kernel, out_shape=jax.ShapeDtypeStruct(arrived.shap...  19.7 us
    all_to_all x1, starting transfers between devices, per_device(): lax.all_to_all(pack_blocks(dest_table, (queries[0], keys[0], values[0], c...  17.6 us
    all_to_all x1, starting transfers between devices, per_device(): lax.all_to_all(outgoing, 'seq', split_axis=0, concat_axis=0, tiled=True)  13.3 us
  transfers between devices with their start and end apart: 5, of which 4 were waited for; matrix products, arithmetic and copies ran while one was open for 1% of the time, Pallas kernels for 6%

profile of v4, /device:TPU:16, one launch (start us, length us, event | category | flops | bytes accessed | tf_op | source)
XLA Modules:
  0.0 305.0 jit_solution(2290942200872637044)
XLA Ops:
  0.7 0.8 copy.36
  1.4 0.1 copy.40
  1.5 0.1 fusion.7
  1.6 0.1 copy.42
  1.7 0.7 add_add_fusion.dest_ref
  2.3 4.4 %shard_map.110 = bf16[64,4,64,128]{3,2,1,0:T(8,128)(2,1)} custom-call(s32[16,2]{1,0:T(8,128)} %add_add_fusion.dest_ref, bf16[128,2048]{1,0:T(8,128)(2,1)} %bitcast.17, bf16[128,2048]{1,0:T(8,128)(2,1)} %bitcast.18, bf16[128,2048]{1,0:T(8,128)(2,1)} %bitcast.19, bf16[128,2048]{1,0:T(8,128)(2,1)} %bitcast.20), custom_call_target="tpu_custom_call" | custom-call | tf_op jit(solution)/shard_map/pallas_call | solution.py:120
  6.7 0.0 copy-start.1
  6.7 17.6 %all-to-all-start = ((bf16[64,4,64,128]{3,2,1,0:T(8,128)(2,1)}), bf16[64,4,64,128]{3,2,1,0:T(8,128)(2,1)}, u32[]{:S(2)}, u32[]{:S(2)}) async-start(bf16[64,4,64,128]{3,2,1,0:T(8,128)(2,1)} %shard_map.110), calls=%async_computation | async-start | bytes 8388608 | tf_op jit(solution)/shard_map/all_to_all | solution.py:176
  24.4 0.0 copy-done.1
  24.4 0.1 copy.48
  24.5 0.1 reshape_squeeze.8
  24.6 0.1 reshape_squeeze.9
  24.7 0.1 copy.43
  24.8 0.2 convert_reduce_fusion.1
  25.0 0.6 broadcast_select_fusion
  25.6 96.5 %all-to-all-done.arrived_ref = bf16[64,4,64,128]{3,2,1,0:T(8,128)(2,1)} async-done(((bf16[64,4,64,128]{3,2,1,0:T(8,128)(2,1)}), bf16[64,4,64,128]{3,2,1,0:T(8,128)(2,1)}, u32[]{:S(2)}, u32[]{:S(2)}) %all-to-all-start) | async-done | bytes 4194336 | tf_op jit(solution)/shard_map/all_to_all | solution.py:176
  122.2 1.5 convert_reduce_fusion
  123.7 0.6 gather_fusion
  124.3 0.1 select_reduce_fusion
  124.5 1.9 collective-permute-start
  126.4 1.1 collective-permute-done
  127.5 16.1 %collective-permute-start.1 = (f32[32,128]{1,0:T(8,128)S(1)}, f32[32,128]{1,0:T(8,128)S(1)}, u32[]{:S(2)}, u32[]{:S(2)}) collective-permute-start(f32[32,128]{1,0:T(8,128)S(1)} %add.81), channel_id=1, source_target_pairs={{0,128},{64,192},{128,0},{192,64},{256,384},{320,448},{384,256},{4... | collective-permute-start | bytes 49160 | tf_op jit(solution)/shard_map/ppermute | solution.py:199
  143.6 0.1 reduce_sum.51
  143.7 1.6 collective-permute-done.1
  145.3 1.9 collective-permute-start.2
  147.3 1.2 convert_reduce_fusion.2
  148.5 19.7 %shard_map.111 = bf16[64,4,64,128]{3,2,1,0:T(8,128)(2,1)} custom-call(s32[32,4]{1,0:T(8,128)} %get-tuple-element.20.recv_ref, s32[32]{0:T(128)} %get-tuple-element.19.count_ref, s32[32,4]{1,0:T(8,128)} %get-tuple-element.17.member_ref, bf16[64,4,64,128]{3,2,1,0:T(8,128)(2,1)} %all-to-all-done.arrived_ref), custom_call_target="tpu_custom_call" | custom-call | tf_op jit(solution)/shard_map/pallas_call | solution.py:78
  168.2 0.0 collective-permute-done.2
  168.2 0.0 copy-start
  168.2 13.3 %all-to-all-start.1 = ((bf16[64,4,64,128]{3,2,1,0:T(8,128)(2,1)}), bf16[64,4,64,128]{3,2,1,0:T(8,128)(2,1)}, u32[]{:S(2)}, u32[]{:S(2)}) async-start(bf16[64,4,64,128]{3,2,1,0:T(8,128)(2,1)} %shard_map.111), calls=%async_computation.1 | async-start | bytes 8388608 | tf_op jit(solution)/shard_map/all_to_all | solution.py:211
  181.5 0.0 copy-done
  181.5 0.6 multiply_add_fusion
  182.1 118.7 %all-to-all-done.1.in_ref = bf16[64,4,64,128]{3,2,1,0:T(8,128)(2,1)} async-done(((bf16[64,4,64,128]{3,2,1,0:T(8,128)(2,1)}), bf16[64,4,64,128]{3,2,1,0:T(8,128)(2,1)}, u32[]{:S(2)}, u32[]{:S(2)}) %all-to-all-start.1) | async-done | bytes 4194336 | tf_op jit(solution)/shard_map/all_to_all | solution.py:211
  300.9 4.1 %shard_map.112 = (bf16[128,2048]{1,0:T(8,128)(2,1)}, bf16[128,2048]{1,0:T(8,128)(2,1)}, bf16[128,2048]{1,0:T(8,128)(2,1)}, bf16[128,2048]{1,0:T(8,128)(2,1)}) custom-call(s32[16,2]{1,0:T(8,128)} %add_add_fusion.dest_ref, bf16[64,4,64,128]{3,2,1,0:T(8,128)(2,1)} %all-to-all-done.1.in_ref), custom_call_target="tpu_custom_call" | custom-call | tf_op jit(solution)/shard_map/pallas_call | solution.py:135
  (10 shorter events, 0.1 us)
Async XLA Ops:
  6.7 17.7 %copy-start.1 = (s32[1,32,4]{1,2,0:T(4,128)S(1)}, s32[1,32,4]{1,2,0:T(4,128)}, u32[]{:S(2)}) copy-start(s32[1,32,4]{1,2,0:T(4,128)} %param.12) | copy-start | bytes 1540
  6.7 115.4 %all-to-all-start = ((bf16[64,4,64,128]{3,2,1,0:T(8,128)(2,1)}), bf16[64,4,64,128]{3,2,1,0:T(8,128)(2,1)}, u32[]{:S(2)}, u32[]{:S(2)}) async-start(bf16[64,4,64,128]{3,2,1,0:T(8,128)(2,1)} %shard_map.110), calls=%async_computation | async-start | bytes 8388608 | tf_op jit(solution)/shard_map/all_to_all | solution.py:176
  124.5 3.1 %collective-permute-start = (f32[32,128]{1,0:T(8,128)S(1)}, f32[32,128]{1,0:T(8,128)S(1)}, u32[]{:S(2)}, u32[]{:S(2)}) collective-permute-start(f32[32,128]{1,0:T(8,128)S(1)} %select_reduce_fusion), channel_id=1, source_target_pairs={{0,64},{64,0},{128,192},{192,128},{256,320},{320,256},{384,448},{4... | collective-permute-start | bytes 49160 | tf_op jit(solution)/shard_map/ppermute | solution.py:199
  127.5 17.8 %collective-permute-start.1 = (f32[32,128]{1,0:T(8,128)S(1)}, f32[32,128]{1,0:T(8,128)S(1)}, u32[]{:S(2)}, u32[]{:S(2)}) collective-permute-start(f32[32,128]{1,0:T(8,128)S(1)} %add.81), channel_id=1, source_target_pairs={{0,128},{64,192},{128,0},{192,64},{256,384},{320,448},{384,256},{4... | collective-permute-start | bytes 49160 | tf_op jit(solution)/shard_map/ppermute | solution.py:199
  145.3 22.8 %collective-permute-start.2 = (f32[32,128]{1,0:T(8,128)S(1)}, f32[32,128]{1,0:T(8,128)S(1)}, u32[]{:S(2)}, u32[]{:S(2)}) collective-permute-start(f32[32,128]{1,0:T(8,128)S(1)} %add.82), channel_id=1, source_target_pairs={{0,256},{64,320},{128,384},{192,448},{256,0},{320,64},{384,128},{4... | collective-permute-start | bytes 49160 | tf_op jit(solution)/shard_map/ppermute | solution.py:199
  168.2 13.3 %copy-start = (f32[32,128]{1,0:T(8,128)S(1)}, f32[32,128]{1,0:T(8,128)}, u32[]{:S(2)}) copy-start(f32[32,128]{1,0:T(8,128)} %param.13) | copy-start | bytes 49156
  168.2 132.7 %all-to-all-start.1 = ((bf16[64,4,64,128]{3,2,1,0:T(8,128)(2,1)}), bf16[64,4,64,128]{3,2,1,0:T(8,128)(2,1)}, u32[]{:S(2)}, u32[]{:S(2)}) async-start(bf16[64,4,64,128]{3,2,1,0:T(8,128)(2,1)} %shard_map.111), calls=%async_computation.1 | async-start | bytes 8388608 | tf_op jit(solution)/shard_map/all_to_all | solution.py:211

commit v5 on v4

--- a/solution.py
+++ b/solution.py
@@ -192,6 +192,14 @@
         ),
         axis=1,
     )
+    present_count = jnp.sum(present.reshape(groups_here, cluster_cap).astype(jnp.int32), axis=1)
+    outgoing = routed_attention(
+        recv_row.reshape(groups_here, cluster_cap).astype(jnp.int32),
+        present_count,
+        jnp.where(present, members, 0).reshape(groups_here, cluster_cap).astype(jnp.int32),
+        arrived,
+    )
+    outgoing, key_sum = lax.optimization_barrier((outgoing, key_sum))
     dp_size = lax.axis_size("dp")
     summed = key_sum
     stride = 1
@@ -200,14 +208,6 @@
             summed, "dp", [(index, index ^ stride) for index in range(dp_size)]
         )
         stride *= 2
-    present_count = jnp.sum(present.reshape(groups_here, cluster_cap).astype(jnp.int32), axis=1)
-    outgoing = routed_attention(
-        recv_row.reshape(groups_here, cluster_cap).astype(jnp.int32),
-        present_count,
-        jnp.where(present, members, 0).reshape(groups_here, cluster_cap).astype(jnp.int32),
-        arrived,
-    )
-    outgoing, summed = lax.optimization_barrier((outgoing, summed))
     returned = lax.all_to_all(outgoing, "seq", split_axis=0, concat_axis=0, tiled=True)
     centroid_next = decay_rate * centroid_sums + (1.0 - decay_rate) * summed
     finished = unpack_blocks(dest_table, returned, token_count)

time: 305 us -> 288 us (0.944)
  waiting for transfers between devices: 218 us -> 195 us
  starting transfers between devices: 50.9 us -> 54.4 us
    all_to_all x1, waiting for transfers between devices: 119 us -> 9.49 us  [per_device(): lax.all_to_all(outgoing, 'seq', split_axis=0, concat_axis=0, tiled=True)]
    ppermute x3, waiting for transfers between devices: 2.75 us -> 90.5 us  [per_device(): lax.ppermute(summed, 'dp', [(index, index ^ stride) for index in range(dp...]
  transfers between devices with their start and end apart: 5 -> 5, of which waited for: 4 -> 5; matrix products, arithmetic and copies ran while one was open for 1% -> 1% of each run, Pallas kernels for 6% -> 0%
where the time goes in v5:
time: 288 us; the launch traced here: 287 us
  waiting for transfers between devices  195 us (68%)
  starting transfers between devices  54.4 us (19%)
  Pallas kernels  30 us (10%)
  other arithmetic  5.08 us (2%)
    all_to_all x1, waiting for transfers between devices, per_device(): lax.all_to_all(pack_blocks(dest_table, (queries[0], keys[0], values[0], c...  95.2 us
    ppermute x3, waiting for transfers between devices, per_device(): lax.ppermute(summed, 'dp', [(index, index ^ stride) for index in range(dp...  90.5 us
    ppermute x3, starting transfers between devices, per_device(): lax.ppermute(summed, 'dp', [(index, index ^ stride) for index in range(dp...  22.8 us
    pallas_call x1, Pallas kernels, routed_attention(): pl.pallas_call(routed_kernel, out_shape=jax.ShapeDtypeStruct(arrived.shap...  21.5 us
    all_to_all x1, starting transfers between devices, per_device(): lax.all_to_all(pack_blocks(dest_table, (queries[0], keys[0], values[0], c...  17.6 us
    all_to_all x1, starting transfers between devices, per_device(): lax.all_to_all(outgoing, 'seq', split_axis=0, concat_axis=0, tiled=True)  14 us
    all_to_all x1, waiting for transfers between devices, per_device(): lax.all_to_all(outgoing, 'seq', split_axis=0, concat_axis=0, tiled=True)  9.49 us
  transfers between devices with their start and end apart: 5, of which 5 were waited for; matrix products, arithmetic and copies ran while one was open for 1% of the time, Pallas kernels for 0%

profile of v5, /device:TPU:16, one launch (start us, length us, event | category | flops | bytes accessed | tf_op | source)
XLA Modules:
  0.0 287.5 jit_solution(4292316827949746061)
XLA Ops:
  0.7 0.8 copy.36
  1.4 0.1 copy.40
  1.5 0.1 fusion.7
  1.6 0.1 copy.42
  1.7 0.7 add_add_fusion.dest_ref
  2.3 4.4 %shard_map.110 = bf16[64,4,64,128]{3,2,1,0:T(8,128)(2,1)} custom-call(s32[16,2]{1,0:T(8,128)} %add_add_fusion.dest_ref, bf16[128,2048]{1,0:T(8,128)(2,1)} %bitcast.17, bf16[128,2048]{1,0:T(8,128)(2,1)} %bitcast.18, bf16[128,2048]{1,0:T(8,128)(2,1)} %bitcast.19, bf16[128,2048]{1,0:T(8,128)(2,1)} %bitcast.20), custom_call_target="tpu_custom_call" | custom-call | tf_op jit(solution)/shard_map/pallas_call | solution.py:120
  6.7 0.0 copy-start.1
  6.7 17.6 %all-to-all-start = ((bf16[64,4,64,128]{3,2,1,0:T(8,128)(2,1)}), bf16[64,4,64,128]{3,2,1,0:T(8,128)(2,1)}, u32[]{:S(2)}, u32[]{:S(2)}) async-start(bf16[64,4,64,128]{3,2,1,0:T(8,128)(2,1)} %shard_map.110), calls=%async_computation | async-start | bytes 8388608 | tf_op jit(solution)/shard_map/all_to_all | solution.py:176
  24.4 0.0 copy-done.1
  24.4 0.1 copy.48
  24.5 0.1 reshape_squeeze.8
  24.6 0.1 reshape_squeeze.9
  24.7 0.1 copy.43
  24.8 0.2 convert_reduce_fusion.1
  25.0 0.1 reduce_sum.51
  25.2 0.6 broadcast_select_fusion
  25.8 1.2 convert_reduce_fusion.2
  27.0 95.2 %all-to-all-done.arrived_ref = bf16[64,4,64,128]{3,2,1,0:T(8,128)(2,1)} async-done(((bf16[64,4,64,128]{3,2,1,0:T(8,128)(2,1)}), bf16[64,4,64,128]{3,2,1,0:T(8,128)(2,1)}, u32[]{:S(2)}, u32[]{:S(2)}) %all-to-all-start) | async-done | bytes 4194336 | tf_op jit(solution)/shard_map/all_to_all | solution.py:176
  122.2 1.5 convert_reduce_fusion
  123.7 0.6 gather_fusion
  124.3 0.1 select_reduce_fusion
  124.5 21.5 %shard_map.111 = bf16[64,4,64,128]{3,2,1,0:T(8,128)(2,1)} custom-call(s32[32,4]{1,0:T(8,128)} %get-tuple-element.20.recv_ref, s32[32]{0:T(128)} %get-tuple-element.19.count_ref, s32[32,4]{1,0:T(8,128)} %get-tuple-element.17.member_ref, bf16[64,4,64,128]{3,2,1,0:T(8,128)(2,1)} %all-to-all-done.arrived_ref), custom_call_target="tpu_custom_call" | custom-call | tf_op jit(solution)/shard_map/pallas_call | solution.py:78
  146.0 0.0 copy-start
  146.0 14.0 %all-to-all-start.1 = ((bf16[64,4,64,128]{3,2,1,0:T(8,128)(2,1)}), bf16[64,4,64,128]{3,2,1,0:T(8,128)(2,1)}, u32[]{:S(2)}, u32[]{:S(2)}) async-start(bf16[64,4,64,128]{3,2,1,0:T(8,128)(2,1)} %shard_map.111), calls=%async_computation.1 | async-start | bytes 8388608 | tf_op jit(solution)/shard_map/all_to_all | solution.py:211
  159.9 1.9 collective-permute-start
  161.9 1.1 collective-permute-done
  163.0 8.9 %collective-permute-start.1 = (f32[32,128]{1,0:T(8,128)S(1)}, f32[32,128]{1,0:T(8,128)S(1)}, u32[]{:S(2)}, u32[]{:S(2)}) collective-permute-start(f32[32,128]{1,0:T(8,128)S(1)} %add.81), channel_id=1, source_target_pairs={{0,128},{64,192},{128,0},{192,64},{256,384},{320,448},{384,256},{4... | collective-permute-start | bytes 49160 | tf_op jit(solution)/shard_map/ppermute | solution.py:207
  171.9 87.6 %collective-permute-done.1 = f32[32,128]{1,0:T(8,128)S(1)} collective-permute-done((f32[32,128]{1,0:T(8,128)S(1)}, f32[32,128]{1,0:T(8,128)S(1)}, u32[]{:S(2)}, u32[]{:S(2)}) %collective-permute-start.1) | collective-permute-done | bytes 16416 | tf_op jit(solution)/shard_map/ppermute | solution.py:207
  259.6 12.0 %collective-permute-start.2 = (f32[32,128]{1,0:T(8,128)S(1)}, f32[32,128]{1,0:T(8,128)S(1)}, u32[]{:S(2)}, u32[]{:S(2)}) collective-permute-start(f32[32,128]{1,0:T(8,128)S(1)} %add.82), channel_id=1, source_target_pairs={{0,256},{64,320},{128,384},{192,448},{256,0},{320,64},{384,128},{4... | collective-permute-start | bytes 49160 | tf_op jit(solution)/shard_map/ppermute | solution.py:207
  271.6 1.7 collective-permute-done.2
  273.3 0.0 copy-done
  273.3 0.6 multiply_add_fusion
  273.9 9.5 %all-to-all-done.1.in_ref = bf16[64,4,64,128]{3,2,1,0:T(8,128)(2,1)} async-done(((bf16[64,4,64,128]{3,2,1,0:T(8,128)(2,1)}), bf16[64,4,64,128]{3,2,1,0:T(8,128)(2,1)}, u32[]{:S(2)}, u32[]{:S(2)}) %all-to-all-start.1) | async-done | bytes 4194336 | tf_op jit(solution)/shard_map/all_to_all | solution.py:211
  283.4 4.1 %shard_map.112 = (bf16[128,2048]{1,0:T(8,128)(2,1)}, bf16[128,2048]{1,0:T(8,128)(2,1)}, bf16[128,2048]{1,0:T(8,128)(2,1)}, bf16[128,2048]{1,0:T(8,128)(2,1)}) custom-call(s32[16,2]{1,0:T(8,128)} %add_add_fusion.dest_ref, bf16[64,4,64,128]{3,2,1,0:T(8,128)(2,1)} %all-to-all-done.1.in_ref), custom_call_target="tpu_custom_call" | custom-call | tf_op jit(solution)/shard_map/pallas_call | solution.py:135
  (9 shorter events, 0.1 us)
Async XLA Ops:
  6.7 17.7 %copy-start.1 = (s32[1,32,4]{1,2,0:T(4,128)S(1)}, s32[1,32,4]{1,2,0:T(4,128)}, u32[]{:S(2)}) copy-start(s32[1,32,4]{1,2,0:T(4,128)} %param.12) | copy-start | bytes 1540
  6.7 115.4 %all-to-all-start = ((bf16[64,4,64,128]{3,2,1,0:T(8,128)(2,1)}), bf16[64,4,64,128]{3,2,1,0:T(8,128)(2,1)}, u32[]{:S(2)}, u32[]{:S(2)}) async-start(bf16[64,4,64,128]{3,2,1,0:T(8,128)(2,1)} %shard_map.110), calls=%async_computation | async-start | bytes 8388608 | tf_op jit(solution)/shard_map/all_to_all | solution.py:176
  146.0 127.3 %copy-start = (f32[32,128]{1,0:T(8,128)S(1)}, f32[32,128]{1,0:T(8,128)}, u32[]{:S(2)}) copy-start(f32[32,128]{1,0:T(8,128)} %param.13) | copy-start | bytes 49156
  146.0 137.4 %all-to-all-start.1 = ((bf16[64,4,64,128]{3,2,1,0:T(8,128)(2,1)}), bf16[64,4,64,128]{3,2,1,0:T(8,128)(2,1)}, u32[]{:S(2)}, u32[]{:S(2)}) async-start(bf16[64,4,64,128]{3,2,1,0:T(8,128)(2,1)} %shard_map.111), calls=%async_computation.1 | async-start | bytes 8388608 | tf_op jit(solution)/shard_map/all_to_all | solution.py:211
  159.9 3.1 %collective-permute-start = (f32[32,128]{1,0:T(8,128)S(1)}, f32[32,128]{1,0:T(8,128)S(1)}, u32[]{:S(2)}, u32[]{:S(2)}) collective-permute-start(f32[32,128]{1,0:T(8,128)S(1)} %select_reduce_fusion), channel_id=1, source_target_pairs={{0,64},{64,0},{128,192},{192,128},{256,320},{320,256},{384,448},{4... | collective-permute-start | bytes 49160 | tf_op jit(solution)/shard_map/ppermute | solution.py:207
  163.0 96.5 %collective-permute-start.1 = (f32[32,128]{1,0:T(8,128)S(1)}, f32[32,128]{1,0:T(8,128)S(1)}, u32[]{:S(2)}, u32[]{:S(2)}) collective-permute-start(f32[32,128]{1,0:T(8,128)S(1)} %add.81), channel_id=1, source_target_pairs={{0,128},{64,192},{128,0},{192,64},{256,384},{320,448},{384,256},{4... | collective-permute-start | bytes 49160 | tf_op jit(solution)/shard_map/ppermute | solution.py:207
  259.6 13.7 %collective-permute-start.2 = (f32[32,128]{1,0:T(8,128)S(1)}, f32[32,128]{1,0:T(8,128)S(1)}, u32[]{:S(2)}, u32[]{:S(2)}) collective-permute-start(f32[32,128]{1,0:T(8,128)S(1)} %add.82), channel_id=1, source_target_pairs={{0,256},{64,320},{128,384},{192,448},{256,0},{320,64},{384,128},{4... | collective-permute-start | bytes 49160 | tf_op jit(solution)/shard_map/ppermute | solution.py:207

commit v6 on v5

--- a/solution.py
+++ b/solution.py
@@ -201,13 +201,19 @@
     )
     outgoing, key_sum = lax.optimization_barrier((outgoing, key_sum))
     dp_size = lax.axis_size("dp")
-    summed = key_sum
-    stride = 1
-    while stride < dp_size:
-        summed = summed + lax.ppermute(
-            summed, "dp", [(index, index ^ stride) for index in range(dp_size)]
-        )
-        stride *= 2
+    received = jnp.stack(
+        [key_sum]
+        + [
+            lax.ppermute(
+                key_sum, "dp", [(index, (index + shift) % dp_size) for index in range(dp_size)]
+            )
+            for shift in range(1, dp_size)
+        ]
+    )
+    dp_index = lax.axis_index("dp")
+    summed = received[dp_index % dp_size]
+    for source in range(1, dp_size):
+        summed = summed + received[(dp_index - source) % dp_size]
     returned = lax.all_to_all(outgoing, "seq", split_axis=0, concat_axis=0, tiled=True)
     centroid_next = decay_rate * centroid_sums + (1.0 - decay_rate) * summed
     finished = unpack_blocks(dest_table, returned, token_count)

time: 288 us -> 285 us (0.990)
  the two profiles are of different devices: /device:TPU:16 before, /device:TPU:72 now
where the time goes in v6:
time: 285 us; the launch traced here: 284 us
  waiting for transfers between devices  197 us (69%)
  starting transfers between devices  50.4 us (18%)
  Pallas kernels  28.4 us (10%)
  other arithmetic  5.08 us (2%)
    all_to_all x1, waiting for transfers between devices, per_device(): lax.all_to_all(pack_blocks(dest_table, (queries[0], keys[0], values[0], c...  105 us
    ppermute x7, waiting for transfers between devices, per_device(): lax.ppermute(key_sum, 'dp', [(index, (index + shift) % dp_size) for index...  79.2 us
    pallas_call x1, Pallas kernels, routed_attention(): pl.pallas_call(routed_kernel, out_shape=jax.ShapeDtypeStruct(arrived.shap...  19.9 us
    all_to_all x1, starting transfers between devices, per_device(): lax.all_to_all(pack_blocks(dest_table, (queries[0], keys[0], values[0], c...  17.7 us
    ppermute x7, starting transfers between devices, per_device(): lax.ppermute(key_sum, 'dp', [(index, (index + shift) % dp_size) for index...  17.5 us
    all_to_all x1, starting transfers between devices, per_device(): lax.all_to_all(outgoing, 'seq', split_axis=0, concat_axis=0, tiled=True)  15.2 us
    all_to_all x1, waiting for transfers between devices, per_device(): lax.all_to_all(outgoing, 'seq', split_axis=0, concat_axis=0, tiled=True)  13 us
  transfers between devices with their start and end apart: 9, of which 6 were waited for; matrix products, arithmetic and copies ran while one was open for 1% of the time, Pallas kernels for 0%

profile of v6, /device:TPU:72, one launch (start us, length us, event | category | flops | bytes accessed | tf_op | source)
XLA Modules:
  0.0 284.4 jit_solution(10412403059399713010)
XLA Ops:
  0.7 0.8 copy.36
  1.4 0.1 copy.40
  1.5 0.1 fusion.7
  1.6 0.1 copy.42
  1.7 0.7 add_add_fusion.dest_ref
  2.3 4.4 %shard_map.110 = bf16[64,4,64,128]{3,2,1,0:T(8,128)(2,1)} custom-call(s32[16,2]{1,0:T(8,128)} %add_add_fusion.dest_ref, bf16[128,2048]{1,0:T(8,128)(2,1)} %bitcast.35, bf16[128,2048]{1,0:T(8,128)(2,1)} %bitcast.36, bf16[128,2048]{1,0:T(8,128)(2,1)} %bitcast.37, bf16[128,2048]{1,0:T(8,128)(2,1)} %bitcast.38), custom_call_target="tpu_custom_call" | custom-call | tf_op jit(solution)/shard_map/pallas_call | solution.py:120
  6.7 0.0 copy-start.1
  6.7 17.7 %all-to-all-start = ((bf16[64,4,64,128]{3,2,1,0:T(8,128)(2,1)}), bf16[64,4,64,128]{3,2,1,0:T(8,128)(2,1)}, u32[]{:S(2)}, u32[]{:S(2)}) async-start(bf16[64,4,64,128]{3,2,1,0:T(8,128)(2,1)} %shard_map.110), calls=%async_computation | async-start | bytes 8388608 | tf_op jit(solution)/shard_map/all_to_all | solution.py:176
  24.4 0.0 copy-done.1
  24.4 0.1 copy.48
  24.5 0.1 reshape_squeeze.8
  24.6 0.1 reshape_squeeze.9
  24.7 0.1 copy.43
  24.8 0.2 convert_reduce_fusion.1
  25.0 0.1 reduce_sum.51
  25.2 0.6 broadcast_select_fusion
  25.8 1.2 convert_reduce_fusion.2
  27.0 105.2 %all-to-all-done.arrived_ref = bf16[64,4,64,128]{3,2,1,0:T(8,128)(2,1)} async-done(((bf16[64,4,64,128]{3,2,1,0:T(8,128)(2,1)}), bf16[64,4,64,128]{3,2,1,0:T(8,128)(2,1)}, u32[]{:S(2)}, u32[]{:S(2)}) %all-to-all-start) | async-done | bytes 4194336 | tf_op jit(solution)/shard_map/all_to_all | solution.py:176
  132.3 1.5 convert_reduce_fusion
  133.8 0.6 gather_fusion
  134.4 0.1 select_reduce_fusion
  134.5 19.9 %shard_map.111 = bf16[64,4,64,128]{3,2,1,0:T(8,128)(2,1)} custom-call(s32[32,4]{1,0:T(8,128)} %get-tuple-element.20.recv_ref, s32[32]{0:T(128)} %get-tuple-element.19.count_ref, s32[32,4]{1,0:T(8,128)} %get-tuple-element.17.member_ref, bf16[64,4,64,128]{3,2,1,0:T(8,128)(2,1)} %all-to-all-done.arrived_ref), custom_call_target="tpu_custom_call" | custom-call | tf_op jit(solution)/shard_map/pallas_call | solution.py:78
  154.5 0.0 copy-start
  154.5 15.2 %all-to-all-start.1 = ((bf16[64,4,64,128]{3,2,1,0:T(8,128)(2,1)}), bf16[64,4,64,128]{3,2,1,0:T(8,128)(2,1)}, u32[]{:S(2)}, u32[]{:S(2)}) async-start(bf16[64,4,64,128]{3,2,1,0:T(8,128)(2,1)} %shard_map.111), calls=%async_computation.1 | async-start | bytes 8388608 | tf_op jit(solution)/shard_map/all_to_all | solution.py:217
  169.9 1.9 collective-permute-start
  171.8 1.9 collective-permute-start.1
  173.7 1.9 collective-permute-start.2
  175.6 6.0 %collective-permute-start.3 = (f32[32,128]{1,0:T(8,128)S(1)}, f32[32,128]{1,0:T(8,128)S(1)}, u32[]{:S(2)}, u32[]{:S(2)}) collective-permute-start(f32[32,128]{1,0:T(8,128)S(1)} %select_reduce_fusion), channel_id=1, source_target_pairs={{0,256},{64,320},{128,384},{192,448},{256,0},{320,64},{384,128},{4... | collective-permute-start | bytes 49160 | tf_op jit(solution)/shard_map/ppermute | solution.py:207
  181.6 1.9 collective-permute-start.4
  183.6 64.6 %collective-permute-done = f32[32,128]{1,0:T(8,128)S(1)} collective-permute-done((f32[32,128]{1,0:T(8,128)S(1)}, f32[32,128]{1,0:T(8,128)S(1)}, u32[]{:S(2)}, u32[]{:S(2)}) %collective-permute-start) | collective-permute-done | bytes 16416 | tf_op jit(solution)/shard_map/ppermute | solution.py:207
  248.2 1.9 collective-permute-start.5
  250.1 1.3 collective-permute-done.1
  251.4 1.9 collective-permute-start.6
  253.3 0.0 collective-permute-done.2
  253.3 0.0 collective-permute-done.3
  253.3 0.0 collective-permute-done.4
  253.4 13.1 %collective-permute-done.5 = f32[32,128]{1,0:T(8,128)S(1)} collective-permute-done((f32[32,128]{1,0:T(8,128)S(1)}, f32[32,128]{1,0:T(8,128)S(1)}, u32[]{:S(2)}, u32[]{:S(2)}) %collective-permute-start.5) | collective-permute-done | bytes 16416 | tf_op jit(solution)/shard_map/ppermute | solution.py:207
  266.4 0.3 collective-permute-done.6
  266.7 0.0 copy-done
  266.7 0.6 bitcast_add_fusion
  267.3 13.0 %all-to-all-done.1.in_ref = bf16[64,4,64,128]{3,2,1,0:T(8,128)(2,1)} async-done(((bf16[64,4,64,128]{3,2,1,0:T(8,128)(2,1)}), bf16[64,4,64,128]{3,2,1,0:T(8,128)(2,1)}, u32[]{:S(2)}, u32[]{:S(2)}) %all-to-all-start.1) | async-done | bytes 4194336 | tf_op jit(solution)/shard_map/all_to_all | solution.py:217
  280.3 4.1 %shard_map.112 = (bf16[128,2048]{1,0:T(8,128)(2,1)}, bf16[128,2048]{1,0:T(8,128)(2,1)}, bf16[128,2048]{1,0:T(8,128)(2,1)}, bf16[128,2048]{1,0:T(8,128)(2,1)}) custom-call(s32[16,2]{1,0:T(8,128)} %add_add_fusion.dest_ref, bf16[64,4,64,128]{3,2,1,0:T(8,128)(2,1)} %all-to-all-done.1.in_ref), custom_call_target="tpu_custom_call" | custom-call | tf_op jit(solution)/shard_map/pallas_call | solution.py:135
  (15 shorter events, 0.1 us)
Async XLA Ops:
  6.7 17.7 %copy-start.1 = (s32[1,32,4]{1,2,0:T(4,128)S(1)}, s32[1,32,4]{1,2,0:T(4,128)}, u32[]{:S(2)}) copy-start(s32[1,32,4]{1,2,0:T(4,128)} %param.12) | copy-start | bytes 1540
  6.7 125.5 %all-to-all-start = ((bf16[64,4,64,128]{3,2,1,0:T(8,128)(2,1)}), bf16[64,4,64,128]{3,2,1,0:T(8,128)(2,1)}, u32[]{:S(2)}, u32[]{:S(2)}) async-start(bf16[64,4,64,128]{3,2,1,0:T(8,128)(2,1)} %shard_map.110), calls=%async_computation | async-start | bytes 8388608 | tf_op jit(solution)/shard_map/all_to_all | solution.py:176
  154.5 112.2 %copy-start = (f32[32,128]{1,0:T(8,128)S(1)}, f32[32,128]{1,0:T(8,128)}, u32[]{:S(2)}) copy-start(f32[32,128]{1,0:T(8,128)} %param.13) | copy-start | bytes 49156
  154.5 125.9 %all-to-all-start.1 = ((bf16[64,4,64,128]{3,2,1,0:T(8,128)(2,1)}), bf16[64,4,64,128]{3,2,1,0:T(8,128)(2,1)}, u32[]{:S(2)}, u32[]{:S(2)}) async-start(bf16[64,4,64,128]{3,2,1,0:T(8,128)(2,1)} %shard_map.111), calls=%async_computation.1 | async-start | bytes 8388608 | tf_op jit(solution)/shard_map/all_to_all | solution.py:217
  169.9 78.3 %collective-permute-start = (f32[32,128]{1,0:T(8,128)S(1)}, f32[32,128]{1,0:T(8,128)S(1)}, u32[]{:S(2)}, u32[]{:S(2)}) collective-permute-start(f32[32,128]{1,0:T(8,128)S(1)} %select_reduce_fusion), channel_id=1, source_target_pairs={{0,64},{64,128},{128,192},{192,256},{256,320},{320,384},{384,448},... | collective-permute-start | bytes 49160 | tf_op jit(solution)/shard_map/ppermute | solution.py:207
  171.8 79.6 %collective-permute-start.1 = (f32[32,128]{1,0:T(8,128)S(1)}, f32[32,128]{1,0:T(8,128)S(1)}, u32[]{:S(2)}, u32[]{:S(2)}) collective-permute-start(f32[32,128]{1,0:T(8,128)S(1)} %select_reduce_fusion), channel_id=1, source_target_pairs={{0,128},{64,192},{128,256},{192,320},{256,384},{320,448},{384,0},{... | collective-permute-start | bytes 49160 | tf_op jit(solution)/shard_map/ppermute | solution.py:207
  173.7 79.6 %collective-permute-start.2 = (f32[32,128]{1,0:T(8,128)S(1)}, f32[32,128]{1,0:T(8,128)S(1)}, u32[]{:S(2)}, u32[]{:S(2)}) collective-permute-start(f32[32,128]{1,0:T(8,128)S(1)} %select_reduce_fusion), channel_id=1, source_target_pairs={{0,192},{64,256},{128,320},{192,384},{256,448},{320,0},{384,64},{4... | collective-permute-start | bytes 49160 | tf_op jit(solution)/shard_map/ppermute | solution.py:207
  175.6 77.7 %collective-permute-start.3 = (f32[32,128]{1,0:T(8,128)S(1)}, f32[32,128]{1,0:T(8,128)S(1)}, u32[]{:S(2)}, u32[]{:S(2)}) collective-permute-start(f32[32,128]{1,0:T(8,128)S(1)} %select_reduce_fusion), channel_id=1, source_target_pairs={{0,256},{64,320},{128,384},{192,448},{256,0},{320,64},{384,128},{4... | collective-permute-start | bytes 49160 | tf_op jit(solution)/shard_map/ppermute | solution.py:207
  181.6 71.7 %collective-permute-start.4 = (f32[32,128]{1,0:T(8,128)S(1)}, f32[32,128]{1,0:T(8,128)S(1)}, u32[]{:S(2)}, u32[]{:S(2)}) collective-permute-start(f32[32,128]{1,0:T(8,128)S(1)} %select_reduce_fusion), channel_id=1, source_target_pairs={{0,320},{64,384},{128,448},{192,0},{256,64},{320,128},{384,192},{4... | collective-permute-start | bytes 49160 | tf_op jit(solution)/shard_map/ppermute | solution.py:207
  248.2 18.2 %collective-permute-start.5 = (f32[32,128]{1,0:T(8,128)S(1)}, f32[32,128]{1,0:T(8,128)S(1)}, u32[]{:S(2)}, u32[]{:S(2)}) collective-permute-start(f32[32,128]{1,0:T(8,128)S(1)} %select_reduce_fusion), channel_id=1, source_target_pairs={{0,384},{64,448},{128,0},{192,64},{256,128},{320,192},{384,256},{4... | collective-permute-start | bytes 49160 | tf_op jit(solution)/shard_map/ppermute | solution.py:207
  251.4 15.3 %collective-permute-start.6 = (f32[32,128]{1,0:T(8,128)S(1)}, f32[32,128]{1,0:T(8,128)S(1)}, u32[]{:S(2)}, u32[]{:S(2)}) collective-permute-start(f32[32,128]{1,0:T(8,128)S(1)} %select_reduce_fusion), channel_id=1, source_target_pairs={{0,448},{64,0},{128,64},{192,128},{256,192},{320,256},{384,320},{4... | collective-permute-start | bytes 49160 | tf_op jit(solution)/shard_map/ppermute | solution.py:207

commit v7 on v6

--- a/solution.py
+++ b/solution.py
@@ -26,13 +26,14 @@
     out_full = jnp.dot(weights, v, preferred_element_type=jnp.float32)
     dprobs = lax.dot_general(g, v, (((1,), (1,)), ((), ())), preferred_element_type=jnp.float32)
     row_dot = jnp.sum(g.astype(jnp.float32) * out_full, axis=-1, keepdims=True)
-    dscores_wide = probabilities * (dprobs - row_dot) * score_scale
-    dscores = dscores_wide.astype(jnp.bfloat16)
-    grad_values = jnp.dot(
-        probabilities.T.astype(jnp.bfloat16), g, preferred_element_type=jnp.float32
+    dscores = (probabilities * (dprobs - row_dot) * score_scale).astype(jnp.bfloat16)
+    grad_values = lax.dot_general(
+        weights, g, (((0,), (0,)), ((), ())), preferred_element_type=jnp.float32
     )
     grad_queries = jnp.dot(dscores, k, preferred_element_type=jnp.float32)
-    grad_keys = jnp.dot(dscores_wide.T.astype(jnp.bfloat16), q, preferred_element_type=jnp.float32)
+    grad_keys = lax.dot_general(
+        dscores, q, (((0,), (0,)), ((), ())), preferred_element_type=jnp.float32
+    )
     return (out_full, grad_queries, grad_keys, grad_values)
 
 

time: 285 us -> 286 us (level)
  the two profiles are of different devices: /device:TPU:72 before, /device:TPU:40 now
where the time goes in v7:
time: 286 us; the launch traced here: 285 us
  waiting for transfers between devices  197 us (69%)
  starting transfers between devices  52.2 us (18%)
  Pallas kernels  27.6 us (10%)
  other arithmetic  5.08 us (2%)
    all_to_all x1, waiting for transfers between devices, per_device(): lax.all_to_all(pack_blocks(dest_table, (queries[0], keys[0], values[0], c...  105 us
    ppermute x7, waiting for transfers between devices, per_device(): lax.ppermute(key_sum, 'dp', [(index, (index + shift) % dp_size) for index...  76.7 us
    pallas_call x1, Pallas kernels, routed_attention(): pl.pallas_call(routed_kernel, out_shape=jax.ShapeDtypeStruct(arrived.shap...  19.1 us
    all_to_all x1, starting transfers between devices, per_device(): lax.all_to_all(pack_blocks(dest_table, (queries[0], keys[0], values[0], c...  19 us
    ppermute x7, starting transfers between devices, per_device(): lax.ppermute(key_sum, 'dp', [(index, (index + shift) % dp_size) for index...  17.5 us
    all_to_all x1, starting transfers between devices, per_device(): lax.all_to_all(outgoing, 'seq', split_axis=0, concat_axis=0, tiled=True)  15.7 us
    all_to_all x1, waiting for transfers between devices, per_device(): lax.all_to_all(outgoing, 'seq', split_axis=0, concat_axis=0, tiled=True)  15.1 us
  transfers between devices with their start and end apart: 9, of which 6 were waited for; matrix products, arithmetic and copies ran while one was open for 1% of the time, Pallas kernels for 0%

profile of v7, /device:TPU:40, one launch (start us, length us, event | category | flops | bytes accessed | tf_op | source)
XLA Modules:
  0.0 285.3 jit_solution(7521768143597199668)
XLA Ops:
  0.7 0.8 copy.36
  1.4 0.1 copy.40
  1.5 0.1 fusion.7
  1.6 0.1 copy.42
  1.7 0.7 add_add_fusion.dest_ref
  2.3 4.4 %shard_map.110 = bf16[64,4,64,128]{3,2,1,0:T(8,128)(2,1)} custom-call(s32[16,2]{1,0:T(8,128)} %add_add_fusion.dest_ref, bf16[128,2048]{1,0:T(8,128)(2,1)} %bitcast.35, bf16[128,2048]{1,0:T(8,128)(2,1)} %bitcast.36, bf16[128,2048]{1,0:T(8,128)(2,1)} %bitcast.37, bf16[128,2048]{1,0:T(8,128)(2,1)} %bitcast.38), custom_call_target="tpu_custom_call" | custom-call | tf_op jit(solution)/shard_map/pallas_call | solution.py:121
  6.7 0.0 copy-start.1
  6.7 19.0 %all-to-all-start = ((bf16[64,4,64,128]{3,2,1,0:T(8,128)(2,1)}), bf16[64,4,64,128]{3,2,1,0:T(8,128)(2,1)}, u32[]{:S(2)}, u32[]{:S(2)}) async-start(bf16[64,4,64,128]{3,2,1,0:T(8,128)(2,1)} %shard_map.110), calls=%async_computation | async-start | bytes 8388608 | tf_op jit(solution)/shard_map/all_to_all | solution.py:177
  25.8 0.0 copy-done.1
  25.8 0.1 copy.48
  25.9 0.1 reshape_squeeze.8
  26.0 0.1 reshape_squeeze.9
  26.1 0.1 copy.43
  26.2 0.2 convert_reduce_fusion.1
  26.4 0.1 reduce_sum.51
  26.5 0.6 broadcast_select_fusion
  27.1 1.2 convert_reduce_fusion.2
  28.4 105.5 %all-to-all-done.arrived_ref = bf16[64,4,64,128]{3,2,1,0:T(8,128)(2,1)} async-done(((bf16[64,4,64,128]{3,2,1,0:T(8,128)(2,1)}), bf16[64,4,64,128]{3,2,1,0:T(8,128)(2,1)}, u32[]{:S(2)}, u32[]{:S(2)}) %all-to-all-start) | async-done | bytes 4194336 | tf_op jit(solution)/shard_map/all_to_all | solution.py:177
  133.9 1.5 convert_reduce_fusion
  135.4 0.6 gather_fusion
  136.0 0.1 select_reduce_fusion
  136.1 19.1 %shard_map.111 = bf16[64,4,64,128]{3,2,1,0:T(8,128)(2,1)} custom-call(s32[32,4]{1,0:T(8,128)} %get-tuple-element.20.recv_ref, s32[32]{0:T(128)} %get-tuple-element.19.count_ref, s32[32,4]{1,0:T(8,128)} %get-tuple-element.17.member_ref, bf16[64,4,64,128]{3,2,1,0:T(8,128)(2,1)} %all-to-all-done.arrived_ref), custom_call_target="tpu_custom_call" | custom-call | tf_op jit(solution)/shard_map/pallas_call | solution.py:79
  155.3 0.0 copy-start
  155.3 15.7 %all-to-all-start.1 = ((bf16[64,4,64,128]{3,2,1,0:T(8,128)(2,1)}), bf16[64,4,64,128]{3,2,1,0:T(8,128)(2,1)}, u32[]{:S(2)}, u32[]{:S(2)}) async-start(bf16[64,4,64,128]{3,2,1,0:T(8,128)(2,1)} %shard_map.111), calls=%async_computation.1 | async-start | bytes 8388608 | tf_op jit(solution)/shard_map/all_to_all | solution.py:218
  171.1 1.9 collective-permute-start
  173.1 1.9 collective-permute-start.1
  175.0 1.9 collective-permute-start.2
  176.9 6.0 %collective-permute-start.3 = (f32[32,128]{1,0:T(8,128)S(1)}, f32[32,128]{1,0:T(8,128)S(1)}, u32[]{:S(2)}, u32[]{:S(2)}) collective-permute-start(f32[32,128]{1,0:T(8,128)S(1)} %select_reduce_fusion), channel_id=1, source_target_pairs={{0,256},{64,320},{128,384},{192,448},{256,0},{320,64},{384,128},{4... | collective-permute-start | bytes 49160 | tf_op jit(solution)/shard_map/ppermute | solution.py:208
  182.9 1.9 collective-permute-start.4
  184.9 62.5 %collective-permute-done = f32[32,128]{1,0:T(8,128)S(1)} collective-permute-done((f32[32,128]{1,0:T(8,128)S(1)}, f32[32,128]{1,0:T(8,128)S(1)}, u32[]{:S(2)}, u32[]{:S(2)}) %collective-permute-start) | collective-permute-done | bytes 16416 | tf_op jit(solution)/shard_map/ppermute | solution.py:208
  247.4 1.9 collective-permute-start.5
  249.3 0.1 collective-permute-done.1
  249.5 1.9 collective-permute-start.6
  251.4 0.0 collective-permute-done.2
  251.4 0.0 collective-permute-done.3
  251.4 0.0 collective-permute-done.4
  251.5 13.7 %collective-permute-done.5 = f32[32,128]{1,0:T(8,128)S(1)} collective-permute-done((f32[32,128]{1,0:T(8,128)S(1)}, f32[32,128]{1,0:T(8,128)S(1)}, u32[]{:S(2)}, u32[]{:S(2)}) %collective-permute-start.5) | collective-permute-done | bytes 16416 | tf_op jit(solution)/shard_map/ppermute | solution.py:208
  265.2 0.3 collective-permute-done.6
  265.4 0.0 copy-done
  265.4 0.6 bitcast_add_fusion
  266.1 15.1 %all-to-all-done.1.in_ref = bf16[64,4,64,128]{3,2,1,0:T(8,128)(2,1)} async-done(((bf16[64,4,64,128]{3,2,1,0:T(8,128)(2,1)}), bf16[64,4,64,128]{3,2,1,0:T(8,128)(2,1)}, u32[]{:S(2)}, u32[]{:S(2)}) %all-to-all-start.1) | async-done | bytes 4194336 | tf_op jit(solution)/shard_map/all_to_all | solution.py:218
  281.2 4.1 %shard_map.112 = (bf16[128,2048]{1,0:T(8,128)(2,1)}, bf16[128,2048]{1,0:T(8,128)(2,1)}, bf16[128,2048]{1,0:T(8,128)(2,1)}, bf16[128,2048]{1,0:T(8,128)(2,1)}) custom-call(s32[16,2]{1,0:T(8,128)} %add_add_fusion.dest_ref, bf16[64,4,64,128]{3,2,1,0:T(8,128)(2,1)} %all-to-all-done.1.in_ref), custom_call_target="tpu_custom_call" | custom-call | tf_op jit(solution)/shard_map/pallas_call | solution.py:136
  (15 shorter events, 0.1 us)
Async XLA Ops:
  6.7 19.0 %copy-start.1 = (s32[1,32,4]{1,2,0:T(4,128)S(1)}, s32[1,32,4]{1,2,0:T(4,128)}, u32[]{:S(2)}) copy-start(s32[1,32,4]{1,2,0:T(4,128)} %param.12) | copy-start | bytes 1540
  6.7 127.1 %all-to-all-start = ((bf16[64,4,64,128]{3,2,1,0:T(8,128)(2,1)}), bf16[64,4,64,128]{3,2,1,0:T(8,128)(2,1)}, u32[]{:S(2)}, u32[]{:S(2)}) async-start(bf16[64,4,64,128]{3,2,1,0:T(8,128)(2,1)} %shard_map.110), calls=%async_computation | async-start | bytes 8388608 | tf_op jit(solution)/shard_map/all_to_all | solution.py:177
  155.3 110.2 %copy-start = (f32[32,128]{1,0:T(8,128)S(1)}, f32[32,128]{1,0:T(8,128)}, u32[]{:S(2)}) copy-start(f32[32,128]{1,0:T(8,128)} %param.13) | copy-start | bytes 49156
  155.3 125.9 %all-to-all-start.1 = ((bf16[64,4,64,128]{3,2,1,0:T(8,128)(2,1)}), bf16[64,4,64,128]{3,2,1,0:T(8,128)(2,1)}, u32[]{:S(2)}, u32[]{:S(2)}) async-start(bf16[64,4,64,128]{3,2,1,0:T(8,128)(2,1)} %shard_map.111), calls=%async_computation.1 | async-start | bytes 8388608 | tf_op jit(solution)/shard_map/all_to_all | solution.py:218
  171.1 76.3 %collective-permute-start = (f32[32,128]{1,0:T(8,128)S(1)}, f32[32,128]{1,0:T(8,128)S(1)}, u32[]{:S(2)}, u32[]{:S(2)}) collective-permute-start(f32[32,128]{1,0:T(8,128)S(1)} %select_reduce_fusion), channel_id=1, source_target_pairs={{0,64},{64,128},{128,192},{192,256},{256,320},{320,384},{384,448},... | collective-permute-start | bytes 49160 | tf_op jit(solution)/shard_map/ppermute | solution.py:208
  173.1 76.4 %collective-permute-start.1 = (f32[32,128]{1,0:T(8,128)S(1)}, f32[32,128]{1,0:T(8,128)S(1)}, u32[]{:S(2)}, u32[]{:S(2)}) collective-permute-start(f32[32,128]{1,0:T(8,128)S(1)} %select_reduce_fusion), channel_id=1, source_target_pairs={{0,128},{64,192},{128,256},{192,320},{256,384},{320,448},{384,0},{... | collective-permute-start | bytes 49160 | tf_op jit(solution)/shard_map/ppermute | solution.py:208
  175.0 76.4 %collective-permute-start.2 = (f32[32,128]{1,0:T(8,128)S(1)}, f32[32,128]{1,0:T(8,128)S(1)}, u32[]{:S(2)}, u32[]{:S(2)}) collective-permute-start(f32[32,128]{1,0:T(8,128)S(1)} %select_reduce_fusion), channel_id=1, source_target_pairs={{0,192},{64,256},{128,320},{192,384},{256,448},{320,0},{384,64},{4... | collective-permute-start | bytes 49160 | tf_op jit(solution)/shard_map/ppermute | solution.py:208
  176.9 74.5 %collective-permute-start.3 = (f32[32,128]{1,0:T(8,128)S(1)}, f32[32,128]{1,0:T(8,128)S(1)}, u32[]{:S(2)}, u32[]{:S(2)}) collective-permute-start(f32[32,128]{1,0:T(8,128)S(1)} %select_reduce_fusion), channel_id=1, source_target_pairs={{0,256},{64,320},{128,384},{192,448},{256,0},{320,64},{384,128},{4... | collective-permute-start | bytes 49160 | tf_op jit(solution)/shard_map/ppermute | solution.py:208
  182.9 68.5 %collective-permute-start.4 = (f32[32,128]{1,0:T(8,128)S(1)}, f32[32,128]{1,0:T(8,128)S(1)}, u32[]{:S(2)}, u32[]{:S(2)}) collective-permute-start(f32[32,128]{1,0:T(8,128)S(1)} %select_reduce_fusion), channel_id=1, source_target_pairs={{0,320},{64,384},{128,448},{192,0},{256,64},{320,128},{384,192},{4... | collective-permute-start | bytes 49160 | tf_op jit(solution)/shard_map/ppermute | solution.py:208
  247.4 17.8 %collective-permute-start.5 = (f32[32,128]{1,0:T(8,128)S(1)}, f32[32,128]{1,0:T(8,128)S(1)}, u32[]{:S(2)}, u32[]{:S(2)}) collective-permute-start(f32[32,128]{1,0:T(8,128)S(1)} %select_reduce_fusion), channel_id=1, source_target_pairs={{0,384},{64,448},{128,0},{192,64},{256,128},{320,192},{384,256},{4... | collective-permute-start | bytes 49160 | tf_op jit(solution)/shard_map/ppermute | solution.py:208
  249.5 16.0 %collective-permute-start.6 = (f32[32,128]{1,0:T(8,128)S(1)}, f32[32,128]{1,0:T(8,128)S(1)}, u32[]{:S(2)}, u32[]{:S(2)}) collective-permute-start(f32[32,128]{1,0:T(8,128)S(1)} %select_reduce_fusion), channel_id=1, source_target_pairs={{0,448},{64,0},{128,64},{192,128},{256,192},{320,256},{384,320},{4... | collective-permute-start | bytes 49160 | tf_op jit(solution)/shard_map/ppermute | solution.py:208

commit v8 on v7

--- a/solution.py
+++ b/solution.py
@@ -40,37 +40,55 @@
 def routed_kernel(recv_ref, count_ref, member_ref, arrived_ref, out_ref):
     cluster_count, cluster_cap = member_ref.shape
     block_len = arrived_ref.shape[2]
+    lanes = math.gcd(cluster_count, 2)
+    stride = cluster_count // lanes
     out_ref[...] = jnp.zeros(out_ref.shape, out_ref.dtype)
 
-    def one_cluster(cluster, carry):
-        present_count = count_ref[cluster]
+    def one_step(step, carry):
+        clusters = [step + lane * stride for lane in range(lanes)]
+        counts = [count_ref[cluster] for cluster in clusters]
+        widest = counts[0]
+        for count in counts[1:]:
+            widest = jnp.maximum(widest, count)
         for used in range(1, cluster_cap + 1):
 
-            @pl.when(present_count == used)
+            @pl.when(widest == used)
             def _():
-                rows = [recv_ref[cluster, slot] for slot in range(used)]
-                tiles = [
-                    jnp.concatenate([arrived_ref[row, index] for row in rows], axis=0)
-                    for index in range(4)
-                ]
-                offsets = lax.broadcasted_iota(jnp.int32, (used * block_len, 1), 0)
-                query_pos = offsets % block_len
-                key_offsets = lax.broadcasted_iota(jnp.int32, (1, used * block_len), 1)
-                key_pos = key_offsets % block_len
-                for slot in range(used):
-                    base = member_ref[cluster, slot] * block_len
-                    query_pos = jnp.where(offsets // block_len == slot, query_pos + base, query_pos)
-                    key_pos = jnp.where(key_offsets // block_len == slot, key_pos + base, key_pos)
-                results = attend_block(*tiles, query_pos, key_pos)
-                for slot in range(used):
-                    for index in range(4):
-                        out_ref[rows[slot], index] = results[index][
-                            slot * block_len : (slot + 1) * block_len
-                        ].astype(out_ref.dtype)
+                computed = []
+                for cluster, count in zip(clusters, counts):
+                    rows = [recv_ref[cluster, slot] for slot in range(used)]
+                    tiles = [
+                        jnp.concatenate([arrived_ref[row, index] for row in rows], axis=0)
+                        for index in range(4)
+                    ]
+                    offsets = lax.broadcasted_iota(jnp.int32, (used * block_len, 1), 0)
+                    query_pos = offsets % block_len
+                    key_offsets = lax.broadcasted_iota(jnp.int32, (1, used * block_len), 1)
+                    key_pos = key_offsets % block_len
+                    for slot in range(used):
+                        base = member_ref[cluster, slot] * block_len
+                        query_pos = jnp.where(
+                            offsets // block_len == slot, query_pos + base, query_pos
+                        )
+                        key_pos = jnp.where(
+                            key_offsets // block_len == slot, key_pos + base, key_pos
+                        )
+                    query_pos = jnp.where(offsets // block_len < count, query_pos, -1)
+                    key_pos = jnp.where(key_offsets // block_len < count, key_pos, 1 << 30)
+                    computed.append((rows, count, attend_block(*tiles, query_pos, key_pos)))
+                for rows, count, results in computed:
+                    for slot in range(used):
+
+                        @pl.when(slot < count)
+                        def _():
+                            for index in range(4):
+                                out_ref[rows[slot], index] = results[index][
+                                    slot * block_len : (slot + 1) * block_len
+                                ].astype(out_ref.dtype)
 
         return carry
 
-    lax.fori_loop(0, cluster_count, one_cluster, 0)
+    lax.fori_loop(0, stride, one_step, 0)
 
 
 def routed_attention(recv_table, present_count, member_table, arrived):

time: 286 us -> 287 us (level)
  the two profiles are of different devices: /device:TPU:40 before, /device:TPU:92 now
where the time goes in v8:
time: 287 us; the launch traced here: 286 us
  waiting for transfers between devices  199 us (69%)
  starting transfers between devices  45.7 us (16%)
  Pallas kernels  33.5 us (12%)
  other arithmetic  5.09 us (2%)
    all_to_all x1, waiting for transfers between devices, per_device(): lax.all_to_all(pack_blocks(dest_table, (queries[0], keys[0], values[0], c...  107 us
    ppermute x7, waiting for transfers between devices, per_device(): lax.ppermute(key_sum, 'dp', [(index, (index + shift) % dp_size) for index...  63.8 us
    all_to_all x1, waiting for transfers between devices, per_device(): lax.all_to_all(outgoing, 'seq', split_axis=0, concat_axis=0, tiled=True)  28.2 us
    pallas_call x1, Pallas kernels, routed_attention(): pl.pallas_call(routed_kernel, out_shape=jax.ShapeDtypeStruct(arrived.shap...  25 us
    ppermute x7, starting transfers between devices, per_device(): lax.ppermute(key_sum, 'dp', [(index, (index + shift) % dp_size) for index...  18.8 us
    all_to_all x1, starting transfers between devices, per_device(): lax.all_to_all(pack_blocks(dest_table, (queries[0], keys[0], values[0], c...  15.9 us
    all_to_all x1, starting transfers between devices, per_device(): lax.all_to_all(outgoing, 'seq', split_axis=0, concat_axis=0, tiled=True)  11 us
  transfers between devices with their start and end apart: 9, of which 7 were waited for; matrix products, arithmetic and copies ran while one was open for 1% of the time, Pallas kernels for 0%

profile of v8, /device:TPU:92, one launch (start us, length us, event | category | flops | bytes accessed | tf_op | source)
XLA Modules:
  0.0 286.4 jit_solution(17766802195701464075)
XLA Ops:
  0.7 0.8 copy.36
  1.4 0.1 copy.40
  1.5 0.1 fusion.7
  1.6 0.1 copy.42
  1.7 0.7 add_add_fusion.dest_ref
  2.3 4.4 %shard_map.110 = bf16[64,4,64,128]{3,2,1,0:T(8,128)(2,1)} custom-call(s32[16,2]{1,0:T(8,128)} %add_add_fusion.dest_ref, bf16[128,2048]{1,0:T(8,128)(2,1)} %bitcast.35, bf16[128,2048]{1,0:T(8,128)(2,1)} %bitcast.36, bf16[128,2048]{1,0:T(8,128)(2,1)} %bitcast.37, bf16[128,2048]{1,0:T(8,128)(2,1)} %bitcast.38), custom_call_target="tpu_custom_call" | custom-call | tf_op jit(solution)/shard_map/pallas_call | solution.py:139
  6.7 0.0 copy-start.1
  6.7 15.9 %all-to-all-start = ((bf16[64,4,64,128]{3,2,1,0:T(8,128)(2,1)}), bf16[64,4,64,128]{3,2,1,0:T(8,128)(2,1)}, u32[]{:S(2)}, u32[]{:S(2)}) async-start(bf16[64,4,64,128]{3,2,1,0:T(8,128)(2,1)} %shard_map.110), calls=%async_computation | async-start | bytes 8388608 | tf_op jit(solution)/shard_map/all_to_all | solution.py:195
  22.7 0.0 copy-done.1
  22.7 0.1 copy.48
  22.8 0.1 reshape_squeeze.8
  22.9 0.1 reshape_squeeze.9
  23.0 0.1 copy.43
  23.1 0.2 convert_reduce_fusion.1
  23.3 0.1 reduce_sum.51
  23.4 0.6 broadcast_select_fusion
  24.0 1.2 convert_reduce_fusion.2
  25.3 107.0 %all-to-all-done.arrived_ref = bf16[64,4,64,128]{3,2,1,0:T(8,128)(2,1)} async-done(((bf16[64,4,64,128]{3,2,1,0:T(8,128)(2,1)}), bf16[64,4,64,128]{3,2,1,0:T(8,128)(2,1)}, u32[]{:S(2)}, u32[]{:S(2)}) %all-to-all-start) | async-done | bytes 4194336 | tf_op jit(solution)/shard_map/all_to_all | solution.py:195
  132.3 1.5 convert_reduce_fusion
  133.8 0.6 gather_fusion
  134.4 0.1 select_reduce_fusion
  134.5 25.0 %shard_map.111 = bf16[64,4,64,128]{3,2,1,0:T(8,128)(2,1)} custom-call(s32[32,4]{1,0:T(8,128)} %get-tuple-element.20.recv_ref, s32[32]{0:T(128)} %get-tuple-element.19.count_ref, s32[32,4]{1,0:T(8,128)} %get-tuple-element.17.member_ref, bf16[64,4,64,128]{3,2,1,0:T(8,128)(2,1)} %all-to-all-done.arrived_ref), custom_call_target="tpu_custom_call" | custom-call | tf_op jit(solution)/shard_map/pallas_call | solution.py:97
  159.6 0.0 copy-start
  159.6 11.0 %all-to-all-start.1 = ((bf16[64,4,64,128]{3,2,1,0:T(8,128)(2,1)}), bf16[64,4,64,128]{3,2,1,0:T(8,128)(2,1)}, u32[]{:S(2)}, u32[]{:S(2)}) async-start(bf16[64,4,64,128]{3,2,1,0:T(8,128)(2,1)} %shard_map.111), calls=%async_computation.1 | async-start | bytes 8388608 | tf_op jit(solution)/shard_map/all_to_all | solution.py:236
  170.7 1.9 collective-permute-start
  172.6 1.9 collective-permute-start.1
  174.5 4.9 %collective-permute-start.2 = (f32[32,128]{1,0:T(8,128)S(1)}, f32[32,128]{1,0:T(8,128)S(1)}, u32[]{:S(2)}, u32[]{:S(2)}) collective-permute-start(f32[32,128]{1,0:T(8,128)S(1)} %select_reduce_fusion), channel_id=1, source_target_pairs={{0,192},{64,256},{128,320},{192,384},{256,448},{320,0},{384,64},{4... | collective-permute-start | bytes 49160 | tf_op jit(solution)/shard_map/ppermute | solution.py:226
  179.5 2.1 collective-permute-start.3
  181.6 4.1 %collective-permute-start.4 = (f32[32,128]{1,0:T(8,128)S(1)}, f32[32,128]{1,0:T(8,128)S(1)}, u32[]{:S(2)}, u32[]{:S(2)}) collective-permute-start(f32[32,128]{1,0:T(8,128)S(1)} %select_reduce_fusion), channel_id=1, source_target_pairs={{0,320},{64,384},{128,448},{192,0},{256,64},{320,128},{384,192},{4... | collective-permute-start | bytes 49160 | tf_op jit(solution)/shard_map/ppermute | solution.py:226
  185.7 40.0 %collective-permute-done = f32[32,128]{1,0:T(8,128)S(1)} collective-permute-done((f32[32,128]{1,0:T(8,128)S(1)}, f32[32,128]{1,0:T(8,128)S(1)}, u32[]{:S(2)}, u32[]{:S(2)}) %collective-permute-start) | collective-permute-done | bytes 16416 | tf_op jit(solution)/shard_map/ppermute | solution.py:226
  225.7 1.9 collective-permute-start.5
  227.6 2.1 collective-permute-done.1
  229.7 1.9 collective-permute-start.6
  231.7 0.0 collective-permute-done.2
  231.7 17.3 %collective-permute-done.3 = f32[32,128]{1,0:T(8,128)S(1)} collective-permute-done((f32[32,128]{1,0:T(8,128)S(1)}, f32[32,128]{1,0:T(8,128)S(1)}, u32[]{:S(2)}, u32[]{:S(2)}) %collective-permute-start.3) | collective-permute-done | bytes 16416 | tf_op jit(solution)/shard_map/ppermute | solution.py:226
  249.0 1.4 collective-permute-done.4
  250.3 3.1 %collective-permute-done.5 = f32[32,128]{1,0:T(8,128)S(1)} collective-permute-done((f32[32,128]{1,0:T(8,128)S(1)}, f32[32,128]{1,0:T(8,128)S(1)}, u32[]{:S(2)}, u32[]{:S(2)}) %collective-permute-start.5) | collective-permute-done | bytes 16416 | tf_op jit(solution)/shard_map/ppermute | solution.py:226
  253.4 0.0 collective-permute-done.6
  253.4 0.0 copy-done
  253.4 0.6 bitcast_add_fusion
  254.1 28.2 %all-to-all-done.1.in_ref = bf16[64,4,64,128]{3,2,1,0:T(8,128)(2,1)} async-done(((bf16[64,4,64,128]{3,2,1,0:T(8,128)(2,1)}), bf16[64,4,64,128]{3,2,1,0:T(8,128)(2,1)}, u32[]{:S(2)}, u32[]{:S(2)}) %all-to-all-start.1) | async-done | bytes 4194336 | tf_op jit(solution)/shard_map/all_to_all | solution.py:236
  282.3 4.1 %shard_map.112 = (bf16[128,2048]{1,0:T(8,128)(2,1)}, bf16[128,2048]{1,0:T(8,128)(2,1)}, bf16[128,2048]{1,0:T(8,128)(2,1)}, bf16[128,2048]{1,0:T(8,128)(2,1)}) custom-call(s32[16,2]{1,0:T(8,128)} %add_add_fusion.dest_ref, bf16[64,4,64,128]{3,2,1,0:T(8,128)(2,1)} %all-to-all-done.1.in_ref), custom_call_target="tpu_custom_call" | custom-call | tf_op jit(solution)/shard_map/pallas_call | solution.py:154
  (15 shorter events, 0.1 us)
Async XLA Ops:
  6.7 15.9 %copy-start.1 = (s32[1,32,4]{1,2,0:T(4,128)S(1)}, s32[1,32,4]{1,2,0:T(4,128)}, u32[]{:S(2)}) copy-start(s32[1,32,4]{1,2,0:T(4,128)} %param.12) | copy-start | bytes 1540
  6.7 125.5 %all-to-all-start = ((bf16[64,4,64,128]{3,2,1,0:T(8,128)(2,1)}), bf16[64,4,64,128]{3,2,1,0:T(8,128)(2,1)}, u32[]{:S(2)}, u32[]{:S(2)}) async-start(bf16[64,4,64,128]{3,2,1,0:T(8,128)(2,1)} %shard_map.110), calls=%async_computation | async-start | bytes 8388608 | tf_op jit(solution)/shard_map/all_to_all | solution.py:195
  159.6 93.9 %copy-start = (f32[32,128]{1,0:T(8,128)S(1)}, f32[32,128]{1,0:T(8,128)}, u32[]{:S(2)}) copy-start(f32[32,128]{1,0:T(8,128)} %param.13) | copy-start | bytes 49156
  159.6 122.7 %all-to-all-start.1 = ((bf16[64,4,64,128]{3,2,1,0:T(8,128)(2,1)}), bf16[64,4,64,128]{3,2,1,0:T(8,128)(2,1)}, u32[]{:S(2)}, u32[]{:S(2)}) async-start(bf16[64,4,64,128]{3,2,1,0:T(8,128)(2,1)} %shard_map.111), calls=%async_computation.1 | async-start | bytes 8388608 | tf_op jit(solution)/shard_map/all_to_all | solution.py:236
  170.7 55.0 %collective-permute-start = (f32[32,128]{1,0:T(8,128)S(1)}, f32[32,128]{1,0:T(8,128)S(1)}, u32[]{:S(2)}, u32[]{:S(2)}) collective-permute-start(f32[32,128]{1,0:T(8,128)S(1)} %select_reduce_fusion), channel_id=1, source_target_pairs={{0,64},{64,128},{128,192},{192,256},{256,320},{320,384},{384,448},... | collective-permute-start | bytes 49160 | tf_op jit(solution)/shard_map/ppermute | solution.py:226
  172.6 57.1 %collective-permute-start.1 = (f32[32,128]{1,0:T(8,128)S(1)}, f32[32,128]{1,0:T(8,128)S(1)}, u32[]{:S(2)}, u32[]{:S(2)}) collective-permute-start(f32[32,128]{1,0:T(8,128)S(1)} %select_reduce_fusion), channel_id=1, source_target_pairs={{0,128},{64,192},{128,256},{192,320},{256,384},{320,448},{384,0},{... | collective-permute-start | bytes 49160 | tf_op jit(solution)/shard_map/ppermute | solution.py:226
  174.5 57.1 %collective-permute-start.2 = (f32[32,128]{1,0:T(8,128)S(1)}, f32[32,128]{1,0:T(8,128)S(1)}, u32[]{:S(2)}, u32[]{:S(2)}) collective-permute-start(f32[32,128]{1,0:T(8,128)S(1)} %select_reduce_fusion), channel_id=1, source_target_pairs={{0,192},{64,256},{128,320},{192,384},{256,448},{320,0},{384,64},{4... | collective-permute-start | bytes 49160 | tf_op jit(solution)/shard_map/ppermute | solution.py:226
  179.5 69.5 %collective-permute-start.3 = (f32[32,128]{1,0:T(8,128)S(1)}, f32[32,128]{1,0:T(8,128)S(1)}, u32[]{:S(2)}, u32[]{:S(2)}) collective-permute-start(f32[32,128]{1,0:T(8,128)S(1)} %select_reduce_fusion), channel_id=1, source_target_pairs={{0,256},{64,320},{128,384},{192,448},{256,0},{320,64},{384,128},{4... | collective-permute-start | bytes 49160 | tf_op jit(solution)/shard_map/ppermute | solution.py:226
  181.6 68.8 %collective-permute-start.4 = (f32[32,128]{1,0:T(8,128)S(1)}, f32[32,128]{1,0:T(8,128)S(1)}, u32[]{:S(2)}, u32[]{:S(2)}) collective-permute-start(f32[32,128]{1,0:T(8,128)S(1)} %select_reduce_fusion), channel_id=1, source_target_pairs={{0,320},{64,384},{128,448},{192,0},{256,64},{320,128},{384,192},{4... | collective-permute-start | bytes 49160 | tf_op jit(solution)/shard_map/ppermute | solution.py:226
  225.7 27.7 %collective-permute-start.5 = (f32[32,128]{1,0:T(8,128)S(1)}, f32[32,128]{1,0:T(8,128)S(1)}, u32[]{:S(2)}, u32[]{:S(2)}) collective-permute-start(f32[32,128]{1,0:T(8,128)S(1)} %select_reduce_fusion), channel_id=1, source_target_pairs={{0,384},{64,448},{128,0},{192,64},{256,128},{320,192},{384,256},{4... | collective-permute-start | bytes 49160 | tf_op jit(solution)/shard_map/ppermute | solution.py:226
  229.7 23.7 %collective-permute-start.6 = (f32[32,128]{1,0:T(8,128)S(1)}, f32[32,128]{1,0:T(8,128)S(1)}, u32[]{:S(2)}, u32[]{:S(2)}) collective-permute-start(f32[32,128]{1,0:T(8,128)S(1)} %select_reduce_fusion), channel_id=1, source_target_pairs={{0,448},{64,0},{128,64},{192,128},{256,192},{320,256},{384,320},{4... | collective-permute-start | bytes 49160 | tf_op jit(solution)/shard_map/ppermute | solution.py:226

commit v9 on v7

--- a/solution.py
+++ b/solution.py
@@ -40,7 +40,6 @@
 def routed_kernel(recv_ref, count_ref, member_ref, arrived_ref, out_ref):
     cluster_count, cluster_cap = member_ref.shape
     block_len = arrived_ref.shape[2]
-    out_ref[...] = jnp.zeros(out_ref.shape, out_ref.dtype)
 
     def one_cluster(cluster, carry):
         present_count = count_ref[cluster]
@@ -89,7 +88,6 @@
     head_count, block_count = dest_ref.shape
     block_len = out_ref.shape[2]
     head_dim = out_ref.shape[3]
-    out_ref[...] = jnp.zeros(out_ref.shape, out_ref.dtype)
     for head in range(head_count):
         for block in range(block_count):
             slot = dest_ref[head, block]

time: 286 us -> 284 us (level)
  the two profiles are of different devices: /device:TPU:40 before, /device:TPU:26 now
where the time goes in v9:
time: 284 us; the launch traced here: 283 us
  waiting for transfers between devices  200 us (70%)
  starting transfers between devices  47.7 us (17%)
  Pallas kernels  27.7 us (10%)
  other arithmetic  5.09 us (2%)
    all_to_all x1, waiting for transfers between devices, per_device(): lax.all_to_all(pack_blocks(dest_table, (queries[0], keys[0], values[0], c...  108 us
    ppermute x7, waiting for transfers between devices, per_device(): lax.ppermute(key_sum, 'dp', [(index, (index + shift) % dp_size) for index...  87.2 us
    pallas_call x1, Pallas kernels, routed_attention(): pl.pallas_call(routed_kernel, out_shape=jax.ShapeDtypeStruct(arrived.shap...  19.8 us
    ppermute x7, starting transfers between devices, per_device(): lax.ppermute(key_sum, 'dp', [(index, (index + shift) % dp_size) for index...  17.3 us
    all_to_all x1, starting transfers between devices, per_device(): lax.all_to_all(pack_blocks(dest_table, (queries[0], keys[0], values[0], c...  16.8 us
    all_to_all x1, starting transfers between devices, per_device(): lax.all_to_all(outgoing, 'seq', split_axis=0, concat_axis=0, tiled=True)  13.6 us
  transfers between devices with their start and end apart: 9, of which 4 were waited for; matrix products, arithmetic and copies ran while one was open for 1% of the time, Pallas kernels for 0%

profile of v9, /device:TPU:26, one launch (start us, length us, event | category | flops | bytes accessed | tf_op | source)
XLA Modules:
  0.0 283.5 jit_solution(11327792990984929654)
XLA Ops:
  0.7 0.8 copy.36
  1.4 0.1 copy.40
  1.5 0.1 fusion.7
  1.6 0.1 copy.42
  1.7 0.7 add_add_fusion.dest_ref
  2.3 3.9 %shard_map.110 = bf16[64,4,64,128]{3,2,1,0:T(8,128)(2,1)} custom-call(s32[16,2]{1,0:T(8,128)} %add_add_fusion.dest_ref, bf16[128,2048]{1,0:T(8,128)(2,1)} %bitcast.35, bf16[128,2048]{1,0:T(8,128)(2,1)} %bitcast.36, bf16[128,2048]{1,0:T(8,128)(2,1)} %bitcast.37, bf16[128,2048]{1,0:T(8,128)(2,1)} %bitcast.38), custom_call_target="tpu_custom_call" | custom-call | tf_op jit(solution)/shard_map/pallas_call | solution.py:119
  6.2 0.0 copy-start.1
  6.2 16.8 %all-to-all-start = ((bf16[64,4,64,128]{3,2,1,0:T(8,128)(2,1)}), bf16[64,4,64,128]{3,2,1,0:T(8,128)(2,1)}, u32[]{:S(2)}, u32[]{:S(2)}) async-start(bf16[64,4,64,128]{3,2,1,0:T(8,128)(2,1)} %shard_map.110), calls=%async_computation | async-start | bytes 8388608 | tf_op jit(solution)/shard_map/all_to_all | solution.py:175
  23.0 0.0 copy-done.1
  23.0 0.1 copy.48
  23.1 0.1 reshape_squeeze.8
  23.2 0.1 reshape_squeeze.9
  23.3 0.1 copy.43
  23.4 0.2 convert_reduce_fusion.1
  23.6 0.1 reduce_sum.51
  23.7 0.6 broadcast_select_fusion
  24.3 1.2 convert_reduce_fusion.2
  25.6 107.7 %all-to-all-done.arrived_ref = bf16[64,4,64,128]{3,2,1,0:T(8,128)(2,1)} async-done(((bf16[64,4,64,128]{3,2,1,0:T(8,128)(2,1)}), bf16[64,4,64,128]{3,2,1,0:T(8,128)(2,1)}, u32[]{:S(2)}, u32[]{:S(2)}) %all-to-all-start) | async-done | bytes 4194336 | tf_op jit(solution)/shard_map/all_to_all | solution.py:175
  133.3 1.5 convert_reduce_fusion
  134.8 0.6 gather_fusion
  135.4 0.1 select_reduce_fusion
  135.6 19.8 %shard_map.111 = bf16[64,4,64,128]{3,2,1,0:T(8,128)(2,1)} custom-call(s32[32,4]{1,0:T(8,128)} %get-tuple-element.20.recv_ref, s32[32]{0:T(128)} %get-tuple-element.19.count_ref, s32[32,4]{1,0:T(8,128)} %get-tuple-element.17.member_ref, bf16[64,4,64,128]{3,2,1,0:T(8,128)(2,1)} %all-to-all-done.arrived_ref), custom_call_target="tpu_custom_call" | custom-call | tf_op jit(solution)/shard_map/pallas_call | solution.py:78
  155.3 0.0 copy-start
  155.4 13.6 %all-to-all-start.1 = ((bf16[64,4,64,128]{3,2,1,0:T(8,128)(2,1)}), bf16[64,4,64,128]{3,2,1,0:T(8,128)(2,1)}, u32[]{:S(2)}, u32[]{:S(2)}) async-start(bf16[64,4,64,128]{3,2,1,0:T(8,128)(2,1)} %shard_map.111), calls=%async_computation.1 | async-start | bytes 8388608 | tf_op jit(solution)/shard_map/all_to_all | solution.py:216
  169.1 1.9 collective-permute-start
  171.1 1.9 collective-permute-start.1
  173.0 3.5 %collective-permute-start.2 = (f32[32,128]{1,0:T(8,128)S(1)}, f32[32,128]{1,0:T(8,128)S(1)}, u32[]{:S(2)}, u32[]{:S(2)}) collective-permute-start(f32[32,128]{1,0:T(8,128)S(1)} %select_reduce_fusion), channel_id=1, source_target_pairs={{0,192},{64,256},{128,320},{192,384},{256,448},{320,0},{384,64},{4... | collective-permute-start | bytes 49160 | tf_op jit(solution)/shard_map/ppermute | solution.py:206
  176.4 3.6 %collective-permute-start.3 = (f32[32,128]{1,0:T(8,128)S(1)}, f32[32,128]{1,0:T(8,128)S(1)}, u32[]{:S(2)}, u32[]{:S(2)}) collective-permute-start(f32[32,128]{1,0:T(8,128)S(1)} %select_reduce_fusion), channel_id=1, source_target_pairs={{0,256},{64,320},{128,384},{192,448},{256,0},{320,64},{384,128},{4... | collective-permute-start | bytes 49160 | tf_op jit(solution)/shard_map/ppermute | solution.py:206
  180.0 2.6 collective-permute-start.4
  182.6 83.7 %collective-permute-done = f32[32,128]{1,0:T(8,128)S(1)} collective-permute-done((f32[32,128]{1,0:T(8,128)S(1)}, f32[32,128]{1,0:T(8,128)S(1)}, u32[]{:S(2)}, u32[]{:S(2)}) %collective-permute-start) | collective-permute-done | bytes 16416 | tf_op jit(solution)/shard_map/ppermute | solution.py:206
  266.3 1.9 collective-permute-start.5
  268.3 0.0 collective-permute-done.1
  268.3 1.9 collective-permute-start.6
  270.2 0.0 collective-permute-done.2
  270.2 0.0 collective-permute-done.3
  270.2 0.0 collective-permute-done.4
  270.3 3.5 %collective-permute-done.5 = f32[32,128]{1,0:T(8,128)S(1)} collective-permute-done((f32[32,128]{1,0:T(8,128)S(1)}, f32[32,128]{1,0:T(8,128)S(1)}, u32[]{:S(2)}, u32[]{:S(2)}) %collective-permute-start.5) | collective-permute-done | bytes 16416 | tf_op jit(solution)/shard_map/ppermute | solution.py:206
  273.7 0.0 collective-permute-done.6
  273.8 0.0 copy-done
  273.8 0.6 bitcast_add_fusion
  274.4 5.0 %all-to-all-done.1.in_ref = bf16[64,4,64,128]{3,2,1,0:T(8,128)(2,1)} async-done(((bf16[64,4,64,128]{3,2,1,0:T(8,128)(2,1)}), bf16[64,4,64,128]{3,2,1,0:T(8,128)(2,1)}, u32[]{:S(2)}, u32[]{:S(2)}) %all-to-all-start.1) | async-done | bytes 4194336 | tf_op jit(solution)/shard_map/all_to_all | solution.py:216
  279.4 4.1 %shard_map.112 = (bf16[128,2048]{1,0:T(8,128)(2,1)}, bf16[128,2048]{1,0:T(8,128)(2,1)}, bf16[128,2048]{1,0:T(8,128)(2,1)}, bf16[128,2048]{1,0:T(8,128)(2,1)}) custom-call(s32[16,2]{1,0:T(8,128)} %add_add_fusion.dest_ref, bf16[64,4,64,128]{3,2,1,0:T(8,128)(2,1)} %all-to-all-done.1.in_ref), custom_call_target="tpu_custom_call" | custom-call | tf_op jit(solution)/shard_map/pallas_call | solution.py:134
  (15 shorter events, 0.1 us)
Async XLA Ops:
  6.2 16.8 %copy-start.1 = (s32[1,32,4]{1,2,0:T(4,128)S(1)}, s32[1,32,4]{1,2,0:T(4,128)}, u32[]{:S(2)}) copy-start(s32[1,32,4]{1,2,0:T(4,128)} %param.12) | copy-start | bytes 1540
  6.2 127.1 %all-to-all-start = ((bf16[64,4,64,128]{3,2,1,0:T(8,128)(2,1)}), bf16[64,4,64,128]{3,2,1,0:T(8,128)(2,1)}, u32[]{:S(2)}, u32[]{:S(2)}) async-start(bf16[64,4,64,128]{3,2,1,0:T(8,128)(2,1)} %shard_map.110), calls=%async_computation | async-start | bytes 8388608 | tf_op jit(solution)/shard_map/all_to_all | solution.py:175
  155.3 118.4 %copy-start = (f32[32,128]{1,0:T(8,128)S(1)}, f32[32,128]{1,0:T(8,128)}, u32[]{:S(2)}) copy-start(f32[32,128]{1,0:T(8,128)} %param.13) | copy-start | bytes 49156
  155.4 124.0 %all-to-all-start.1 = ((bf16[64,4,64,128]{3,2,1,0:T(8,128)(2,1)}), bf16[64,4,64,128]{3,2,1,0:T(8,128)(2,1)}, u32[]{:S(2)}, u32[]{:S(2)}) async-start(bf16[64,4,64,128]{3,2,1,0:T(8,128)(2,1)} %shard_map.111), calls=%async_computation.1 | async-start | bytes 8388608 | tf_op jit(solution)/shard_map/all_to_all | solution.py:216
  169.1 97.2 %collective-permute-start = (f32[32,128]{1,0:T(8,128)S(1)}, f32[32,128]{1,0:T(8,128)S(1)}, u32[]{:S(2)}, u32[]{:S(2)}) collective-permute-start(f32[32,128]{1,0:T(8,128)S(1)} %select_reduce_fusion), channel_id=1, source_target_pairs={{0,64},{64,128},{128,192},{192,256},{256,320},{320,384},{384,448},... | collective-permute-start | bytes 49160 | tf_op jit(solution)/shard_map/ppermute | solution.py:206
  171.1 97.2 %collective-permute-start.1 = (f32[32,128]{1,0:T(8,128)S(1)}, f32[32,128]{1,0:T(8,128)S(1)}, u32[]{:S(2)}, u32[]{:S(2)}) collective-permute-start(f32[32,128]{1,0:T(8,128)S(1)} %select_reduce_fusion), channel_id=1, source_target_pairs={{0,128},{64,192},{128,256},{192,320},{256,384},{320,448},{384,0},{... | collective-permute-start | bytes 49160 | tf_op jit(solution)/shard_map/ppermute | solution.py:206
  173.0 97.2 %collective-permute-start.2 = (f32[32,128]{1,0:T(8,128)S(1)}, f32[32,128]{1,0:T(8,128)S(1)}, u32[]{:S(2)}, u32[]{:S(2)}) collective-permute-start(f32[32,128]{1,0:T(8,128)S(1)} %select_reduce_fusion), channel_id=1, source_target_pairs={{0,192},{64,256},{128,320},{192,384},{256,448},{320,0},{384,64},{4... | collective-permute-start | bytes 49160 | tf_op jit(solution)/shard_map/ppermute | solution.py:206
  176.4 93.8 %collective-permute-start.3 = (f32[32,128]{1,0:T(8,128)S(1)}, f32[32,128]{1,0:T(8,128)S(1)}, u32[]{:S(2)}, u32[]{:S(2)}) collective-permute-start(f32[32,128]{1,0:T(8,128)S(1)} %select_reduce_fusion), channel_id=1, source_target_pairs={{0,256},{64,320},{128,384},{192,448},{256,0},{320,64},{384,128},{4... | collective-permute-start | bytes 49160 | tf_op jit(solution)/shard_map/ppermute | solution.py:206
  180.0 90.2 %collective-permute-start.4 = (f32[32,128]{1,0:T(8,128)S(1)}, f32[32,128]{1,0:T(8,128)S(1)}, u32[]{:S(2)}, u32[]{:S(2)}) collective-permute-start(f32[32,128]{1,0:T(8,128)S(1)} %select_reduce_fusion), channel_id=1, source_target_pairs={{0,320},{64,384},{128,448},{192,0},{256,64},{320,128},{384,192},{4... | collective-permute-start | bytes 49160 | tf_op jit(solution)/shard_map/ppermute | solution.py:206
  266.3 7.4 %collective-permute-start.5 = (f32[32,128]{1,0:T(8,128)S(1)}, f32[32,128]{1,0:T(8,128)S(1)}, u32[]{:S(2)}, u32[]{:S(2)}) collective-permute-start(f32[32,128]{1,0:T(8,128)S(1)} %select_reduce_fusion), channel_id=1, source_target_pairs={{0,384},{64,448},{128,0},{192,64},{256,128},{320,192},{384,256},{4... | collective-permute-start | bytes 49160 | tf_op jit(solution)/shard_map/ppermute | solution.py:206
  268.3 5.5 %collective-permute-start.6 = (f32[32,128]{1,0:T(8,128)S(1)}, f32[32,128]{1,0:T(8,128)S(1)}, u32[]{:S(2)}, u32[]{:S(2)}) collective-permute-start(f32[32,128]{1,0:T(8,128)S(1)} %select_reduce_fusion), channel_id=1, source_target_pairs={{0,448},{64,0},{128,64},{192,128},{256,192},{320,256},{384,320},{4... | collective-permute-start | bytes 49160 | tf_op jit(solution)/shard_map/ppermute | solution.py:206

commit v10 on v9

--- a/solution.py
+++ b/solution.py
@@ -84,51 +84,69 @@
 
 
 def pack_kernel(dest_ref, *refs):
-    in_refs, out_ref = refs[:-1], refs[-1]
+    in_refs, out_ref, sems = refs[:-2], refs[-2], refs[-1]
     head_count, block_count = dest_ref.shape
     block_len = out_ref.shape[2]
     head_dim = out_ref.shape[3]
+    copies = []
     for head in range(head_count):
         for block in range(block_count):
             slot = dest_ref[head, block]
             for index, in_ref in enumerate(in_refs):
-                out_ref[slot, index] = in_ref[
-                    block * block_len : (block + 1) * block_len,
-                    head * head_dim : (head + 1) * head_dim,
-                ]
-
-
-def unpack_kernel(dest_ref, in_ref, *out_refs):
+                copy = pltpu.make_async_copy(
+                    in_ref.at[
+                        pl.ds(block * block_len, block_len), pl.ds(head * head_dim, head_dim)
+                    ],
+                    out_ref.at[slot, index],
+                    sems.at[len(copies)],
+                )
+                copy.start()
+                copies.append(copy)
+    for copy in copies:
+        copy.wait()
+
+
+def unpack_kernel(dest_ref, in_ref, *refs):
+    out_refs, sems = refs[:-1], refs[-1]
     head_count, block_count = dest_ref.shape
     block_len = in_ref.shape[2]
     head_dim = in_ref.shape[3]
+    copies = []
     for head in range(head_count):
         for block in range(block_count):
             slot = dest_ref[head, block]
             for index, out_ref in enumerate(out_refs):
-                out_ref[
-                    block * block_len : (block + 1) * block_len,
-                    head * head_dim : (head + 1) * head_dim,
-                ] = in_ref[slot, index]
+                copy = pltpu.make_async_copy(
+                    in_ref.at[slot, index],
+                    out_ref.at[
+                        pl.ds(block * block_len, block_len), pl.ds(head * head_dim, head_dim)
+                    ],
+                    sems.at[len(copies)],
+                )
+                copy.start()
+                copies.append(copy)
+    for copy in copies:
+        copy.wait()
 
 
 def pack_blocks(dest_table, sources, slot_count, block_len):
     smem = pl.BlockSpec(memory_space=pltpu.SMEM)
-    vmem = pl.BlockSpec(memory_space=pltpu.VMEM)
+    anywhere = pl.BlockSpec(memory_space=pl.ANY)
     head_dim = sources[0].shape[1] // dest_table.shape[0]
     return pl.pallas_call(
         pack_kernel,
         out_shape=jax.ShapeDtypeStruct(
             (slot_count, len(sources), block_len, head_dim), sources[0].dtype
         ),
-        in_specs=[smem] + [vmem] * len(sources),
-        out_specs=vmem,
+        in_specs=[smem] + [anywhere] * len(sources),
+        out_specs=anywhere,
+        scratch_shapes=[pltpu.SemaphoreType.DMA((dest_table.size * len(sources),))],
     )(dest_table, *sources)
 
 
 def unpack_blocks(dest_table, returned, token_count):
     smem = pl.BlockSpec(memory_space=pltpu.SMEM)
-    vmem = pl.BlockSpec(memory_space=pltpu.VMEM)
+    anywhere = pl.BlockSpec(memory_space=pl.ANY)
     width = dest_table.shape[0] * returned.shape[3]
     count = returned.shape[1]
     return pl.pallas_call(
@@ -136,8 +154,9 @@
         out_shape=tuple(
             jax.ShapeDtypeStruct((token_count, width), returned.dtype) for _ in range(count)
         ),
-        in_specs=[smem, vmem],
-        out_specs=tuple(vmem for _ in range(count)),
+        in_specs=[smem, anywhere],
+        out_specs=tuple(anywhere for _ in range(count)),
+        scratch_shapes=[pltpu.SemaphoreType.DMA((dest_table.size * count,))],
     )(dest_table, returned)
 
 

time: 284 us -> 408 us (1.44)
  the two profiles are of different devices: /device:TPU:26 before, /device:TPU:46 now
where the time goes in v10:
time: 408 us; the launch traced here: 407 us
  waiting for transfers between devices  189 us (46%)
  Pallas kernels  152 us (37%)
  starting transfers between devices  57.7 us (14%)
  other arithmetic  5.08 us (1%)
    all_to_all x1, waiting for transfers between devices, per_device(): lax.all_to_all(pack_blocks(dest_table, (queries[0], keys[0], values[0], c...  104 us
    ppermute x7, waiting for transfers between devices, per_device(): lax.ppermute(key_sum, 'dp', [(index, (index + shift) % dp_size) for index...  70.9 us
    pallas_call x1, Pallas kernels, unpack_blocks(): pl.pallas_call(unpack_kernel, out_shape=tuple((jax.ShapeDtypeStruct((toke...  66.6 us
    pallas_call x1, Pallas kernels, pack_blocks(): pl.pallas_call(pack_kernel, out_shape=jax.ShapeDtypeStruct((slot_count, l...  66.6 us
    ppermute x7, starting transfers between devices, per_device(): lax.ppermute(key_sum, 'dp', [(index, (index + shift) % dp_size) for index...  23 us
    pallas_call x1, Pallas kernels, routed_attention(): pl.pallas_call(routed_kernel, out_shape=jax.ShapeDtypeStruct(arrived.shap...  19.1 us
    all_to_all x1, starting transfers between devices, per_device(): lax.all_to_all(pack_blocks(dest_table, (queries[0], keys[0], values[0], c...  19 us
    all_to_all x1, starting transfers between devices, per_device(): lax.all_to_all(outgoing, 'seq', split_axis=0, concat_axis=0, tiled=True)  15.6 us
  transfers between devices with their start and end apart: 9, of which 7 were waited for; matrix products, arithmetic and copies ran while one was open for 1% of the time, Pallas kernels for 0%

profile of v10, /device:TPU:46, one launch (start us, length us, event | category | flops | bytes accessed | tf_op | source)
XLA Modules:
  0.0 407.2 jit_solution(14708629635676548000)
XLA Ops:
  0.7 0.8 copy.36
  1.4 0.1 copy.40
  1.5 0.1 fusion.7
  1.6 0.1 copy.42
  1.7 0.7 add_add_fusion.dest_ref
  2.3 66.6 %shard_map.110 = bf16[64,4,64,128]{3,2,1,0:T(8,128)(2,1)} custom-call(s32[16,2]{1,0:T(8,128)} %add_add_fusion.dest_ref, bf16[128,2048]{1,0:T(8,128)(2,1)} %bitcast.35, bf16[128,2048]{1,0:T(8,128)(2,1)} %bitcast.36, bf16[128,2048]{1,0:T(8,128)(2,1)} %bitcast.37, bf16[128,2048]{1,0:T(8,128)(2,1)} %bitcast.38), custom_call_target="tpu_custom_call" | custom-call | tf_op jit(solution)/shard_map/pallas_call | solution.py:136
  68.9 0.0 copy-start.1
  68.9 19.0 %all-to-all-start = ((bf16[64,4,64,128]{3,2,1,0:T(8,128)(2,1)}), bf16[64,4,64,128]{3,2,1,0:T(8,128)(2,1)}, u32[]{:S(2)}, u32[]{:S(2)}) async-start(bf16[64,4,64,128]{3,2,1,0:T(8,128)(2,1)} %shard_map.110), calls=%async_computation | async-start | bytes 8388608 | tf_op jit(solution)/shard_map/all_to_all | solution.py:194
  88.0 0.0 copy-done.1
  88.0 0.1 copy.48
  88.1 0.1 reshape_squeeze.8
  88.2 0.1 reshape_squeeze.9
  88.3 0.1 copy.43
  88.4 0.2 convert_reduce_fusion.1
  88.6 0.1 reduce_sum.51
  88.7 0.6 broadcast_select_fusion
  89.3 1.2 convert_reduce_fusion.2
  90.6 103.9 %all-to-all-done.arrived_ref = bf16[64,4,64,128]{3,2,1,0:T(8,128)(2,1)} async-done(((bf16[64,4,64,128]{3,2,1,0:T(8,128)(2,1)}), bf16[64,4,64,128]{3,2,1,0:T(8,128)(2,1)}, u32[]{:S(2)}, u32[]{:S(2)}) %all-to-all-start) | async-done | bytes 4194336 | tf_op jit(solution)/shard_map/all_to_all | solution.py:194
  194.5 1.5 convert_reduce_fusion
  196.0 0.6 gather_fusion
  196.6 0.1 select_reduce_fusion
  196.7 19.1 %shard_map.111 = bf16[64,4,64,128]{3,2,1,0:T(8,128)(2,1)} custom-call(s32[32,4]{1,0:T(8,128)} %get-tuple-element.20.recv_ref, s32[32]{0:T(128)} %get-tuple-element.19.count_ref, s32[32,4]{1,0:T(8,128)} %get-tuple-element.17.member_ref, bf16[64,4,64,128]{3,2,1,0:T(8,128)(2,1)} %all-to-all-done.arrived_ref), custom_call_target="tpu_custom_call" | custom-call | tf_op jit(solution)/shard_map/pallas_call | solution.py:78
  215.8 0.0 copy-start
  215.8 15.6 %all-to-all-start.1 = ((bf16[64,4,64,128]{3,2,1,0:T(8,128)(2,1)}), bf16[64,4,64,128]{3,2,1,0:T(8,128)(2,1)}, u32[]{:S(2)}, u32[]{:S(2)}) async-start(bf16[64,4,64,128]{3,2,1,0:T(8,128)(2,1)} %shard_map.111), calls=%async_computation.1 | async-start | bytes 8388608 | tf_op jit(solution)/shard_map/all_to_all | solution.py:235
  231.6 1.9 collective-permute-start
  233.5 1.9 collective-permute-start.1
  235.4 1.9 collective-permute-start.2
  237.4 6.0 %collective-permute-start.3 = (f32[32,128]{1,0:T(8,128)S(1)}, f32[32,128]{1,0:T(8,128)S(1)}, u32[]{:S(2)}, u32[]{:S(2)}) collective-permute-start(f32[32,128]{1,0:T(8,128)S(1)} %select_reduce_fusion), channel_id=1, source_target_pairs={{0,256},{64,320},{128,384},{192,448},{256,0},{320,64},{384,128},{4... | collective-permute-start | bytes 49160 | tf_op jit(solution)/shard_map/ppermute | solution.py:225
  243.4 1.9 collective-permute-start.4
  245.3 25.4 %collective-permute-done = f32[32,128]{1,0:T(8,128)S(1)} collective-permute-done((f32[32,128]{1,0:T(8,128)S(1)}, f32[32,128]{1,0:T(8,128)S(1)}, u32[]{:S(2)}, u32[]{:S(2)}) %collective-permute-start) | collective-permute-done | bytes 16416 | tf_op jit(solution)/shard_map/ppermute | solution.py:225
  270.7 7.4 %collective-permute-start.5 = (f32[32,128]{1,0:T(8,128)S(1)}, f32[32,128]{1,0:T(8,128)S(1)}, u32[]{:S(2)}, u32[]{:S(2)}) collective-permute-start(f32[32,128]{1,0:T(8,128)S(1)} %select_reduce_fusion), channel_id=1, source_target_pairs={{0,384},{64,448},{128,0},{192,64},{256,128},{320,192},{384,256},{4... | collective-permute-start | bytes 49160 | tf_op jit(solution)/shard_map/ppermute | solution.py:225
  278.1 0.0 collective-permute-done.1
  278.2 1.9 collective-permute-start.6
  280.1 0.0 collective-permute-done.2
  280.1 5.9 %collective-permute-done.3 = f32[32,128]{1,0:T(8,128)S(1)} collective-permute-done((f32[32,128]{1,0:T(8,128)S(1)}, f32[32,128]{1,0:T(8,128)S(1)}, u32[]{:S(2)}, u32[]{:S(2)}) %collective-permute-start.3) | collective-permute-done | bytes 16416 | tf_op jit(solution)/shard_map/ppermute | solution.py:225
  286.1 1.3 collective-permute-done.4
  287.4 38.0 %collective-permute-done.5 = f32[32,128]{1,0:T(8,128)S(1)} collective-permute-done((f32[32,128]{1,0:T(8,128)S(1)}, f32[32,128]{1,0:T(8,128)S(1)}, u32[]{:S(2)}, u32[]{:S(2)}) %collective-permute-start.5) | collective-permute-done | bytes 16416 | tf_op jit(solution)/shard_map/ppermute | solution.py:225
  325.4 0.3 collective-permute-done.6
  325.6 0.0 copy-done
  325.6 0.6 bitcast_add_fusion
  326.2 14.4 %all-to-all-done.1.in_ref = bf16[64,4,64,128]{3,2,1,0:T(8,128)(2,1)} async-done(((bf16[64,4,64,128]{3,2,1,0:T(8,128)(2,1)}), bf16[64,4,64,128]{3,2,1,0:T(8,128)(2,1)}, u32[]{:S(2)}, u32[]{:S(2)}) %all-to-all-start.1) | async-done | bytes 4194336 | tf_op jit(solution)/shard_map/all_to_all | solution.py:235
  340.6 66.6 %shard_map.112 = (bf16[128,2048]{1,0:T(8,128)(2,1)}, bf16[128,2048]{1,0:T(8,128)(2,1)}, bf16[128,2048]{1,0:T(8,128)(2,1)}, bf16[128,2048]{1,0:T(8,128)(2,1)}) custom-call(s32[16,2]{1,0:T(8,128)} %add_add_fusion.dest_ref, bf16[64,4,64,128]{3,2,1,0:T(8,128)(2,1)} %all-to-all-done.1.in_ref), custom_call_target="tpu_custom_call" | custom-call | tf_op jit(solution)/shard_map/pallas_call | solution.py:152
  (15 shorter events, 0.1 us)
Async XLA Ops:
  68.9 19.1 %copy-start.1 = (s32[1,32,4]{1,2,0:T(4,128)S(1)}, s32[1,32,4]{1,2,0:T(4,128)}, u32[]{:S(2)}) copy-start(s32[1,32,4]{1,2,0:T(4,128)} %param.12) | copy-start | bytes 1540
  68.9 125.5 %all-to-all-start = ((bf16[64,4,64,128]{3,2,1,0:T(8,128)(2,1)}), bf16[64,4,64,128]{3,2,1,0:T(8,128)(2,1)}, u32[]{:S(2)}, u32[]{:S(2)}) async-start(bf16[64,4,64,128]{3,2,1,0:T(8,128)(2,1)} %shard_map.110), calls=%async_computation | async-start | bytes 8388608 | tf_op jit(solution)/shard_map/all_to_all | solution.py:194
  215.8 109.8 %copy-start = (f32[32,128]{1,0:T(8,128)S(1)}, f32[32,128]{1,0:T(8,128)}, u32[]{:S(2)}) copy-start(f32[32,128]{1,0:T(8,128)} %param.13) | copy-start | bytes 49156
  215.8 124.8 %all-to-all-start.1 = ((bf16[64,4,64,128]{3,2,1,0:T(8,128)(2,1)}), bf16[64,4,64,128]{3,2,1,0:T(8,128)(2,1)}, u32[]{:S(2)}, u32[]{:S(2)}) async-start(bf16[64,4,64,128]{3,2,1,0:T(8,128)(2,1)} %shard_map.111), calls=%async_computation.1 | async-start | bytes 8388608 | tf_op jit(solution)/shard_map/all_to_all | solution.py:235
  231.6 39.1 %collective-permute-start = (f32[32,128]{1,0:T(8,128)S(1)}, f32[32,128]{1,0:T(8,128)S(1)}, u32[]{:S(2)}, u32[]{:S(2)}) collective-permute-start(f32[32,128]{1,0:T(8,128)S(1)} %select_reduce_fusion), channel_id=1, source_target_pairs={{0,64},{64,128},{128,192},{192,256},{256,320},{320,384},{384,448},... | collective-permute-start | bytes 49160 | tf_op jit(solution)/shard_map/ppermute | solution.py:225
  233.5 44.6 %collective-permute-start.1 = (f32[32,128]{1,0:T(8,128)S(1)}, f32[32,128]{1,0:T(8,128)S(1)}, u32[]{:S(2)}, u32[]{:S(2)}) collective-permute-start(f32[32,128]{1,0:T(8,128)S(1)} %select_reduce_fusion), channel_id=1, source_target_pairs={{0,128},{64,192},{128,256},{192,320},{256,384},{320,448},{384,0},{... | collective-permute-start | bytes 49160 | tf_op jit(solution)/shard_map/ppermute | solution.py:225
  235.4 44.7 %collective-permute-start.2 = (f32[32,128]{1,0:T(8,128)S(1)}, f32[32,128]{1,0:T(8,128)S(1)}, u32[]{:S(2)}, u32[]{:S(2)}) collective-permute-start(f32[32,128]{1,0:T(8,128)S(1)} %select_reduce_fusion), channel_id=1, source_target_pairs={{0,192},{64,256},{128,320},{192,384},{256,448},{320,0},{384,64},{4... | collective-permute-start | bytes 49160 | tf_op jit(solution)/shard_map/ppermute | solution.py:225
  237.4 48.7 %collective-permute-start.3 = (f32[32,128]{1,0:T(8,128)S(1)}, f32[32,128]{1,0:T(8,128)S(1)}, u32[]{:S(2)}, u32[]{:S(2)}) collective-permute-start(f32[32,128]{1,0:T(8,128)S(1)} %select_reduce_fusion), channel_id=1, source_target_pairs={{0,256},{64,320},{128,384},{192,448},{256,0},{320,64},{384,128},{4... | collective-permute-start | bytes 49160 | tf_op jit(solution)/shard_map/ppermute | solution.py:225
  243.4 44.0 %collective-permute-start.4 = (f32[32,128]{1,0:T(8,128)S(1)}, f32[32,128]{1,0:T(8,128)S(1)}, u32[]{:S(2)}, u32[]{:S(2)}) collective-permute-start(f32[32,128]{1,0:T(8,128)S(1)} %select_reduce_fusion), channel_id=1, source_target_pairs={{0,320},{64,384},{128,448},{192,0},{256,64},{320,128},{384,192},{4... | collective-permute-start | bytes 49160 | tf_op jit(solution)/shard_map/ppermute | solution.py:225
  270.7 54.7 %collective-permute-start.5 = (f32[32,128]{1,0:T(8,128)S(1)}, f32[32,128]{1,0:T(8,128)S(1)}, u32[]{:S(2)}, u32[]{:S(2)}) collective-permute-start(f32[32,128]{1,0:T(8,128)S(1)} %select_reduce_fusion), channel_id=1, source_target_pairs={{0,384},{64,448},{128,0},{192,64},{256,128},{320,192},{384,256},{4... | collective-permute-start | bytes 49160 | tf_op jit(solution)/shard_map/ppermute | solution.py:225
  278.2 47.5 %collective-permute-start.6 = (f32[32,128]{1,0:T(8,128)S(1)}, f32[32,128]{1,0:T(8,128)S(1)}, u32[]{:S(2)}, u32[]{:S(2)}) collective-permute-start(f32[32,128]{1,0:T(8,128)S(1)} %select_reduce_fusion), channel_id=1, source_target_pairs={{0,448},{64,0},{128,64},{192,128},{256,192},{320,256},{384,320},{4... | collective-permute-start | bytes 49160 | tf_op jit(solution)/shard_map/ppermute | solution.py:225

commit v11 on v9

--- a/solution.py
+++ b/solution.py
@@ -37,9 +37,11 @@
     return (out_full, grad_queries, grad_keys, grad_values)
 
 
-def routed_kernel(recv_ref, count_ref, member_ref, arrived_ref, out_ref):
+def routed_kernel(recv_ref, count_ref, member_ref, arrived_ref, out_ref, sums_ref):
     cluster_count, cluster_cap = member_ref.shape
     block_len = arrived_ref.shape[2]
+
+    sums_ref[...] = jnp.zeros(sums_ref.shape, sums_ref.dtype)
 
     def one_cluster(cluster, carry):
         present_count = count_ref[cluster]
@@ -61,6 +63,8 @@
                     query_pos = jnp.where(offsets // block_len == slot, query_pos + base, query_pos)
                     key_pos = jnp.where(key_offsets // block_len == slot, key_pos + base, key_pos)
                 results = attend_block(*tiles, query_pos, key_pos)
+                key_total = jnp.sum(tiles[1].astype(jnp.float32), axis=0, keepdims=True)
+                sums_ref[cluster] = jnp.broadcast_to(key_total, sums_ref.shape[1:])
                 for slot in range(used):
                     for index in range(4):
                         out_ref[rows[slot], index] = results[index][
@@ -77,9 +81,12 @@
     vmem = pl.BlockSpec(memory_space=pltpu.VMEM)
     return pl.pallas_call(
         routed_kernel,
-        out_shape=jax.ShapeDtypeStruct(arrived.shape, arrived.dtype),
+        out_shape=(
+            jax.ShapeDtypeStruct(arrived.shape, arrived.dtype),
+            jax.ShapeDtypeStruct((member_table.shape[0], 8, arrived.shape[3]), jnp.float32),
+        ),
         in_specs=[smem, smem, smem, vmem],
-        out_specs=vmem,
+        out_specs=(vmem, vmem),
     )(recv_table, present_count, member_table, arrived)
 
 
@@ -184,21 +191,14 @@
         concat_axis=0,
         tiled=True,
     )
-    block_sums = jnp.sum(arrived[:, 1].astype(jnp.float32), axis=1)
-    key_sum = jnp.sum(
-        jnp.where(present[:, None], block_sums[recv_row], 0.0).reshape(
-            groups_here, cluster_cap, head_dim
-        ),
-        axis=1,
-    )
     present_count = jnp.sum(present.reshape(groups_here, cluster_cap).astype(jnp.int32), axis=1)
-    outgoing = routed_attention(
+    outgoing, key_sums = routed_attention(
         recv_row.reshape(groups_here, cluster_cap).astype(jnp.int32),
         present_count,
         jnp.where(present, members, 0).reshape(groups_here, cluster_cap).astype(jnp.int32),
         arrived,
     )
-    outgoing, key_sum = lax.optimization_barrier((outgoing, key_sum))
+    key_sum = key_sums[:, 0]
     dp_size = lax.axis_size("dp")
     received = jnp.stack(
         [key_sum]

time: 284 us -> 281 us (0.989)
  the two profiles are of different devices: /device:TPU:26 before, /device:TPU:72 now
where the time goes in v11:
time: 281 us; the launch traced here: 280 us
  waiting for transfers between devices  199 us (71%)
  starting transfers between devices  48.2 us (17%)
  Pallas kernels  26.7 us (10%)
  other arithmetic  2.84 us (1%)
    all_to_all x1, waiting for transfers between devices, per_device(): lax.all_to_all(pack_blocks(dest_table, (queries[0], keys[0], values[0], c...  106 us
    ppermute x7, waiting for transfers between devices, per_device(): lax.ppermute(key_sum, 'dp', [(index, (index + shift) % dp_size) for index...  76.1 us
    pallas_call x1, Pallas kernels, routed_attention(): pl.pallas_call(routed_kernel, out_shape=(jax.ShapeDtypeStruct(arrived.sha...  18.7 us
    all_to_all x1, starting transfers between devices, per_device(): lax.all_to_all(pack_blocks(dest_table, (queries[0], keys[0], values[0], c...  17.7 us
    ppermute x7, starting transfers between devices, per_device(): lax.ppermute(key_sum, 'dp', [(index, (index + shift) % dp_size) for index...  17.5 us
    all_to_all x1, waiting for transfers between devices, per_device(): lax.all_to_all(outgoing, 'seq', split_axis=0, concat_axis=0, tiled=True)  17.4 us
    all_to_all x1, starting transfers between devices, per_device(): lax.all_to_all(outgoing, 'seq', split_axis=0, concat_axis=0, tiled=True)  13 us
  transfers between devices with their start and end apart: 9, of which 6 were waited for; matrix products, arithmetic and copies ran while one was open for 1% of the time, Pallas kernels for 0%

profile of v11, /device:TPU:72, one launch (start us, length us, event | category | flops | bytes accessed | tf_op | source)
XLA Modules:
  0.0 280.5 jit_solution(1757250749588640258)
XLA Ops:
  0.7 0.8 copy.34
  1.4 0.1 copy.38
  1.5 0.1 fusion.7
  1.6 0.1 copy.40
  1.7 0.7 add_add_fusion.dest_ref
  2.3 3.9 %shard_map.110 = bf16[64,4,64,128]{3,2,1,0:T(8,128)(2,1)} custom-call(s32[16,2]{1,0:T(8,128)} %add_add_fusion.dest_ref, bf16[128,2048]{1,0:T(8,128)(2,1)} %bitcast.30, bf16[128,2048]{1,0:T(8,128)(2,1)} %bitcast.31, bf16[128,2048]{1,0:T(8,128)(2,1)} %bitcast.32, bf16[128,2048]{1,0:T(8,128)(2,1)} %bitcast.33), custom_call_target="tpu_custom_call" | custom-call | tf_op jit(solution)/shard_map/pallas_call | solution.py:126
  6.2 0.0 copy-start.1
  6.2 17.7 %all-to-all-start = ((bf16[64,4,64,128]{3,2,1,0:T(8,128)(2,1)}), bf16[64,4,64,128]{3,2,1,0:T(8,128)(2,1)}, u32[]{:S(2)}, u32[]{:S(2)}) async-start(bf16[64,4,64,128]{3,2,1,0:T(8,128)(2,1)} %shard_map.110), calls=%async_computation | async-start | bytes 8388608 | tf_op jit(solution)/shard_map/all_to_all | solution.py:182
  23.9 0.0 copy-done.1
  23.9 0.1 copy.46
  24.0 0.1 reshape_squeeze.6
  24.2 0.2 convert_reduce_fusion
  24.3 0.1 reduce_sum.31
  24.4 0.1 copy.41
  24.5 1.3 broadcast_select_fusion
  25.8 106.0 %all-to-all-done.arrived_ref = bf16[64,4,64,128]{3,2,1,0:T(8,128)(2,1)} async-done(((bf16[64,4,64,128]{3,2,1,0:T(8,128)(2,1)}), bf16[64,4,64,128]{3,2,1,0:T(8,128)(2,1)}, u32[]{:S(2)}, u32[]{:S(2)}) %all-to-all-start) | async-done | bytes 4194336 | tf_op jit(solution)/shard_map/all_to_all | solution.py:182
  131.8 18.7 %shard_map.111 = (bf16[64,4,64,128]{3,2,1,0:T(8,128)(2,1)}, f32[32,8,128]{2,1,0:T(8,128)}) custom-call(s32[32,4]{1,0:T(8,128)} %get-tuple-element.18.recv_ref, s32[32]{0:T(128)} %get-tuple-element.19.count_ref, s32[32,4]{1,0:T(8,128)} %get-tuple-element.17.member_ref, bf16[64,4,64,128]{3,2,1,0:T(8,128)(2,1)} %all-to-all-done.arrived_ref), custom_call_target="tpu_custom_call" | custom-call | tf_op jit(solution)/shard_map/pallas_call | solution.py:82
  150.5 0.0 copy-start
  150.5 13.0 %all-to-all-start.1 = ((bf16[64,4,64,128]{3,2,1,0:T(8,128)(2,1)}), bf16[64,4,64,128]{3,2,1,0:T(8,128)(2,1)}, u32[]{:S(2)}, u32[]{:S(2)}) async-start(bf16[64,4,64,128]{3,2,1,0:T(8,128)(2,1)} %get-tuple-element.11), calls=%async_computation.1 | async-start | bytes 8388608 | tf_op jit(solution)/shard_map/all_to_all | solution.py:216
  163.7 0.9 slice.3
  164.6 1.9 collective-permute-start
  166.6 1.9 collective-permute-start.1
  168.5 3.4 %collective-permute-start.2 = (f32[32,128]{1,0:T(8,128)S(1)}, f32[32,128]{1,0:T(8,128)S(1)}, u32[]{:S(2)}, u32[]{:S(2)}) collective-permute-start(f32[32,128]{1,0:T(8,128)S(1)} %bitcast.36), channel_id=1, source_target_pairs={{0,192},{64,256},{128,320},{192,384},{256,448},{320,0},{384,64},{4... | collective-permute-start | bytes 49160 | tf_op jit(solution)/shard_map/ppermute | solution.py:206
  171.9 4.5 %collective-permute-start.3 = (f32[32,128]{1,0:T(8,128)S(1)}, f32[32,128]{1,0:T(8,128)S(1)}, u32[]{:S(2)}, u32[]{:S(2)}) collective-permute-start(f32[32,128]{1,0:T(8,128)S(1)} %bitcast.37), channel_id=1, source_target_pairs={{0,256},{64,320},{128,384},{192,448},{256,0},{320,64},{384,128},{4... | collective-permute-start | bytes 49160 | tf_op jit(solution)/shard_map/ppermute | solution.py:206
  176.4 1.9 collective-permute-start.4
  178.3 55.4 %collective-permute-done = f32[32,128]{1,0:T(8,128)S(1)} collective-permute-done((f32[32,128]{1,0:T(8,128)S(1)}, f32[32,128]{1,0:T(8,128)S(1)}, u32[]{:S(2)}, u32[]{:S(2)}) %collective-permute-start) | collective-permute-done | bytes 16416 | tf_op jit(solution)/shard_map/ppermute | solution.py:206
  233.7 1.9 collective-permute-start.5
  235.7 4.1 %collective-permute-done.1 = f32[32,128]{1,0:T(8,128)S(1)} collective-permute-done((f32[32,128]{1,0:T(8,128)S(1)}, f32[32,128]{1,0:T(8,128)S(1)}, u32[]{:S(2)}, u32[]{:S(2)}) %collective-permute-start.1) | collective-permute-done | bytes 16416 | tf_op jit(solution)/shard_map/ppermute | solution.py:206
  239.8 1.9 collective-permute-start.6
  241.7 0.0 collective-permute-done.2
  241.7 0.0 collective-permute-done.3
  241.7 0.0 collective-permute-done.4
  241.8 16.3 %collective-permute-done.5 = f32[32,128]{1,0:T(8,128)S(1)} collective-permute-done((f32[32,128]{1,0:T(8,128)S(1)}, f32[32,128]{1,0:T(8,128)S(1)}, u32[]{:S(2)}, u32[]{:S(2)}) %collective-permute-start.5) | collective-permute-done | bytes 16416 | tf_op jit(solution)/shard_map/ppermute | solution.py:206
  258.1 0.3 collective-permute-done.6
  258.4 0.0 copy-done
  258.4 0.6 bitcast_add_fusion
  259.0 17.4 %all-to-all-done.1.in_ref = bf16[64,4,64,128]{3,2,1,0:T(8,128)(2,1)} async-done(((bf16[64,4,64,128]{3,2,1,0:T(8,128)(2,1)}), bf16[64,4,64,128]{3,2,1,0:T(8,128)(2,1)}, u32[]{:S(2)}, u32[]{:S(2)}) %all-to-all-start.1) | async-done | bytes 4194336 | tf_op jit(solution)/shard_map/all_to_all | solution.py:216
  276.4 4.1 %shard_map.112 = (bf16[128,2048]{1,0:T(8,128)(2,1)}, bf16[128,2048]{1,0:T(8,128)(2,1)}, bf16[128,2048]{1,0:T(8,128)(2,1)}, bf16[128,2048]{1,0:T(8,128)(2,1)}) custom-call(s32[16,2]{1,0:T(8,128)} %add_add_fusion.dest_ref, bf16[64,4,64,128]{3,2,1,0:T(8,128)(2,1)} %all-to-all-done.1.in_ref), custom_call_target="tpu_custom_call" | custom-call | tf_op jit(solution)/shard_map/pallas_call | solution.py:141
  (13 shorter events, 0.1 us)
Async XLA Ops:
  6.2 17.7 %copy-start.1 = (s32[1,32,4]{1,2,0:T(4,128)S(1)}, s32[1,32,4]{1,2,0:T(4,128)}, u32[]{:S(2)}) copy-start(s32[1,32,4]{1,2,0:T(4,128)} %param.12) | copy-start | bytes 1540
  6.2 125.5 %all-to-all-start = ((bf16[64,4,64,128]{3,2,1,0:T(8,128)(2,1)}), bf16[64,4,64,128]{3,2,1,0:T(8,128)(2,1)}, u32[]{:S(2)}, u32[]{:S(2)}) async-start(bf16[64,4,64,128]{3,2,1,0:T(8,128)(2,1)} %shard_map.110), calls=%async_computation | async-start | bytes 8388608 | tf_op jit(solution)/shard_map/all_to_all | solution.py:182
  150.5 107.9 %copy-start = (f32[32,128]{1,0:T(8,128)S(1)}, f32[32,128]{1,0:T(8,128)}, u32[]{:S(2)}) copy-start(f32[32,128]{1,0:T(8,128)} %param.13) | copy-start | bytes 49156
  150.5 125.9 %all-to-all-start.1 = ((bf16[64,4,64,128]{3,2,1,0:T(8,128)(2,1)}), bf16[64,4,64,128]{3,2,1,0:T(8,128)(2,1)}, u32[]{:S(2)}, u32[]{:S(2)}) async-start(bf16[64,4,64,128]{3,2,1,0:T(8,128)(2,1)} %get-tuple-element.11), calls=%async_computation.1 | async-start | bytes 8388608 | tf_op jit(solution)/shard_map/all_to_all | solution.py:216
  164.6 69.1 %collective-permute-start = (f32[32,128]{1,0:T(8,128)S(1)}, f32[32,128]{1,0:T(8,128)S(1)}, u32[]{:S(2)}, u32[]{:S(2)}) collective-permute-start(f32[32,128]{1,0:T(8,128)S(1)} %bitcast.34), channel_id=1, source_target_pairs={{0,64},{64,128},{128,192},{192,256},{256,320},{320,384},{384,448},... | collective-permute-start | bytes 49160 | tf_op jit(solution)/shard_map/ppermute | solution.py:206
  166.6 73.2 %collective-permute-start.1 = (f32[32,128]{1,0:T(8,128)S(1)}, f32[32,128]{1,0:T(8,128)S(1)}, u32[]{:S(2)}, u32[]{:S(2)}) collective-permute-start(f32[32,128]{1,0:T(8,128)S(1)} %bitcast.35), channel_id=1, source_target_pairs={{0,128},{64,192},{128,256},{192,320},{256,384},{320,448},{384,0},{... | collective-permute-start | bytes 49160 | tf_op jit(solution)/shard_map/ppermute | solution.py:206
  168.5 73.2 %collective-permute-start.2 = (f32[32,128]{1,0:T(8,128)S(1)}, f32[32,128]{1,0:T(8,128)S(1)}, u32[]{:S(2)}, u32[]{:S(2)}) collective-permute-start(f32[32,128]{1,0:T(8,128)S(1)} %bitcast.36), channel_id=1, source_target_pairs={{0,192},{64,256},{128,320},{192,384},{256,448},{320,0},{384,64},{4... | collective-permute-start | bytes 49160 | tf_op jit(solution)/shard_map/ppermute | solution.py:206
  171.9 69.8 %collective-permute-start.3 = (f32[32,128]{1,0:T(8,128)S(1)}, f32[32,128]{1,0:T(8,128)S(1)}, u32[]{:S(2)}, u32[]{:S(2)}) collective-permute-start(f32[32,128]{1,0:T(8,128)S(1)} %bitcast.37), channel_id=1, source_target_pairs={{0,256},{64,320},{128,384},{192,448},{256,0},{320,64},{384,128},{4... | collective-permute-start | bytes 49160 | tf_op jit(solution)/shard_map/ppermute | solution.py:206
  176.4 65.3 %collective-permute-start.4 = (f32[32,128]{1,0:T(8,128)S(1)}, f32[32,128]{1,0:T(8,128)S(1)}, u32[]{:S(2)}, u32[]{:S(2)}) collective-permute-start(f32[32,128]{1,0:T(8,128)S(1)} %bitcast.38), channel_id=1, source_target_pairs={{0,320},{64,384},{128,448},{192,0},{256,64},{320,128},{384,192},{4... | collective-permute-start | bytes 49160 | tf_op jit(solution)/shard_map/ppermute | solution.py:206
  233.7 24.4 %collective-permute-start.5 = (f32[32,128]{1,0:T(8,128)S(1)}, f32[32,128]{1,0:T(8,128)S(1)}, u32[]{:S(2)}, u32[]{:S(2)}) collective-permute-start(f32[32,128]{1,0:T(8,128)S(1)} %bitcast.40), channel_id=1, source_target_pairs={{0,384},{64,448},{128,0},{192,64},{256,128},{320,192},{384,256},{4... | collective-permute-start | bytes 49160 | tf_op jit(solution)/shard_map/ppermute | solution.py:206
  239.8 18.6 %collective-permute-start.6 = (f32[32,128]{1,0:T(8,128)S(1)}, f32[32,128]{1,0:T(8,128)S(1)}, u32[]{:S(2)}, u32[]{:S(2)}) collective-permute-start(f32[32,128]{1,0:T(8,128)S(1)} %bitcast.41), channel_id=1, source_target_pairs={{0,448},{64,0},{128,64},{192,128},{256,192},{320,256},{384,320},{4... | collective-permute-start | bytes 49160 | tf_op jit(solution)/shard_map/ppermute | solution.py:206

commit v12 on v9

--- a/solution.py
+++ b/solution.py
@@ -69,7 +69,7 @@
 
         return carry
 
-    lax.fori_loop(0, cluster_count, one_cluster, 0)
+    lax.fori_loop(0, cluster_count, one_cluster, 0, unroll=2)
 
 
 def routed_attention(recv_table, present_count, member_table, arrived):

time: 284 us -> 284 us (level)
  the two profiles are of different devices: /device:TPU:26 before, /device:TPU:74 now
where the time goes in v12:
time: 284 us; the launch traced here: 285 us
  waiting for transfers between devices  184 us (65%)
  starting transfers between devices  66.2 us (23%)
  Pallas kernels  26.8 us (9%)
  other arithmetic  5.08 us (2%)
    all_to_all x1, waiting for transfers between devices, per_device(): lax.all_to_all(pack_blocks(dest_table, (queries[0], keys[0], values[0], c...  105 us
    ppermute x7, waiting for transfers between devices, per_device(): lax.ppermute(key_sum, 'dp', [(index, (index + shift) % dp_size) for index...  61.8 us
    ppermute x7, starting transfers between devices, per_device(): lax.ppermute(key_sum, 'dp', [(index, (index + shift) % dp_size) for index...  33.3 us
    pallas_call x1, Pallas kernels, routed_attention(): pl.pallas_call(routed_kernel, out_shape=jax.ShapeDtypeStruct(arrived.shap...  18.9 us
    all_to_all x1, starting transfers between devices, per_device(): lax.all_to_all(pack_blocks(dest_table, (queries[0], keys[0], values[0], c...  17.6 us
    all_to_all x1, waiting for transfers between devices, per_device(): lax.all_to_all(outgoing, 'seq', split_axis=0, concat_axis=0, tiled=True)  17.5 us
    all_to_all x1, starting transfers between devices, per_device(): lax.all_to_all(outgoing, 'seq', split_axis=0, concat_axis=0, tiled=True)  15.2 us
  transfers between devices with their start and end apart: 9, of which 7 were waited for; matrix products, arithmetic and copies ran while one was open for 1% of the time, Pallas kernels for 0%

profile of v12, /device:TPU:74, one launch (start us, length us, event | category | flops | bytes accessed | tf_op | source)
XLA Modules:
  0.0 285.3 jit_solution(13635087336681594654)
XLA Ops:
  0.7 0.8 copy.36
  1.4 0.1 copy.40
  1.5 0.1 fusion.7
  1.6 0.1 copy.42
  1.7 0.7 add_add_fusion.dest_ref
  2.3 3.9 %shard_map.110 = bf16[64,4,64,128]{3,2,1,0:T(8,128)(2,1)} custom-call(s32[16,2]{1,0:T(8,128)} %add_add_fusion.dest_ref, bf16[128,2048]{1,0:T(8,128)(2,1)} %bitcast.35, bf16[128,2048]{1,0:T(8,128)(2,1)} %bitcast.36, bf16[128,2048]{1,0:T(8,128)(2,1)} %bitcast.37, bf16[128,2048]{1,0:T(8,128)(2,1)} %bitcast.38), custom_call_target="tpu_custom_call" | custom-call | tf_op jit(solution)/shard_map/pallas_call | solution.py:119
  6.2 0.0 copy-start.1
  6.2 17.6 %all-to-all-start = ((bf16[64,4,64,128]{3,2,1,0:T(8,128)(2,1)}), bf16[64,4,64,128]{3,2,1,0:T(8,128)(2,1)}, u32[]{:S(2)}, u32[]{:S(2)}) async-start(bf16[64,4,64,128]{3,2,1,0:T(8,128)(2,1)} %shard_map.110), calls=%async_computation | async-start | bytes 8388608 | tf_op jit(solution)/shard_map/all_to_all | solution.py:175
  23.9 0.0 copy-done.1
  23.9 0.1 copy.48
  24.0 0.1 reshape_squeeze.8
  24.1 0.1 reshape_squeeze.9
  24.2 0.1 copy.43
  24.3 0.2 convert_reduce_fusion.1
  24.5 0.1 reduce_sum.51
  24.6 0.6 broadcast_select_fusion
  25.2 1.2 convert_reduce_fusion.2
  26.5 104.8 %all-to-all-done.arrived_ref = bf16[64,4,64,128]{3,2,1,0:T(8,128)(2,1)} async-done(((bf16[64,4,64,128]{3,2,1,0:T(8,128)(2,1)}), bf16[64,4,64,128]{3,2,1,0:T(8,128)(2,1)}, u32[]{:S(2)}, u32[]{:S(2)}) %all-to-all-start) | async-done | bytes 4194336 | tf_op jit(solution)/shard_map/all_to_all | solution.py:175
  131.3 1.5 convert_reduce_fusion
  132.8 0.6 gather_fusion
  133.5 0.1 select_reduce_fusion
  133.6 18.9 %shard_map.111 = bf16[64,4,64,128]{3,2,1,0:T(8,128)(2,1)} custom-call(s32[32,4]{1,0:T(8,128)} %get-tuple-element.20.recv_ref, s32[32]{0:T(128)} %get-tuple-element.19.count_ref, s32[32,4]{1,0:T(8,128)} %get-tuple-element.17.member_ref, bf16[64,4,64,128]{3,2,1,0:T(8,128)(2,1)} %all-to-all-done.arrived_ref), custom_call_target="tpu_custom_call" | custom-call | tf_op jit(solution)/shard_map/pallas_call | solution.py:78
  152.5 0.0 copy-start
  152.5 15.2 %all-to-all-start.1 = ((bf16[64,4,64,128]{3,2,1,0:T(8,128)(2,1)}), bf16[64,4,64,128]{3,2,1,0:T(8,128)(2,1)}, u32[]{:S(2)}, u32[]{:S(2)}) async-start(bf16[64,4,64,128]{3,2,1,0:T(8,128)(2,1)} %shard_map.111), calls=%async_computation.1 | async-start | bytes 8388608 | tf_op jit(solution)/shard_map/all_to_all | solution.py:216
  167.8 1.9 collective-permute-start
  169.8 1.9 collective-permute-start.1
  171.7 2.1 collective-permute-start.2
  173.8 5.8 %collective-permute-start.3 = (f32[32,128]{1,0:T(8,128)S(1)}, f32[32,128]{1,0:T(8,128)S(1)}, u32[]{:S(2)}, u32[]{:S(2)}) collective-permute-start(f32[32,128]{1,0:T(8,128)S(1)} %select_reduce_fusion), channel_id=1, source_target_pairs={{0,256},{64,320},{128,384},{192,448},{256,0},{320,64},{384,128},{4... | collective-permute-start | bytes 49160 | tf_op jit(solution)/shard_map/ppermute | solution.py:206
  179.6 1.9 collective-permute-start.4
  181.6 22.3 %collective-permute-done = f32[32,128]{1,0:T(8,128)S(1)} collective-permute-done((f32[32,128]{1,0:T(8,128)S(1)}, f32[32,128]{1,0:T(8,128)S(1)}, u32[]{:S(2)}, u32[]{:S(2)}) %collective-permute-start) | collective-permute-done | bytes 16416 | tf_op jit(solution)/shard_map/ppermute | solution.py:206
  203.9 17.7 %collective-permute-start.5 = (f32[32,128]{1,0:T(8,128)S(1)}, f32[32,128]{1,0:T(8,128)S(1)}, u32[]{:S(2)}, u32[]{:S(2)}) collective-permute-start(f32[32,128]{1,0:T(8,128)S(1)} %select_reduce_fusion), channel_id=1, source_target_pairs={{0,384},{64,448},{128,0},{192,64},{256,128},{320,192},{384,256},{4... | collective-permute-start | bytes 49160 | tf_op jit(solution)/shard_map/ppermute | solution.py:206
  221.6 0.0 collective-permute-done.1
  221.6 1.9 collective-permute-start.6
  223.5 0.0 collective-permute-done.2
  223.6 7.7 %collective-permute-done.3 = f32[32,128]{1,0:T(8,128)S(1)} collective-permute-done((f32[32,128]{1,0:T(8,128)S(1)}, f32[32,128]{1,0:T(8,128)S(1)}, u32[]{:S(2)}, u32[]{:S(2)}) %collective-permute-start.3) | collective-permute-done | bytes 16416 | tf_op jit(solution)/shard_map/ppermute | solution.py:206
  231.3 2.3 collective-permute-done.4
  233.6 29.3 %collective-permute-done.5 = f32[32,128]{1,0:T(8,128)S(1)} collective-permute-done((f32[32,128]{1,0:T(8,128)S(1)}, f32[32,128]{1,0:T(8,128)S(1)}, u32[]{:S(2)}, u32[]{:S(2)}) %collective-permute-start.5) | collective-permute-done | bytes 16416 | tf_op jit(solution)/shard_map/ppermute | solution.py:206
  262.8 0.3 collective-permute-done.6
  263.1 0.0 copy-done
  263.1 0.6 bitcast_add_fusion
  263.7 17.5 %all-to-all-done.1.in_ref = bf16[64,4,64,128]{3,2,1,0:T(8,128)(2,1)} async-done(((bf16[64,4,64,128]{3,2,1,0:T(8,128)(2,1)}), bf16[64,4,64,128]{3,2,1,0:T(8,128)(2,1)}, u32[]{:S(2)}, u32[]{:S(2)}) %all-to-all-start.1) | async-done | bytes 4194336 | tf_op jit(solution)/shard_map/all_to_all | solution.py:216
  281.2 4.1 %shard_map.112 = (bf16[128,2048]{1,0:T(8,128)(2,1)}, bf16[128,2048]{1,0:T(8,128)(2,1)}, bf16[128,2048]{1,0:T(8,128)(2,1)}, bf16[128,2048]{1,0:T(8,128)(2,1)}) custom-call(s32[16,2]{1,0:T(8,128)} %add_add_fusion.dest_ref, bf16[64,4,64,128]{3,2,1,0:T(8,128)(2,1)} %all-to-all-done.1.in_ref), custom_call_target="tpu_custom_call" | custom-call | tf_op jit(solution)/shard_map/pallas_call | solution.py:134
  (15 shorter events, 0.1 us)
Async XLA Ops:
  6.2 17.7 %copy-start.1 = (s32[1,32,4]{1,2,0:T(4,128)S(1)}, s32[1,32,4]{1,2,0:T(4,128)}, u32[]{:S(2)}) copy-start(s32[1,32,4]{1,2,0:T(4,128)} %param.12) | copy-start | bytes 1540
  6.2 125.1 %all-to-all-start = ((bf16[64,4,64,128]{3,2,1,0:T(8,128)(2,1)}), bf16[64,4,64,128]{3,2,1,0:T(8,128)(2,1)}, u32[]{:S(2)}, u32[]{:S(2)}) async-start(bf16[64,4,64,128]{3,2,1,0:T(8,128)(2,1)} %shard_map.110), calls=%async_computation | async-start | bytes 8388608 | tf_op jit(solution)/shard_map/all_to_all | solution.py:175
  152.5 110.6 %copy-start = (f32[32,128]{1,0:T(8,128)S(1)}, f32[32,128]{1,0:T(8,128)}, u32[]{:S(2)}) copy-start(f32[32,128]{1,0:T(8,128)} %param.13) | copy-start | bytes 49156
  152.5 128.7 %all-to-all-start.1 = ((bf16[64,4,64,128]{3,2,1,0:T(8,128)(2,1)}), bf16[64,4,64,128]{3,2,1,0:T(8,128)(2,1)}, u32[]{:S(2)}, u32[]{:S(2)}) async-start(bf16[64,4,64,128]{3,2,1,0:T(8,128)(2,1)} %shard_map.111), calls=%async_computation.1 | async-start | bytes 8388608 | tf_op jit(solution)/shard_map/all_to_all | solution.py:216
  167.8 36.0 %collective-permute-start = (f32[32,128]{1,0:T(8,128)S(1)}, f32[32,128]{1,0:T(8,128)S(1)}, u32[]{:S(2)}, u32[]{:S(2)}) collective-permute-start(f32[32,128]{1,0:T(8,128)S(1)} %select_reduce_fusion), channel_id=1, source_target_pairs={{0,64},{64,128},{128,192},{192,256},{256,320},{320,384},{384,448},... | collective-permute-start | bytes 49160 | tf_op jit(solution)/shard_map/ppermute | solution.py:206
  169.8 51.8 %collective-permute-start.1 = (f32[32,128]{1,0:T(8,128)S(1)}, f32[32,128]{1,0:T(8,128)S(1)}, u32[]{:S(2)}, u32[]{:S(2)}) collective-permute-start(f32[32,128]{1,0:T(8,128)S(1)} %select_reduce_fusion), channel_id=1, source_target_pairs={{0,128},{64,192},{128,256},{192,320},{256,384},{320,448},{384,0},{... | collective-permute-start | bytes 49160 | tf_op jit(solution)/shard_map/ppermute | solution.py:206
  171.7 51.8 %collective-permute-start.2 = (f32[32,128]{1,0:T(8,128)S(1)}, f32[32,128]{1,0:T(8,128)S(1)}, u32[]{:S(2)}, u32[]{:S(2)}) collective-permute-start(f32[32,128]{1,0:T(8,128)S(1)} %select_reduce_fusion), channel_id=1, source_target_pairs={{0,192},{64,256},{128,320},{192,384},{256,448},{320,0},{384,64},{4... | collective-permute-start | bytes 49160 | tf_op jit(solution)/shard_map/ppermute | solution.py:206
  173.8 57.5 %collective-permute-start.3 = (f32[32,128]{1,0:T(8,128)S(1)}, f32[32,128]{1,0:T(8,128)S(1)}, u32[]{:S(2)}, u32[]{:S(2)}) collective-permute-start(f32[32,128]{1,0:T(8,128)S(1)} %select_reduce_fusion), channel_id=1, source_target_pairs={{0,256},{64,320},{128,384},{192,448},{256,0},{320,64},{384,128},{4... | collective-permute-start | bytes 49160 | tf_op jit(solution)/shard_map/ppermute | solution.py:206
  179.6 53.9 %collective-permute-start.4 = (f32[32,128]{1,0:T(8,128)S(1)}, f32[32,128]{1,0:T(8,128)S(1)}, u32[]{:S(2)}, u32[]{:S(2)}) collective-permute-start(f32[32,128]{1,0:T(8,128)S(1)} %select_reduce_fusion), channel_id=1, source_target_pairs={{0,320},{64,384},{128,448},{192,0},{256,64},{320,128},{384,192},{4... | collective-permute-start | bytes 49160 | tf_op jit(solution)/shard_map/ppermute | solution.py:206
  203.9 59.0 %collective-permute-start.5 = (f32[32,128]{1,0:T(8,128)S(1)}, f32[32,128]{1,0:T(8,128)S(1)}, u32[]{:S(2)}, u32[]{:S(2)}) collective-permute-start(f32[32,128]{1,0:T(8,128)S(1)} %select_reduce_fusion), channel_id=1, source_target_pairs={{0,384},{64,448},{128,0},{192,64},{256,128},{320,192},{384,256},{4... | collective-permute-start | bytes 49160 | tf_op jit(solution)/shard_map/ppermute | solution.py:206
  221.6 41.5 %collective-permute-start.6 = (f32[32,128]{1,0:T(8,128)S(1)}, f32[32,128]{1,0:T(8,128)S(1)}, u32[]{:S(2)}, u32[]{:S(2)}) collective-permute-start(f32[32,128]{1,0:T(8,128)S(1)} %select_reduce_fusion), channel_id=1, source_target_pairs={{0,448},{64,0},{128,64},{192,128},{256,192},{320,256},{384,320},{4... | collective-permute-start | bytes 49160 | tf_op jit(solution)/shard_map/ppermute | solution.py:206

commit v13 on v12

--- a/solution.py
+++ b/solution.py
@@ -69,7 +69,7 @@
 
         return carry
 
-    lax.fori_loop(0, cluster_count, one_cluster, 0, unroll=2)
+    lax.fori_loop(0, cluster_count, one_cluster, 0, unroll=4)
 
 
 def routed_attention(recv_table, present_count, member_table, arrived):

time: 284 us -> 281 us (0.989)
  the two profiles are of different devices: /device:TPU:74 before, /device:TPU:59 now
where the time goes in v13:
time: 281 us; the launch traced here: 280 us
  waiting for transfers between devices  131 us (47%)
  starting transfers between devices  119 us (42%)
  Pallas kernels  22.3 us (8%)
  other arithmetic  5.08 us (2%)
    all_to_all x1, waiting for transfers between devices, per_device(): lax.all_to_all(pack_blocks(dest_table, (queries[0], keys[0], values[0], c...  93.3 us
    ppermute x7, starting transfers between devices, per_device(): lax.ppermute(key_sum, 'dp', [(index, (index + shift) % dp_size) for index...  73.3 us
    ppermute x7, waiting for transfers between devices, per_device(): lax.ppermute(key_sum, 'dp', [(index, (index + shift) % dp_size) for index...  37.3 us
    all_to_all x1, starting transfers between devices, per_device(): lax.all_to_all(outgoing, 'seq', split_axis=0, concat_axis=0, tiled=True)  27.1 us
    all_to_all x1, starting transfers between devices, per_device(): lax.all_to_all(pack_blocks(dest_table, (queries[0], keys[0], values[0], c...  18.4 us
    pallas_call x1, Pallas kernels, routed_attention(): pl.pallas_call(routed_kernel, out_shape=jax.ShapeDtypeStruct(arrived.shap...  14.4 us
  transfers between devices with their start and end apart: 9, of which 3 were waited for; matrix products, arithmetic and copies ran while one was open for 1% of the time, Pallas kernels for 0%

profile of v13, /device:TPU:59, one launch (start us, length us, event | category | flops | bytes accessed | tf_op | source)
XLA Modules:
  0.0 280.1 jit_solution(723243857121302260)
XLA Ops:
  0.7 0.8 copy.36
  1.4 0.1 copy.40
  1.5 0.1 fusion.7
  1.6 0.1 copy.42
  1.7 0.7 add_add_fusion.dest_ref
  2.3 3.9 %shard_map.110 = bf16[64,4,64,128]{3,2,1,0:T(8,128)(2,1)} custom-call(s32[16,2]{1,0:T(8,128)} %add_add_fusion.dest_ref, bf16[128,2048]{1,0:T(8,128)(2,1)} %bitcast.35, bf16[128,2048]{1,0:T(8,128)(2,1)} %bitcast.36, bf16[128,2048]{1,0:T(8,128)(2,1)} %bitcast.37, bf16[128,2048]{1,0:T(8,128)(2,1)} %bitcast.38), custom_call_target="tpu_custom_call" | custom-call | tf_op jit(solution)/shard_map/pallas_call | solution.py:119
  6.2 0.0 copy-start.1
  6.2 18.4 %all-to-all-start = ((bf16[64,4,64,128]{3,2,1,0:T(8,128)(2,1)}), bf16[64,4,64,128]{3,2,1,0:T(8,128)(2,1)}, u32[]{:S(2)}, u32[]{:S(2)}) async-start(bf16[64,4,64,128]{3,2,1,0:T(8,128)(2,1)} %shard_map.110), calls=%async_computation | async-start | bytes 8388608 | tf_op jit(solution)/shard_map/all_to_all | solution.py:175
  24.7 0.0 copy-done.1
  24.7 0.1 copy.48
  24.8 0.1 reshape_squeeze.8
  24.9 0.1 reshape_squeeze.9
  25.0 0.1 copy.43
  25.1 0.2 convert_reduce_fusion.1
  25.3 0.1 reduce_sum.51
  25.4 0.6 broadcast_select_fusion
  26.0 1.2 convert_reduce_fusion.2
  27.3 93.3 %all-to-all-done.arrived_ref = bf16[64,4,64,128]{3,2,1,0:T(8,128)(2,1)} async-done(((bf16[64,4,64,128]{3,2,1,0:T(8,128)(2,1)}), bf16[64,4,64,128]{3,2,1,0:T(8,128)(2,1)}, u32[]{:S(2)}, u32[]{:S(2)}) %all-to-all-start) | async-done | bytes 4194336 | tf_op jit(solution)/shard_map/all_to_all | solution.py:175
  120.6 1.5 convert_reduce_fusion
  122.1 0.6 gather_fusion
  122.7 0.1 select_reduce_fusion
  122.8 14.4 %shard_map.111 = bf16[64,4,64,128]{3,2,1,0:T(8,128)(2,1)} custom-call(s32[32,4]{1,0:T(8,128)} %get-tuple-element.20.recv_ref, s32[32]{0:T(128)} %get-tuple-element.19.count_ref, s32[32,4]{1,0:T(8,128)} %get-tuple-element.17.member_ref, bf16[64,4,64,128]{3,2,1,0:T(8,128)(2,1)} %all-to-all-done.arrived_ref), custom_call_target="tpu_custom_call" | custom-call | tf_op jit(solution)/shard_map/pallas_call | solution.py:78
  137.2 0.0 copy-start
  137.2 27.1 %all-to-all-start.1 = ((bf16[64,4,64,128]{3,2,1,0:T(8,128)(2,1)}), bf16[64,4,64,128]{3,2,1,0:T(8,128)(2,1)}, u32[]{:S(2)}, u32[]{:S(2)}) async-start(bf16[64,4,64,128]{3,2,1,0:T(8,128)(2,1)} %shard_map.111), calls=%async_computation.1 | async-start | bytes 8388608 | tf_op jit(solution)/shard_map/all_to_all | solution.py:216
  164.5 1.9 collective-permute-start
  166.5 9.3 %collective-permute-start.1 = (f32[32,128]{1,0:T(8,128)S(1)}, f32[32,128]{1,0:T(8,128)S(1)}, u32[]{:S(2)}, u32[]{:S(2)}) collective-permute-start(f32[32,128]{1,0:T(8,128)S(1)} %select_reduce_fusion), channel_id=1, source_target_pairs={{0,128},{64,192},{128,256},{192,320},{256,384},{320,448},{384,0},{... | collective-permute-start | bytes 49160 | tf_op jit(solution)/shard_map/ppermute | solution.py:206
  175.7 1.9 collective-permute-start.2
  177.7 1.9 collective-permute-start.3
  179.6 3.6 %collective-permute-start.4 = (f32[32,128]{1,0:T(8,128)S(1)}, f32[32,128]{1,0:T(8,128)S(1)}, u32[]{:S(2)}, u32[]{:S(2)}) collective-permute-start(f32[32,128]{1,0:T(8,128)S(1)} %select_reduce_fusion), channel_id=1, source_target_pairs={{0,320},{64,384},{128,448},{192,0},{256,64},{320,128},{384,192},{4... | collective-permute-start | bytes 49160 | tf_op jit(solution)/shard_map/ppermute | solution.py:206
  183.2 31.5 %collective-permute-done = f32[32,128]{1,0:T(8,128)S(1)} collective-permute-done((f32[32,128]{1,0:T(8,128)S(1)}, f32[32,128]{1,0:T(8,128)S(1)}, u32[]{:S(2)}, u32[]{:S(2)}) %collective-permute-start) | collective-permute-done | bytes 16416 | tf_op jit(solution)/shard_map/ppermute | solution.py:206
  214.7 6.5 %collective-permute-start.5 = (f32[32,128]{1,0:T(8,128)S(1)}, f32[32,128]{1,0:T(8,128)S(1)}, u32[]{:S(2)}, u32[]{:S(2)}) collective-permute-start(f32[32,128]{1,0:T(8,128)S(1)} %select_reduce_fusion), channel_id=1, source_target_pairs={{0,384},{64,448},{128,0},{192,64},{256,128},{320,192},{384,256},{4... | collective-permute-start | bytes 49160 | tf_op jit(solution)/shard_map/ppermute | solution.py:206
  221.2 0.0 collective-permute-done.1
  221.2 48.2 %collective-permute-start.6 = (f32[32,128]{1,0:T(8,128)S(1)}, f32[32,128]{1,0:T(8,128)S(1)}, u32[]{:S(2)}, u32[]{:S(2)}) collective-permute-start(f32[32,128]{1,0:T(8,128)S(1)} %select_reduce_fusion), channel_id=1, source_target_pairs={{0,448},{64,0},{128,64},{192,128},{256,192},{320,256},{384,320},{4... | collective-permute-start | bytes 49160 | tf_op jit(solution)/shard_map/ppermute | solution.py:206
  269.4 0.0 collective-permute-done.2
  269.5 0.0 collective-permute-done.3
  269.5 0.0 collective-permute-done.4
  269.5 0.0 collective-permute-done.5
  269.5 5.8 %collective-permute-done.6 = f32[32,128]{1,0:T(8,128)S(1)} collective-permute-done((f32[32,128]{1,0:T(8,128)S(1)}, f32[32,128]{1,0:T(8,128)S(1)}, u32[]{:S(2)}, u32[]{:S(2)}) %collective-permute-start.6) | collective-permute-done | bytes 16416 | tf_op jit(solution)/shard_map/ppermute | solution.py:206
  275.4 0.0 copy-done
  275.4 0.6 bitcast_add_fusion
  276.0 0.0 all-to-all-done.1.in_ref
  276.0 4.1 %shard_map.112 = (bf16[128,2048]{1,0:T(8,128)(2,1)}, bf16[128,2048]{1,0:T(8,128)(2,1)}, bf16[128,2048]{1,0:T(8,128)(2,1)}, bf16[128,2048]{1,0:T(8,128)(2,1)}) custom-call(s32[16,2]{1,0:T(8,128)} %add_add_fusion.dest_ref, bf16[64,4,64,128]{3,2,1,0:T(8,128)(2,1)} %all-to-all-done.1.in_ref), custom_call_target="tpu_custom_call" | custom-call | tf_op jit(solution)/shard_map/pallas_call | solution.py:134
  (15 shorter events, 0.1 us)
Async XLA Ops:
  6.2 18.5 %copy-start.1 = (s32[1,32,4]{1,2,0:T(4,128)S(1)}, s32[1,32,4]{1,2,0:T(4,128)}, u32[]{:S(2)}) copy-start(s32[1,32,4]{1,2,0:T(4,128)} %param.12) | copy-start | bytes 1540
  6.2 114.3 %all-to-all-start = ((bf16[64,4,64,128]{3,2,1,0:T(8,128)(2,1)}), bf16[64,4,64,128]{3,2,1,0:T(8,128)(2,1)}, u32[]{:S(2)}, u32[]{:S(2)}) async-start(bf16[64,4,64,128]{3,2,1,0:T(8,128)(2,1)} %shard_map.110), calls=%async_computation | async-start | bytes 8388608 | tf_op jit(solution)/shard_map/all_to_all | solution.py:175
  137.2 138.2 %copy-start = (f32[32,128]{1,0:T(8,128)S(1)}, f32[32,128]{1,0:T(8,128)}, u32[]{:S(2)}) copy-start(f32[32,128]{1,0:T(8,128)} %param.13) | copy-start | bytes 49156
  137.2 138.8 %all-to-all-start.1 = ((bf16[64,4,64,128]{3,2,1,0:T(8,128)(2,1)}), bf16[64,4,64,128]{3,2,1,0:T(8,128)(2,1)}, u32[]{:S(2)}, u32[]{:S(2)}) async-start(bf16[64,4,64,128]{3,2,1,0:T(8,128)(2,1)} %shard_map.111), calls=%async_computation.1 | async-start | bytes 8388608 | tf_op jit(solution)/shard_map/all_to_all | solution.py:216
  164.5 50.2 %collective-permute-start = (f32[32,128]{1,0:T(8,128)S(1)}, f32[32,128]{1,0:T(8,128)S(1)}, u32[]{:S(2)}, u32[]{:S(2)}) collective-permute-start(f32[32,128]{1,0:T(8,128)S(1)} %select_reduce_fusion), channel_id=1, source_target_pairs={{0,64},{64,128},{128,192},{192,256},{256,320},{320,384},{384,448},... | collective-permute-start | bytes 49160 | tf_op jit(solution)/shard_map/ppermute | solution.py:206
  166.5 54.7 %collective-permute-start.1 = (f32[32,128]{1,0:T(8,128)S(1)}, f32[32,128]{1,0:T(8,128)S(1)}, u32[]{:S(2)}, u32[]{:S(2)}) collective-permute-start(f32[32,128]{1,0:T(8,128)S(1)} %select_reduce_fusion), channel_id=1, source_target_pairs={{0,128},{64,192},{128,256},{192,320},{256,384},{320,448},{384,0},{... | collective-permute-start | bytes 49160 | tf_op jit(solution)/shard_map/ppermute | solution.py:206
  175.7 93.7 %collective-permute-start.2 = (f32[32,128]{1,0:T(8,128)S(1)}, f32[32,128]{1,0:T(8,128)S(1)}, u32[]{:S(2)}, u32[]{:S(2)}) collective-permute-start(f32[32,128]{1,0:T(8,128)S(1)} %select_reduce_fusion), channel_id=1, source_target_pairs={{0,192},{64,256},{128,320},{192,384},{256,448},{320,0},{384,64},{4... | collective-permute-start | bytes 49160 | tf_op jit(solution)/shard_map/ppermute | solution.py:206
  177.7 91.8 %collective-permute-start.3 = (f32[32,128]{1,0:T(8,128)S(1)}, f32[32,128]{1,0:T(8,128)S(1)}, u32[]{:S(2)}, u32[]{:S(2)}) collective-permute-start(f32[32,128]{1,0:T(8,128)S(1)} %select_reduce_fusion), channel_id=1, source_target_pairs={{0,256},{64,320},{128,384},{192,448},{256,0},{320,64},{384,128},{4... | collective-permute-start | bytes 49160 | tf_op jit(solution)/shard_map/ppermute | solution.py:206
  179.6 89.9 %collective-permute-start.4 = (f32[32,128]{1,0:T(8,128)S(1)}, f32[32,128]{1,0:T(8,128)S(1)}, u32[]{:S(2)}, u32[]{:S(2)}) collective-permute-start(f32[32,128]{1,0:T(8,128)S(1)} %select_reduce_fusion), channel_id=1, source_target_pairs={{0,320},{64,384},{128,448},{192,0},{256,64},{320,128},{384,192},{4... | collective-permute-start | bytes 49160 | tf_op jit(solution)/shard_map/ppermute | solution.py:206
  214.7 54.8 %collective-permute-start.5 = (f32[32,128]{1,0:T(8,128)S(1)}, f32[32,128]{1,0:T(8,128)S(1)}, u32[]{:S(2)}, u32[]{:S(2)}) collective-permute-start(f32[32,128]{1,0:T(8,128)S(1)} %select_reduce_fusion), channel_id=1, source_target_pairs={{0,384},{64,448},{128,0},{192,64},{256,128},{320,192},{384,256},{4... | collective-permute-start | bytes 49160 | tf_op jit(solution)/shard_map/ppermute | solution.py:206
  221.2 54.2 %collective-permute-start.6 = (f32[32,128]{1,0:T(8,128)S(1)}, f32[32,128]{1,0:T(8,128)S(1)}, u32[]{:S(2)}, u32[]{:S(2)}) collective-permute-start(f32[32,128]{1,0:T(8,128)S(1)} %select_reduce_fusion), channel_id=1, source_target_pairs={{0,448},{64,0},{128,64},{192,128},{256,192},{320,256},{384,320},{4... | collective-permute-start | bytes 49160 | tf_op jit(solution)/shard_map/ppermute | solution.py:206

commit v14 on v11

--- a/solution.py
+++ b/solution.py
@@ -73,7 +73,7 @@
 
         return carry
 
-    lax.fori_loop(0, cluster_count, one_cluster, 0)
+    lax.fori_loop(0, cluster_count, one_cluster, 0, unroll=2)
 
 
 def routed_attention(recv_table, present_count, member_table, arrived):

time: 281 us -> 283 us (level)
  the two profiles are of different devices: /device:TPU:72 before, /device:TPU:80 now
where the time goes in v14:
time: 283 us
  waiting for transfers between devices  170 us (60%)
  starting transfers between devices  77.1 us (27%)
  Pallas kernels  29.2 us (10%)
  other arithmetic  2.86 us (1%)
    all_to_all x1, waiting for transfers between devices, per_device(): lax.all_to_all(pack_blocks(dest_table, (queries[0], keys[0], values[0], c...  97.5 us
    ppermute x7, waiting for transfers between devices, per_device(): lax.ppermute(key_sum, 'dp', [(index, (index + shift) % dp_size) for index...  61.8 us
    ppermute x7, starting transfers between devices, per_device(): lax.ppermute(key_sum, 'dp', [(index, (index + shift) % dp_size) for index...  51.9 us
    pallas_call x1, Pallas kernels, routed_attention(): pl.pallas_call(routed_kernel, out_shape=(jax.ShapeDtypeStruct(arrived.sha...  21.2 us
    all_to_all x1, starting transfers between devices, per_device(): lax.all_to_all(pack_blocks(dest_table, (queries[0], keys[0], values[0], c...  16.8 us
    all_to_all x1, waiting for transfers between devices, per_device(): lax.all_to_all(outgoing, 'seq', split_axis=0, concat_axis=0, tiled=True)  11 us
    all_to_all x1, starting transfers between devices, per_device(): lax.all_to_all(outgoing, 'seq', split_axis=0, concat_axis=0, tiled=True)  8.41 us
  transfers between devices with their start and end apart: 9, of which 4 were waited for; matrix products, arithmetic and copies ran while one was open for 1% of the time, Pallas kernels for 0%

profile of v14, /device:TPU:80, one launch (start us, length us, event | category | flops | bytes accessed | tf_op | source)
XLA Modules:
  0.0 282.6 jit_solution(16494898725580030796)
XLA Ops:
  0.7 0.8 copy.34
  1.4 0.1 copy.38
  1.5 0.1 fusion.7
  1.6 0.1 copy.40
  1.7 0.7 add_add_fusion.dest_ref
  2.3 3.9 %shard_map.110 = bf16[64,4,64,128]{3,2,1,0:T(8,128)(2,1)} custom-call(s32[16,2]{1,0:T(8,128)} %add_add_fusion.dest_ref, bf16[128,2048]{1,0:T(8,128)(2,1)} %bitcast.30, bf16[128,2048]{1,0:T(8,128)(2,1)} %bitcast.31, bf16[128,2048]{1,0:T(8,128)(2,1)} %bitcast.32, bf16[128,2048]{1,0:T(8,128)(2,1)} %bitcast.33), custom_call_target="tpu_custom_call" | custom-call | tf_op jit(solution)/shard_map/pallas_call | solution.py:126
  6.2 0.0 copy-start.1
  6.2 16.8 %all-to-all-start = ((bf16[64,4,64,128]{3,2,1,0:T(8,128)(2,1)}), bf16[64,4,64,128]{3,2,1,0:T(8,128)(2,1)}, u32[]{:S(2)}, u32[]{:S(2)}) async-start(bf16[64,4,64,128]{3,2,1,0:T(8,128)(2,1)} %shard_map.110), calls=%async_computation | async-start | bytes 8388608 | tf_op jit(solution)/shard_map/all_to_all | solution.py:182
  23.0 0.0 copy-done.1
  23.0 0.1 copy.46
  23.1 0.1 reshape_squeeze.6
  23.3 0.2 convert_reduce_fusion
  23.4 0.1 reduce_sum.31
  23.5 0.1 copy.41
  23.6 1.3 broadcast_select_fusion
  24.9 97.5 %all-to-all-done.arrived_ref = bf16[64,4,64,128]{3,2,1,0:T(8,128)(2,1)} async-done(((bf16[64,4,64,128]{3,2,1,0:T(8,128)(2,1)}), bf16[64,4,64,128]{3,2,1,0:T(8,128)(2,1)}, u32[]{:S(2)}, u32[]{:S(2)}) %all-to-all-start) | async-done | bytes 4194336 | tf_op jit(solution)/shard_map/all_to_all | solution.py:182
  122.4 21.2 %shard_map.111 = (bf16[64,4,64,128]{3,2,1,0:T(8,128)(2,1)}, f32[32,8,128]{2,1,0:T(8,128)}) custom-call(s32[32,4]{1,0:T(8,128)} %get-tuple-element.18.recv_ref, s32[32]{0:T(128)} %get-tuple-element.19.count_ref, s32[32,4]{1,0:T(8,128)} %get-tuple-element.17.member_ref, bf16[64,4,64,128]{3,2,1,0:T(8,128)(2,1)} %all-to-all-done.arrived_ref), custom_call_target="tpu_custom_call" | custom-call | tf_op jit(solution)/shard_map/pallas_call | solution.py:82
  143.6 0.0 copy-start
  143.6 8.4 %all-to-all-start.1 = ((bf16[64,4,64,128]{3,2,1,0:T(8,128)(2,1)}), bf16[64,4,64,128]{3,2,1,0:T(8,128)(2,1)}, u32[]{:S(2)}, u32[]{:S(2)}) async-start(bf16[64,4,64,128]{3,2,1,0:T(8,128)(2,1)} %get-tuple-element.11), calls=%async_computation.1 | async-start | bytes 8388608 | tf_op jit(solution)/shard_map/all_to_all | solution.py:216
  152.2 0.9 slice.3
  153.1 1.9 collective-permute-start
  155.0 13.6 %collective-permute-start.1 = (f32[32,128]{1,0:T(8,128)S(1)}, f32[32,128]{1,0:T(8,128)S(1)}, u32[]{:S(2)}, u32[]{:S(2)}) collective-permute-start(f32[32,128]{1,0:T(8,128)S(1)} %bitcast.35), channel_id=1, source_target_pairs={{0,128},{64,192},{128,256},{192,320},{256,384},{320,448},{384,0},{... | collective-permute-start | bytes 49160 | tf_op jit(solution)/shard_map/ppermute | solution.py:206
  168.7 7.4 %collective-permute-start.2 = (f32[32,128]{1,0:T(8,128)S(1)}, f32[32,128]{1,0:T(8,128)S(1)}, u32[]{:S(2)}, u32[]{:S(2)}) collective-permute-start(f32[32,128]{1,0:T(8,128)S(1)} %bitcast.36), channel_id=1, source_target_pairs={{0,192},{64,256},{128,320},{192,384},{256,448},{320,0},{384,64},{4... | collective-permute-start | bytes 49160 | tf_op jit(solution)/shard_map/ppermute | solution.py:206
  176.1 1.9 collective-permute-start.3
  178.0 3.4 %collective-permute-start.4 = (f32[32,128]{1,0:T(8,128)S(1)}, f32[32,128]{1,0:T(8,128)S(1)}, u32[]{:S(2)}, u32[]{:S(2)}) collective-permute-start(f32[32,128]{1,0:T(8,128)S(1)} %bitcast.38), channel_id=1, source_target_pairs={{0,320},{64,384},{128,448},{192,0},{256,64},{320,128},{384,192},{4... | collective-permute-start | bytes 49160 | tf_op jit(solution)/shard_map/ppermute | solution.py:206
  181.4 0.0 collective-permute-done
  181.4 21.7 %collective-permute-start.5 = (f32[32,128]{1,0:T(8,128)S(1)}, f32[32,128]{1,0:T(8,128)S(1)}, u32[]{:S(2)}, u32[]{:S(2)}) collective-permute-start(f32[32,128]{1,0:T(8,128)S(1)} %bitcast.40), channel_id=1, source_target_pairs={{0,384},{64,448},{128,0},{192,64},{256,128},{320,192},{384,256},{4... | collective-permute-start | bytes 49160 | tf_op jit(solution)/shard_map/ppermute | solution.py:206
  203.1 58.1 %collective-permute-done.1 = f32[32,128]{1,0:T(8,128)S(1)} collective-permute-done((f32[32,128]{1,0:T(8,128)S(1)}, f32[32,128]{1,0:T(8,128)S(1)}, u32[]{:S(2)}, u32[]{:S(2)}) %collective-permute-start.1) | collective-permute-done | bytes 16416 | tf_op jit(solution)/shard_map/ppermute | solution.py:206
  261.3 1.9 collective-permute-start.6
  263.2 0.0 collective-permute-done.2
  263.2 0.0 collective-permute-done.3
  263.3 0.0 collective-permute-done.4
  263.3 3.6 %collective-permute-done.5 = f32[32,128]{1,0:T(8,128)S(1)} collective-permute-done((f32[32,128]{1,0:T(8,128)S(1)}, f32[32,128]{1,0:T(8,128)S(1)}, u32[]{:S(2)}, u32[]{:S(2)}) %collective-permute-start.5) | collective-permute-done | bytes 16416 | tf_op jit(solution)/shard_map/ppermute | solution.py:206
  266.9 0.0 collective-permute-done.6
  266.9 0.0 copy-done
  266.9 0.6 bitcast_add_fusion
  267.5 11.0 %all-to-all-done.1.in_ref = bf16[64,4,64,128]{3,2,1,0:T(8,128)(2,1)} async-done(((bf16[64,4,64,128]{3,2,1,0:T(8,128)(2,1)}), bf16[64,4,64,128]{3,2,1,0:T(8,128)(2,1)}, u32[]{:S(2)}, u32[]{:S(2)}) %all-to-all-start.1) | async-done | bytes 4194336 | tf_op jit(solution)/shard_map/all_to_all | solution.py:216
  278.5 4.1 %shard_map.112 = (bf16[128,2048]{1,0:T(8,128)(2,1)}, bf16[128,2048]{1,0:T(8,128)(2,1)}, bf16[128,2048]{1,0:T(8,128)(2,1)}, bf16[128,2048]{1,0:T(8,128)(2,1)}) custom-call(s32[16,2]{1,0:T(8,128)} %add_add_fusion.dest_ref, bf16[64,4,64,128]{3,2,1,0:T(8,128)(2,1)} %all-to-all-done.1.in_ref), custom_call_target="tpu_custom_call" | custom-call | tf_op jit(solution)/shard_map/pallas_call | solution.py:141
  (13 shorter events, 0.1 us)
Async XLA Ops:
  6.2 16.8 %copy-start.1 = (s32[1,32,4]{1,2,0:T(4,128)S(1)}, s32[1,32,4]{1,2,0:T(4,128)}, u32[]{:S(2)}) copy-start(s32[1,32,4]{1,2,0:T(4,128)} %param.12) | copy-start | bytes 1540
  6.2 116.2 %all-to-all-start = ((bf16[64,4,64,128]{3,2,1,0:T(8,128)(2,1)}), bf16[64,4,64,128]{3,2,1,0:T(8,128)(2,1)}, u32[]{:S(2)}, u32[]{:S(2)}) async-start(bf16[64,4,64,128]{3,2,1,0:T(8,128)(2,1)} %shard_map.110), calls=%async_computation | async-start | bytes 8388608 | tf_op jit(solution)/shard_map/all_to_all | solution.py:182
  143.6 123.3 %copy-start = (f32[32,128]{1,0:T(8,128)S(1)}, f32[32,128]{1,0:T(8,128)}, u32[]{:S(2)}) copy-start(f32[32,128]{1,0:T(8,128)} %param.13) | copy-start | bytes 49156
  143.6 134.9 %all-to-all-start.1 = ((bf16[64,4,64,128]{3,2,1,0:T(8,128)(2,1)}), bf16[64,4,64,128]{3,2,1,0:T(8,128)(2,1)}, u32[]{:S(2)}, u32[]{:S(2)}) async-start(bf16[64,4,64,128]{3,2,1,0:T(8,128)(2,1)} %get-tuple-element.11), calls=%async_computation.1 | async-start | bytes 8388608 | tf_op jit(solution)/shard_map/all_to_all | solution.py:216
  153.1 28.3 %collective-permute-start = (f32[32,128]{1,0:T(8,128)S(1)}, f32[32,128]{1,0:T(8,128)S(1)}, u32[]{:S(2)}, u32[]{:S(2)}) collective-permute-start(f32[32,128]{1,0:T(8,128)S(1)} %bitcast.34), channel_id=1, source_target_pairs={{0,64},{64,128},{128,192},{192,256},{256,320},{320,384},{384,448},... | collective-permute-start | bytes 49160 | tf_op jit(solution)/shard_map/ppermute | solution.py:206
  155.0 106.3 %collective-permute-start.1 = (f32[32,128]{1,0:T(8,128)S(1)}, f32[32,128]{1,0:T(8,128)S(1)}, u32[]{:S(2)}, u32[]{:S(2)}) collective-permute-start(f32[32,128]{1,0:T(8,128)S(1)} %bitcast.35), channel_id=1, source_target_pairs={{0,128},{64,192},{128,256},{192,320},{256,384},{320,448},{384,0},{... | collective-permute-start | bytes 49160 | tf_op jit(solution)/shard_map/ppermute | solution.py:206
  168.7 94.6 %collective-permute-start.2 = (f32[32,128]{1,0:T(8,128)S(1)}, f32[32,128]{1,0:T(8,128)S(1)}, u32[]{:S(2)}, u32[]{:S(2)}) collective-permute-start(f32[32,128]{1,0:T(8,128)S(1)} %bitcast.36), channel_id=1, source_target_pairs={{0,192},{64,256},{128,320},{192,384},{256,448},{320,0},{384,64},{4... | collective-permute-start | bytes 49160 | tf_op jit(solution)/shard_map/ppermute | solution.py:206
  176.1 87.1 %collective-permute-start.3 = (f32[32,128]{1,0:T(8,128)S(1)}, f32[32,128]{1,0:T(8,128)S(1)}, u32[]{:S(2)}, u32[]{:S(2)}) collective-permute-start(f32[32,128]{1,0:T(8,128)S(1)} %bitcast.37), channel_id=1, source_target_pairs={{0,256},{64,320},{128,384},{192,448},{256,0},{320,64},{384,128},{4... | collective-permute-start | bytes 49160 | tf_op jit(solution)/shard_map/ppermute | solution.py:206
  178.0 85.2 %collective-permute-start.4 = (f32[32,128]{1,0:T(8,128)S(1)}, f32[32,128]{1,0:T(8,128)S(1)}, u32[]{:S(2)}, u32[]{:S(2)}) collective-permute-start(f32[32,128]{1,0:T(8,128)S(1)} %bitcast.38), channel_id=1, source_target_pairs={{0,320},{64,384},{128,448},{192,0},{256,64},{320,128},{384,192},{4... | collective-permute-start | bytes 49160 | tf_op jit(solution)/shard_map/ppermute | solution.py:206
  181.4 85.5 %collective-permute-start.5 = (f32[32,128]{1,0:T(8,128)S(1)}, f32[32,128]{1,0:T(8,128)S(1)}, u32[]{:S(2)}, u32[]{:S(2)}) collective-permute-start(f32[32,128]{1,0:T(8,128)S(1)} %bitcast.40), channel_id=1, source_target_pairs={{0,384},{64,448},{128,0},{192,64},{256,128},{320,192},{384,256},{4... | collective-permute-start | bytes 49160 | tf_op jit(solution)/shard_map/ppermute | solution.py:206
  261.3 5.6 %collective-permute-start.6 = (f32[32,128]{1,0:T(8,128)S(1)}, f32[32,128]{1,0:T(8,128)S(1)}, u32[]{:S(2)}, u32[]{:S(2)}) collective-permute-start(f32[32,128]{1,0:T(8,128)S(1)} %bitcast.41), channel_id=1, source_target_pairs={{0,448},{64,0},{128,64},{192,128},{256,192},{320,256},{384,320},{4... | collective-permute-start | bytes 49160 | tf_op jit(solution)/shard_map/ppermute | solution.py:206
